TPU v7x, 512 devices: a whole 4x8x8 slice. The times are simulated.
512 devices in a mesh: seq: 64 (over y, x, core), fsdp: 8 (over z).
Axes of the slice: x: 4, y: 8, z: 8, core: 2. Of those that a mesh axis runs over, the one named last changes fastest.
Arguments:
- queries: bfloat16 [32768, 2048], P('seq', 'fsdp'), may hold values from -6 to 6
- keys: bfloat16 [32768, 2048], P('seq', 'fsdp'), may hold values from -6 to 6
- values: bfloat16 [32768, 2048], P('seq', 'fsdp'), may hold values from -6 to 6
- feature_weight: bfloat16 [16, 128, 128], P(None, 'fsdp', 'seq'), may hold values from -0.5 to 0.5
- norm_gain: bfloat16 [16, 128], P('fsdp'), may hold values from 0.099609375 to 1.8984375
- doc_bounds: int32 [4, 2], replicated, may hold values from 0 to 256, as said below
- out_grad: bfloat16 [32768, 2048], P('seq', 'fsdp'), may hold values from -6 to 6
Outputs:
- mixed: bfloat16 [32768, 2048], P('seq', 'fsdp')
- query_grad: bfloat16 [32768, 2048], P('seq', 'fsdp')
- key_grad: bfloat16 [32768, 2048], P('seq', 'fsdp')
- value_grad: bfloat16 [32768, 2048], P('seq', 'fsdp')
- weight_grad: float32 [16, 128, 128], P(None, 'fsdp', 'seq')
- gain_grad: float32 [16, 128], P('fsdp')
Inputs may be any that keep to these rules, and one draw needn't show every extreme that they name: `doc_bounds`: the rows list the 4 documents in order: column 0 is the first block and column 1 the block after the last; the first document starts at block 0, each ends where the next starts, the last ends at block 256; every document holds one block or more of 128 tokens.
All inputs are finite; a program needn't handle non-finite values.
Results may differ from a plain program's by a relative error of at most 0.015.
Values may be sent and summed in bfloat16 or wider, within the bound.
No kernel may reach another device: no remote copies, remote signals or barrier semaphores. Data moves between devices by JAX's collectives and lax.ppermute only.
A program may use at most 64 MiB of HBM per device.

v0:
```python
import jax
import jax.numpy as jnp
from jax import lax
from jax.sharding import PartitionSpec as P

HS = 128
BLK = 128


epsilon = 1.0


def carried_in(shard, axis, join, neutral, backward):
    count = lax.axis_size(axis)
    place = lax.axis_index(axis)
    ahead = count - 1 - place if backward else place
    gathered = jax.tree.map(
        lambda a, kind: lax.all_gather(a.astype(kind), axis), shard, (jnp.bfloat16, jnp.bfloat16)
    )
    state = jax.tree.map(lambda a, e: jnp.zeros_like(a) + jnp.asarray(e, a.dtype), shard, neutral)

    def one(hop, state):
        source = count - 1 - hop if backward else hop
        return join(
            state,
            jax.tree.map(
                lambda a, own: lax.dynamic_index_in_dim(a, source, 0, False).astype(own.dtype),
                gathered,
                shard,
            ),
        )

    return lax.fori_loop(0, ahead, one, state)


def chain_states(earlier, later):
    early_state, early_flag = earlier
    late_state, late_flag = later
    return (
        jnp.where(late_flag > 0.0, late_state, early_state + late_state),
        jnp.maximum(early_flag, late_flag),
    )


def project(rows, weight):
    return jnp.einsum("bthd,hde->bthe", rows, weight, preferred_element_type=jnp.float32).astype(
        jnp.bfloat16
    )


def local(queries, keys, values, feature_weight, norm_gain, doc_bounds, out_grad):
    rows_full = lax.all_gather(feature_weight, "seq", axis=2, tiled=True)
    weight_local = lax.all_to_all(rows_full, "fsdp", split_axis=0, concat_axis=1, tiled=True)
    head_count = weight_local.shape[0]
    tokens_here = queries.shape[0]
    block_count = tokens_here // BLK
    block_shape = (block_count, BLK, head_count, HS)
    query_blocks = queries.reshape(block_shape)
    key_blocks = keys.reshape(block_shape)
    value_blocks = values.reshape(block_shape)
    qfeat = project(query_blocks, weight_local)
    kfeat = project(key_blocks, weight_local)
    first_block = lax.axis_index("seq") * block_count
    block_ids = first_block + jnp.arange(block_count, dtype=jnp.int32)
    starts = doc_bounds[:, 0]
    starts_here = jnp.any(starts[None, :] == block_ids[:, None], axis=1)
    opened = jnp.cumsum(starts_here.astype(jnp.int32))
    reach_left = opened == 0
    reach_right = opened[-1] - opened == 0
    has_start = jnp.any(starts_here).astype(jnp.float32)
    updates = jnp.einsum("bthe,bthf->bhef", kfeat, value_blocks, preferred_element_type=jnp.float32)
    zero_state = jnp.zeros(updates.shape[1:], jnp.float32)
    zero_flag = jnp.zeros((), jnp.float32)
    running = zero_state
    prefix_list = []
    for position in range(block_count):
        held = jnp.where(starts_here[position], zero_state, running)
        prefix_list.append(held)
        running = held + updates[position]
    entering, _ = carried_in(
        (running, has_start), "seq", chain_states, (zero_state, zero_flag), False
    )
    states = jnp.stack(prefix_list) + jnp.where(
        reach_left[:, None, None, None], entering[None], 0.0
    )
    state_half = states.astype(jnp.bfloat16)
    causal = jnp.arange(BLK)[:, None] >= jnp.arange(BLK)[None, :]
    scores = jnp.einsum("bthe,bshe->bhts", qfeat, kfeat, preferred_element_type=jnp.float32)
    prob_half = jnp.where(causal, scores, 0.0).astype(jnp.bfloat16)
    mixed_f = jnp.einsum("bthe,bhef->bthf", qfeat, state_half, preferred_element_type=jnp.float32)
    mixed_f = mixed_f + jnp.einsum(
        "bhts,bshf->bthf", prob_half, value_blocks, preferred_element_type=jnp.float32
    )
    gains = norm_gain.astype(jnp.float32)
    inverse = lax.rsqrt(jnp.mean(mixed_f * mixed_f, axis=-1, keepdims=True) + epsilon)
    mixed = (mixed_f * inverse * gains).astype(jnp.bfloat16)
    grad_y = out_grad.reshape(block_shape).astype(jnp.float32)
    scaled = grad_y * gains
    grad_mix = inverse * (
        scaled - mixed_f * inverse * inverse * jnp.mean(scaled * mixed_f, axis=-1, keepdims=True)
    )
    grad_half = grad_mix.astype(jnp.bfloat16)
    gain_part = jnp.sum(grad_y * mixed_f * inverse, axis=(0, 1))
    state_grads = jnp.einsum(
        "bthe,bthf->bhef", qfeat, grad_half, preferred_element_type=jnp.float32
    )
    running = zero_state
    suffix_list = [zero_state] * block_count
    for position in reversed(range(block_count)):
        suffix_list[position] = running
        running = jnp.where(starts_here[position], zero_state, running + state_grads[position])
    leaving, _ = carried_in(
        (running, has_start), "seq", chain_states, (zero_state, zero_flag), True
    )
    suffix = jnp.stack(suffix_list) + jnp.where(
        reach_right[:, None, None, None], leaving[None], 0.0
    )
    suffix_half = suffix.astype(jnp.bfloat16)
    dot_grads = jnp.einsum(
        "bthf,bshf->bhts", grad_half, value_blocks, preferred_element_type=jnp.float32
    )
    dot_half = jnp.where(causal, dot_grads, 0.0).astype(jnp.bfloat16)
    qfeat_grad = jnp.einsum(
        "bthf,bhef->bthe", grad_half, state_half, preferred_element_type=jnp.float32
    )
    qfeat_grad = (
        qfeat_grad
        + jnp.einsum("bhts,bshe->bthe", dot_half, kfeat, preferred_element_type=jnp.float32)
    ).astype(jnp.bfloat16)
    kfeat_grad = jnp.einsum(
        "bshf,bhef->bshe", value_blocks, suffix_half, preferred_element_type=jnp.float32
    )
    kfeat_grad = (
        kfeat_grad
        + jnp.einsum("bhts,bthe->bshe", dot_half, qfeat, preferred_element_type=jnp.float32)
    ).astype(jnp.bfloat16)
    value_grad = jnp.einsum(
        "bshe,bhef->bshf", kfeat, suffix_half, preferred_element_type=jnp.float32
    )
    value_grad = (
        value_grad
        + jnp.einsum("bhts,bthf->bshf", prob_half, grad_half, preferred_element_type=jnp.float32)
    ).astype(jnp.bfloat16)
    query_grad = jnp.einsum(
        "bthe,hde->bthd", qfeat_grad, weight_local, preferred_element_type=jnp.float32
    ).astype(jnp.bfloat16)
    key_grad = jnp.einsum(
        "bthe,hde->bthd", kfeat_grad, weight_local, preferred_element_type=jnp.float32
    ).astype(jnp.bfloat16)
    weight_part = jnp.einsum(
        "bthd,bthe->hde", query_blocks, qfeat_grad, preferred_element_type=jnp.float32
    )
    weight_part = weight_part + jnp.einsum(
        "bthd,bthe->hde", key_blocks, kfeat_grad, preferred_element_type=jnp.float32
    )
    weight_sum, gain_sum = lax.psum((weight_part, gain_part), "seq")
    column_width = weight_sum.shape[2] // lax.axis_size("seq")
    weight_columns = lax.dynamic_slice_in_dim(
        weight_sum, lax.axis_index("seq") * column_width, column_width, 2
    )
    owned_grad = lax.all_to_all(weight_columns, "fsdp", split_axis=1, concat_axis=0, tiled=True)
    factor = (lax.axis_size("seq") * tokens_here) ** (-0.5)
    flat_shape = (tokens_here, head_count * HS)
    return (
        mixed.reshape(flat_shape),
        query_grad.reshape(flat_shape),
        key_grad.reshape(flat_shape),
        value_grad.reshape(flat_shape),
        owned_grad * factor,
        gain_sum * factor,
    )


def solution(mesh):
    placed = (
        P("seq", "fsdp"),
        P("seq", "fsdp"),
        P("seq", "fsdp"),
        P(None, "fsdp", "seq"),
        P("fsdp", None),
        P(),
        P("seq", "fsdp"),
    )
    return jax.shard_map(
        local,
        mesh=mesh,
        in_specs=placed,
        out_specs=(
            P("seq", "fsdp"),
            P("seq", "fsdp"),
            P("seq", "fsdp"),
            P("seq", "fsdp"),
            P(None, "fsdp", "seq"),
            P("fsdp", None),
        ),
        check_vma=False,
    )
```

profile of v0, /device:TPU:1, one launch (start us, length us, event | category | flops | bytes accessed | tf_op | source)
XLA Modules:
  0.0 827.8 jit_solution(3233053818263169173)
XLA Ops:
  8.0 53.9 %all_gather.19 = bf16[16,16,128]{1,0,2:T(8,128)(2,1)S(1)} all-gather(bf16[16,16,2]{1,0,2:T(8,128)(2,1)S(1)} %copy.146), channel_id=1, replica_groups=mesh['seq'=64,'fsdp'=8] {'seq'}, dimensions={2}, use_global_device_ids=true | all-gather | bytes 66560 | tf_op jit(solution)/shard_map/all_gather | solution.py:52
  61.8 1.1 copy.147
  62.9 8.9 %all-to-all-start = ((bf16[16,16,128]{2,1,0:T(8,128)(2,1)}), bf16[16,16,128]{2,1,0:T(8,128)(2,1)S(1)}, u32[]{:S(2)}, u32[]{:S(2)}) async-start(bf16[16,16,128]{2,1,0:T(8,128)(2,1)} %copy.147), calls=%async_computation | async-start | bytes 131072 | tf_op jit(solution)/shard_map/all_to_all | solution.py:53
  73.3 1.0 reshape.100
  74.3 1.0 reshape.101
  76.0 3.0 all-to-all-done
  79.5 2.5 fusion.43
  84.1 1.3 dynamic-slice
  86.1 125.5 %all-reduce = bf16[64]{0:T(256)(128)(2,1)S(1)} all-reduce(bf16[64]{0:T(256)(128)(2,1)S(1)} %dynamic-update-slice), channel_id=1, replica_groups=mesh['seq'=64,'fsdp'=8] {'seq'}, use_global_device_ids=true, to_apply=%add | all-reduce | flops 64 | bytes 256
  213.9 2.1 while.26
  215.1 0.9 add_select_fusion.4
  217.2 3.2 fusion.40
  220.8 1.2 fusion.48
  222.9 0.9 copy.160
  223.8 252.4 %psum.15 = f32[2,128]{1,0:T(2,128)S(1)} all-reduce(f32[2,128]{1,0:T(2,128)S(1)} %get-tuple-element.136), channel_id=1, replica_groups=mesh['seq'=64,'fsdp'=8] {'seq'}, use_global_device_ids=true, to_apply=%region_11.12 | all-reduce | flops 256 | bytes 2048 | tf_op jit(solution)/shard_map/psum | solution.py:156
  476.8 1.5 fusion.41
  478.3 1.9 copy_bitcast_fusion.2
  480.2 132.8 %while.27 = (s32[]{:T(128)}, f32[2,128,128]{2,1,0:T(8,128)S(1)}, s32[]{:T(128)}, bf16[64]{0:T(256)(128)(2,1)S(1)}, bf16[64,2,128,128]{3,2,1,0:T(8,128)(2,1)}, /*...) while((s32[]{:T(128)}, f32[2,128,128]{2,1,0:T(8,128)S(1)}, s32[]{:T(128)}, ...), condition=%wide.region_8.9_spmd, body=%wide.region_7.8_spmd.sunk | while | flops 98311 | bytes 327847 | solution.py:33
  613.0 1.4 fusion.29
  614.4 1.4 fusion.34
  616.2 0.9 fusion.14
  618.1 184.5 %all-reduce.3.cloned.1.call-done = f32[2,128,128]{1,2,0:T(8,128)} async-done(((f32[2,128,128]{1,2,0:T(8,128)}), f32[2,128,128]{1,2,0:T(8,128)}) %all-reduce.3.cloned.1.call-update) | async-done | bytes 131088 | tf_op jit(solution)/shard_map/psum | solution.py:156
  804.0 7.1 all-to-all-start.1
  812.0 8.5 %all-to-all-done.1 = f32[2,128,2]{2,0,1:T(2,128)S(1)} async-done(((f32[2,128,2]{2,0,1:T(2,128)}), f32[2,128,2]{2,0,1:T(2,128)S(1)}, u32[]{:S(2)}, u32[]{:S(2)}) %all-to-all-start.1) | async-done | bytes 2080 | tf_op jit(solution)/shard_map/all_to_all | solution.py:161
  (197 shorter events, 106.0 us)
Async XLA Ops:
  7.2 75.6 %copy-start.2 = (bf16[512,256]{1,0:T(8,128)(2,1)S(1)}, bf16[512,256]{1,0:T(8,128)(2,1)}, u32[]{:S(2)}) copy-start(bf16[512,256]{1,0:T(8,128)(2,1)} %param.11) | copy-start | bytes 786436
  7.2 76.4 %copy-start.1 = (bf16[512,256]{1,0:T(8,128)(2,1)S(1)}, bf16[512,256]{1,0:T(8,128)(2,1)}, u32[]{:S(2)}) copy-start(bf16[512,256]{1,0:T(8,128)(2,1)} %param.17) | copy-start | bytes 786436
  7.2 76.9 %copy-start.7 = (bf16[2,128]{1,0:T(2,128)(2,1)S(1)}, bf16[2,128]{1,0:T(2,128)(2,1)}, u32[]{:S(2)}) copy-start(bf16[2,128]{1,0:T(2,128)(2,1)} %param.15) | copy-start | bytes 1540
  62.9 16.1 %all-to-all-start = ((bf16[16,16,128]{2,1,0:T(8,128)(2,1)}), bf16[16,16,128]{2,1,0:T(8,128)(2,1)S(1)}, u32[]{:S(2)}, u32[]{:S(2)}) async-start(bf16[16,16,128]{2,1,0:T(8,128)(2,1)} %copy.147), calls=%async_computation | async-start | bytes 131072 | tf_op jit(solution)/shard_map/all_to_all | solution.py:53
  71.8 142.0 %all-gather.3.cloned.1.call-start = ((), (), s32[]{:S(2)}) async-start(), calls=%async_computation.2 | async-start | bytes 4259840 | tf_op jit(solution)/shard_map/all_gather | solution.py:18
  82.0 398.1 %all-gather.5.cloned.1.call-start = ((), (), s32[]{:S(2)}) async-start(), calls=%async_computation.3 | async-start | bytes 4259840 | tf_op jit(solution)/shard_map/all_gather | solution.py:18
  83.8 132.2 %copy-start.6 = (f32[1,2,128,128]{3,2,1,0:T(8,128)S(1)}, f32[1,2,128,128]{3,2,1,0:T(8,128)}, u32[]{:S(2)}) copy-start(f32[1,2,128,128]{3,2,1,0:T(8,128)} %get-tuple-element.165) | copy-start | bytes 393220
  212.9 3.7 copy-start.4
  216.0 6.3 copy-start.3
  220.4 582.1 %all-reduce.3.cloned.1.call-start = ((), (), s32[]{:S(2)}) async-start(), calls=%async_computation.4 | async-start | bytes 262144 | tf_op jit(solution)/shard_map/psum | solution.py:156
  223.8 390.6 %copy-start = (f32[1,2,128,128]{3,2,1,0:T(8,128)S(1)}, f32[1,2,128,128]{3,2,1,0:T(8,128)}, u32[]{:S(2)}) copy-start(f32[1,2,128,128]{3,2,1,0:T(8,128)} %get-tuple-element.161) | copy-start | bytes 393220
  478.3 134.7 %copy-start.5 = (f32[1,2,128,128]{3,2,1,0:T(8,128)}, f32[1,2,128,128]{3,2,1,0:T(8,128)S(1)}, u32[]{:S(2)}) copy-start(f32[1,2,128,128]{3,2,1,0:T(8,128)S(1)} %fusion.41) | copy-start | bytes 393220
  804.0 16.4 %all-to-all-start.1 = ((f32[2,128,2]{2,0,1:T(2,128)}), f32[2,128,2]{2,0,1:T(2,128)S(1)}, u32[]{:S(2)}, u32[]{:S(2)}) async-start(f32[2,128,2]{2,0,1:T(2,128)} %copy.179), calls=%async_computation.1 | async-start | bytes 262144 | tf_op jit(solution)/shard_map/all_to_all | solution.py:161
Sparse Core Ops, SparseCore 0:
  82.1 79.6 all-gather.2
  220.5 208.0 all-gather.4
  617.2 185.2 all-reduce.2
where the time goes:
time: 832 us; the launch traced here: 828 us
  blocking collectives  432 us (52%)
  waiting for transfers between devices  196 us (24%)
  other arithmetic  65.2 us (8%)
  local copies, waits for them, and re-layouts  52 us (6%)
  loops' own time  43.2 us (5%)
  starting transfers between devices  16.1 us (2%)
  between operations  14.8 us (2%)
  matrix products  8.74 us (1%)
    psum x1, blocking collectives, local(): weight_sum, gain_sum = lax.psum((weight_part, gain_part), 'seq')  252 us
    psum x1, waiting for transfers between devices, local(): weight_sum, gain_sum = lax.psum((weight_part, gain_part), 'seq')  184 us
    unnamed x1, blocking collectives  126 us
    select_n x63, other arithmetic, chain_states(): jnp.where(late_flag > 0.0, late_state, early_state + late_state)  54.7 us
    all_gather x1, blocking collectives, local(): rows_full = lax.all_gather(feature_weight, 'seq', axis=2, tiled=True)  53.9 us
    another operation x2, loops' own time, carried_in(): return lax.fori_loop(0, ahead, one, state)  43.2 us
    dynamic_slice x63, local copies, waits for them, and re-layouts, one(): lax.dynamic_index_in_dim(a, source, 0, False).astype(own.dtype)  37 us
  transfers between devices with their start and end apart: 5, of which 3 were waited for; matrix products, arithmetic and copies ran while one was open for 2% of the time, Pallas kernels for 0%

commit v1 on v0

v1 whole, which is shorter than its diff:
```python
import jax
import jax.numpy as jnp
from jax import lax
from jax.sharding import PartitionSpec as P

HS = 128
BLK = 128


epsilon = 1.0
HIGH = lax.Precision.HIGHEST


def shifted(x, dist, backward):
    count = lax.axis_size("seq")
    if backward:
        pairs = [(i, i - dist) for i in range(dist, count)]
    else:
        pairs = [(i, i + dist) for i in range(count - dist)]
    return lax.ppermute(x, "seq", pairs)


def carried_in(aggregate, opens, backward):
    count = lax.axis_size("seq")
    place = lax.axis_index("seq")
    sign = 1 if backward else -1
    near = shifted(aggregate, 1, backward)
    far = shifted(aggregate, 2, backward)
    one = place + sign
    state = jnp.where(opens(one, one), near, far + near)
    covered = 2
    while covered < count:
        far = shifted(state, covered, backward)
        lo, hi = (place + 1, place + covered) if backward else (place - covered, place - 1)
        state = jnp.where(opens(lo, hi), state, far + state)
        covered *= 2
    return state


def project(rows, weight):
    return jnp.einsum("bthd,hde->bthe", rows, weight, preferred_element_type=jnp.float32).astype(
        jnp.bfloat16
    )


def local(queries, keys, values, feature_weight, norm_gain, doc_bounds, out_grad):
    head_groups = lax.all_to_all(feature_weight, "fsdp", split_axis=0, concat_axis=1, tiled=True)
    weight_local = lax.all_gather(head_groups, "seq", axis=2, tiled=True)
    head_count = weight_local.shape[0]
    tokens_here = queries.shape[0]
    block_count = tokens_here // BLK
    block_shape = (block_count, BLK, head_count, HS)
    query_blocks = queries.reshape(block_shape)
    key_blocks = keys.reshape(block_shape)
    value_blocks = values.reshape(block_shape)

    place = lax.axis_index("seq")
    starts = doc_bounds[:, 0]
    start_device = starts // block_count

    def opens(lo, hi):
        return jnp.any((start_device >= lo) & (start_device <= hi))

    block_ids = place * block_count + jnp.arange(block_count, dtype=jnp.int32)
    starts_here = jnp.any(starts[None, :] == block_ids[:, None], axis=1)
    opened = jnp.cumsum(starts_here.astype(jnp.int32))
    reach_left = opened == 0
    reach_right = opened[-1] - opened == 0

    raw_updates = jnp.einsum(
        "bthd,bthf->bhdf", key_blocks, value_blocks, preferred_element_type=jnp.float32
    )
    zero_state = jnp.zeros(raw_updates.shape[1:], jnp.float32)
    running = zero_state
    prefix_list = []
    for position in range(block_count):
        held = jnp.where(starts_here[position], zero_state, running)
        prefix_list.append(held)
        running = held + raw_updates[position]
    entering = carried_in(running, opens, False)
    raw_states = jnp.stack(prefix_list) + jnp.where(
        reach_left[:, None, None, None], entering[None], 0.0
    )

    qfeat = project(query_blocks, weight_local)
    kfeat = project(key_blocks, weight_local)
    weight_f = weight_local.astype(jnp.float32)
    states = jnp.einsum("hde,bhdf->bhef", weight_f, raw_states, precision=HIGH)
    state_half = states.astype(jnp.bfloat16)
    causal = jnp.arange(BLK)[:, None] >= jnp.arange(BLK)[None, :]
    scores = jnp.einsum("bthe,bshe->bhts", qfeat, kfeat, preferred_element_type=jnp.float32)
    prob_half = jnp.where(causal, scores, 0.0).astype(jnp.bfloat16)
    mixed_f = jnp.einsum("bthe,bhef->bthf", qfeat, state_half, preferred_element_type=jnp.float32)
    mixed_f = mixed_f + jnp.einsum(
        "bhts,bshf->bthf", prob_half, value_blocks, preferred_element_type=jnp.float32
    )
    gains = norm_gain.astype(jnp.float32)
    inverse = lax.rsqrt(jnp.mean(mixed_f * mixed_f, axis=-1, keepdims=True) + epsilon)
    mixed = (mixed_f * inverse * gains).astype(jnp.bfloat16)
    grad_y = out_grad.reshape(block_shape).astype(jnp.float32)
    scaled = grad_y * gains
    grad_mix = inverse * (
        scaled - mixed_f * inverse * inverse * jnp.mean(scaled * mixed_f, axis=-1, keepdims=True)
    )
    grad_half = grad_mix.astype(jnp.bfloat16)
    gain_part = jnp.sum(grad_y * mixed_f * inverse, axis=(0, 1))
    gain_sum = lax.psum(gain_part, "seq")

    state_grads = jnp.einsum(
        "bthe,bthf->bhef", qfeat, grad_half, preferred_element_type=jnp.float32
    )
    dot_grads = jnp.einsum(
        "bthf,bshf->bhts", grad_half, value_blocks, preferred_element_type=jnp.float32
    )
    dot_half = jnp.where(causal, dot_grads, 0.0).astype(jnp.bfloat16)
    qfeat_grad = jnp.einsum(
        "bthf,bhef->bthe", grad_half, state_half, preferred_element_type=jnp.float32
    )
    qfeat_grad = (
        qfeat_grad
        + jnp.einsum("bhts,bshe->bthe", dot_half, kfeat, preferred_element_type=jnp.float32)
    ).astype(jnp.bfloat16)
    kfeat_inner = jnp.einsum(
        "bhts,bthe->bshe", dot_half, qfeat, preferred_element_type=jnp.float32
    )
    weight_part = jnp.einsum(
        "bthd,bthe->hde", query_blocks, qfeat_grad, preferred_element_type=jnp.float32
    )
    weight_part = weight_part + jnp.einsum(
        "bthd,bthe->hde", key_blocks, kfeat_inner.astype(jnp.bfloat16),
        preferred_element_type=jnp.float32,
    )
    weight_part = weight_part + jnp.einsum(
        "bhdf,bhef->hde", raw_states, state_grads, precision=HIGH
    )
    weight_columns = lax.psum_scatter(weight_part, "seq", scatter_dimension=2, tiled=True)
    owned_grad = lax.all_to_all(weight_columns, "fsdp", split_axis=1, concat_axis=0, tiled=True)

    running = zero_state
    suffix_list = [zero_state] * block_count
    for position in reversed(range(block_count)):
        suffix_list[position] = running
        running = jnp.where(starts_here[position], zero_state, running + state_grads[position])
    leaving = carried_in(running, opens, True)
    suffix = jnp.stack(suffix_list) + jnp.where(
        reach_right[:, None, None, None], leaving[None], 0.0
    )
    suffix_half = suffix.astype(jnp.bfloat16)
    kfeat_grad = jnp.einsum(
        "bshf,bhef->bshe", value_blocks, suffix_half, preferred_element_type=jnp.float32
    )
    kfeat_grad = (kfeat_grad + kfeat_inner).astype(jnp.bfloat16)
    value_grad = jnp.einsum(
        "bshe,bhef->bshf", kfeat, suffix_half, preferred_element_type=jnp.float32
    )
    value_grad = (
        value_grad
        + jnp.einsum("bhts,bthf->bshf", prob_half, grad_half, preferred_element_type=jnp.float32)
    ).astype(jnp.bfloat16)
    query_grad = jnp.einsum(
        "bthe,hde->bthd", qfeat_grad, weight_local, preferred_element_type=jnp.float32
    ).astype(jnp.bfloat16)
    key_grad = jnp.einsum(
        "bthe,hde->bthd", kfeat_grad, weight_local, preferred_element_type=jnp.float32
    ).astype(jnp.bfloat16)
    factor = (lax.axis_size("seq") * tokens_here) ** (-0.5)
    flat_shape = (tokens_here, head_count * HS)
    return (
        mixed.reshape(flat_shape),
        query_grad.reshape(flat_shape),
        key_grad.reshape(flat_shape),
        value_grad.reshape(flat_shape),
        owned_grad * factor,
        gain_sum * factor,
    )


def solution(mesh):
    placed = (
        P("seq", "fsdp"),
        P("seq", "fsdp"),
        P("seq", "fsdp"),
        P(None, "fsdp", "seq"),
        P("fsdp", None),
        P(),
        P("seq", "fsdp"),
    )
    return jax.shard_map(
        local,
        mesh=mesh,
        in_specs=placed,
        out_specs=(
            P("seq", "fsdp"),
            P("seq", "fsdp"),
            P("seq", "fsdp"),
            P("seq", "fsdp"),
            P(None, "fsdp", "seq"),
            P("fsdp", None),
        ),
        check_vma=False,
    )
```

time: 832 us -> 353 us (0.42)
  blocking collectives: 432 us -> 163 us
  waiting for transfers between devices: 196 us -> 69.5 us
  starting transfers between devices: 16.1 us -> 67.8 us
  other arithmetic: 65.2 us -> 17.8 us
  loops' own time: 43.2 us -> 0 us
  local copies, waits for them, and re-layouts: 52 us -> 11.1 us
    psum x1 -> x0, waiting for transfers between devices: 184 us -> none  [local(): weight_sum, gain_sum = lax.psum((weight_part, gain_part), 'seq')]
    psum x1, blocking collectives: 252 us -> 124 us  [local(): gain_sum = lax.psum(gain_part, 'seq')]
    unnamed x1 -> x0, blocking collectives: 126 us -> none
    ppermute x0 -> x14, starting transfers between devices: none -> 50.6 us  [shifted(): return lax.ppermute(x, 'seq', pairs)]
    select_n x64 -> x12, other arithmetic: 55.4 us -> 9.65 us  [the longest x10 7.33 us: carried_in(): state = jnp.where(opens(lo, hi), state, far + state)]
    another operation x2 -> x0, loops' own time: 43.2 us -> none  [carried_in(): return lax.fori_loop(0, ahead, one, state)]
    unnamed x3 -> x2, waiting for transfers between devices: 0.05 us -> 40.1 us
    dynamic_slice x65 -> x0, local copies, waits for them, and re-layouts: 38.5 us -> none  [the longest x63 37 us: one(): lax.dynamic_index_in_dim(a, source, 0, False).astype(own.dtype)]
  transfers between devices with their start and end apart: 5 -> 17, of which waited for: 3 -> 10; matrix products, arithmetic and copies ran while one was open for 2% -> 5% of each run, Pallas kernels for 0% -> 0%
where the time goes in v1:
time: 353 us; the launch traced here: 351 us
  blocking collectives  163 us (46%)
  waiting for transfers between devices  69.5 us (20%)
  starting transfers between devices  67.8 us (19%)
  other arithmetic  17.8 us (5%)
  between operations  15.2 us (4%)
  local copies, waits for them, and re-layouts  11.1 us (3%)
  matrix products  6.97 us (2%)
    psum x1, blocking collectives, local(): gain_sum = lax.psum(gain_part, 'seq')  124 us
    ppermute x14, starting transfers between devices, shifted(): return lax.ppermute(x, 'seq', pairs)  50.6 us
    unnamed x2, waiting for transfers between devices  40.1 us
    all_gather x1, blocking collectives, local(): weight_local = lax.all_gather(head_groups, 'seq', axis=2, tiled=True)  38.9 us
    ppermute x14, waiting for transfers between devices, shifted(): return lax.ppermute(x, 'seq', pairs)  21.9 us
    all_to_all x1, starting transfers between devices, local(): lax.all_to_all(feature_weight, 'fsdp', split_axis=0, concat_axis=1, tiled...  10 us
    all_to_all x1, waiting for transfers between devices, local(): lax.all_to_all(weight_columns, 'fsdp', split_axis=1, concat_axis=0, tiled...  7.48 us
    select_n x10, other arithmetic, carried_in(): state = jnp.where(opens(lo, hi), state, far + state)  7.33 us
  transfers between devices with their start and end apart: 17, of which 10 were waited for; matrix products, arithmetic and copies ran while one was open for 5% of the time, Pallas kernels for 0%

profile of v1, /device:TPU:1, one launch (start us, length us, event | category | flops | bytes accessed | tf_op | source)
XLA Modules:
  0.0 351.1 jit_solution(5588233773056950007)
XLA Ops:
  10.1 2.0 fusion.50
  12.1 4.6 %collective-permute-start = (f32[2,128,128]{2,1,0:T(8,128)S(1)}, f32[2,128,128]{2,1,0:T(8,128)S(1)}, u32[]{:S(2)}, u32[]{:S(2)}) collective-permute-start(f32[2,128,128]{2,1,0:T(8,128)S(1)} %get-tuple-element.23), channel_id=1, source_target_pairs={{0,8},{8,16},{16,24},{24,32},{32,40},{40,48},{48,56},{56,64},{64,7... | collective-permute-start | bytes 393224 | tf_op jit(solution)/shard_map/ppermute | solution.py:20
  16.7 3.1 collective-permute-start.1
  19.8 10.0 %all-to-all-start = ((bf16[16,16,2]{1,2,0:T(2,128)(2,1)}), bf16[16,16,2]{1,2,0:T(2,128)(2,1)S(1)}, u32[]{:S(2)}, u32[]{:S(2)}) async-start(bf16[16,16,2]{1,2,0:T(2,128)(2,1)} %param.10), calls=%async_computation | async-start | bytes 16384 | tf_op jit(solution)/shard_map/all_to_all | solution.py:47
  32.3 2.8 collective-permute-start.2
  39.7 38.9 %all_gather.3 = bf16[2,128,128]{1,0,2:T(2,128)(2,1)S(1)} all-gather(bf16[2,128,2]{1,0,2:T(2,128)(2,1)S(1)} %all_to_all.23), channel_id=1, replica_groups=mesh['seq'=64,'fsdp'=8] {'seq'}, dimensions={2}, use_global_device_ids=true | all-gather | bytes 66560 | tf_op jit(solution)/shard_map/all_gather | solution.py:48
  79.3 3.3 collective-permute-start.3
  82.9 2.6 collective-permute-done.3
  86.1 6.5 %collective-permute-start.4 = (f32[2,128,128]{2,1,0:T(8,128)S(1)}, f32[2,128,128]{2,1,0:T(8,128)S(1)}, u32[]{:S(2)}, u32[]{:S(2)}) collective-permute-start(f32[2,128,128]{2,1,0:T(8,128)S(1)} %add_select_fusion.9), channel_id=1, source_target_pairs={{0,64},{8,72},{16,80},{24,88},{32,96},{40,104},{48,112},{56,120},{... | collective-permute-start | bytes 393224 | tf_op jit(solution)/shard_map/ppermute | solution.py:20
  92.9 1.7 collective-permute-done.4
  95.2 5.1 %collective-permute-start.5 = (f32[2,128,128]{2,1,0:T(8,128)S(1)}, f32[2,128,128]{2,1,0:T(8,128)S(1)}, u32[]{:S(2)}, u32[]{:S(2)}) collective-permute-start(f32[2,128,128]{2,1,0:T(8,128)S(1)} %add_select_fusion.8), channel_id=1, source_target_pairs={{0,128},{8,136},{16,144},{24,152},{32,160},{40,168},{48,176},{56,1... | collective-permute-start | bytes 393224 | tf_op jit(solution)/shard_map/ppermute | solution.py:20
  100.6 1.6 collective-permute-done.5
  102.9 13.1 %collective-permute-start.6 = (f32[2,128,128]{2,1,0:T(8,128)S(1)}, f32[2,128,128]{2,1,0:T(8,128)S(1)}, u32[]{:S(2)}, u32[]{:S(2)}) collective-permute-start(f32[2,128,128]{2,1,0:T(8,128)S(1)} %add_select_fusion.7), channel_id=1, source_target_pairs={{0,256},{8,264},{16,272},{24,280},{32,288},{40,296},{48,304},{56,3... | collective-permute-start | bytes 393224 | tf_op jit(solution)/shard_map/ppermute | solution.py:20
  116.3 1.6 collective-permute-done.6
  121.6 2.6 fusion.47
  124.2 4.2 %collective-permute-start.7 = (f32[2,128,128]{2,1,0:T(8,128)S(1)}, f32[2,128,128]{2,1,0:T(8,128)}, u32[]{:S(2)}, u32[]{:S(2)}) collective-permute-start(f32[2,128,128]{2,1,0:T(8,128)S(1)} %get-tuple-element.20), channel_id=1, source_target_pairs={{8,0},{16,8},{24,16},{32,24},{40,32},{48,40},{56,48},{64,56},{72,6... | collective-permute-start | bytes 393224 | tf_op jit(solution)/shard_map/ppermute | solution.py:20
  131.4 4.2 %collective-permute-done.8 = f32[2,128,128]{2,1,0:T(8,128)} collective-permute-done((f32[2,128,128]{2,1,0:T(8,128)S(1)}, f32[2,128,128]{2,1,0:T(8,128)}, u32[]{:S(2)}, u32[]{:S(2)}) %collective-permute-start.8) | collective-permute-done | bytes 131104 | tf_op jit(solution)/shard_map/ppermute | solution.py:20
  135.6 1.7 add_select_fusion.5
  139.3 123.8 %psum.7 = f32[2,128]{1,0:T(2,128)S(1)} all-reduce(f32[2,128]{1,0:T(2,128)S(1)} %get-tuple-element.6), channel_id=1, replica_groups=mesh['seq'=64,'fsdp'=8] {'seq'}, use_global_device_ids=true, to_apply=%region_18.19 | all-reduce | flops 256 | bytes 2048 | tf_op jit(solution)/shard_map/psum | solution.py:107
  266.8 5.1 %collective-permute-done.10 = f32[2,128,128]{2,1,0:T(8,128)S(1)} collective-permute-done((f32[2,128,128]{2,1,0:T(8,128)S(1)}, f32[2,128,128]{2,1,0:T(8,128)S(1)}, u32[]{:S(2)}, u32[]{:S(2)}) %collective-permute-start.10) | collective-permute-done | bytes 131104 | tf_op jit(solution)/shard_map/ppermute | solution.py:20
  274.6 3.7 %collective-permute-done.11 = f32[2,128,128]{2,1,0:T(8,128)S(1)} collective-permute-done((f32[2,128,128]{2,1,0:T(8,128)S(1)}, f32[2,128,128]{2,1,0:T(8,128)S(1)}, u32[]{:S(2)}, u32[]{:S(2)}) %collective-permute-start.11) | collective-permute-done | bytes 131104 | tf_op jit(solution)/shard_map/ppermute | solution.py:20
  280.8 40.1 %all-reduce.3.cloned.1.call-done = f32[2,128,128]{1,2,0:T(8,128)} async-done(((f32[2,128,128]{1,2,0:T(8,128)}), f32[2,128,128]{1,2,0:T(8,128)}) %all-reduce.3.cloned.1.call-update) | async-done | bytes 131088
  322.4 7.1 %all-to-all-start.1 = ((f32[2,128,2]{2,0,1:T(2,128)}), f32[2,128,2]{2,0,1:T(2,128)S(1)}, u32[]{:S(2)}, u32[]{:S(2)}) async-start(f32[2,128,2]{2,0,1:T(2,128)} %copy.154), calls=%async_computation.1 | async-start | bytes 262144 | tf_op jit(solution)/shard_map/all_to_all | solution.py:137
  331.4 7.5 %all-to-all-done.1 = f32[2,128,2]{2,0,1:T(2,128)S(1)} async-done(((f32[2,128,2]{2,0,1:T(2,128)}), f32[2,128,2]{2,0,1:T(2,128)S(1)}, u32[]{:S(2)}, u32[]{:S(2)}) %all-to-all-start.1) | async-done | bytes 2080 | tf_op jit(solution)/shard_map/all_to_all | solution.py:137
  (93 shorter events, 38.8 us)
Async XLA Ops:
  7.2 0.7 copy-start.3
  8.6 1.1 copy-start.1
  12.1 23.7 %copy-start.2 = (bf16[512,256]{1,0:T(8,128)(2,1)S(1)}, bf16[512,256]{1,0:T(8,128)(2,1)}, u32[]{:S(2)}) copy-start(bf16[512,256]{1,0:T(8,128)(2,1)} %param.7) | copy-start | bytes 786436
  12.1 19.5 %collective-permute-start = (f32[2,128,128]{2,1,0:T(8,128)S(1)}, f32[2,128,128]{2,1,0:T(8,128)S(1)}, u32[]{:S(2)}, u32[]{:S(2)}) collective-permute-start(f32[2,128,128]{2,1,0:T(8,128)S(1)} %get-tuple-element.23), channel_id=1, source_target_pairs={{0,8},{8,16},{16,24},{24,32},{32,40},{40,48},{48,56},{56,64},{64,7... | collective-permute-start | bytes 393224 | tf_op jit(solution)/shard_map/ppermute | solution.py:20
  16.7 14.9 %collective-permute-start.1 = (f32[2,128,128]{2,1,0:T(8,128)S(1)}, f32[2,128,128]{2,1,0:T(8,128)S(1)}, u32[]{:S(2)}, u32[]{:S(2)}) collective-permute-start(f32[2,128,128]{2,1,0:T(8,128)S(1)} %get-tuple-element.23), channel_id=1, source_target_pairs={{0,16},{8,24},{16,32},{24,40},{32,48},{40,56},{48,64},{56,72},{64,... | collective-permute-start | bytes 393224 | tf_op jit(solution)/shard_map/ppermute | solution.py:20
  19.8 19.7 %all-to-all-start = ((bf16[16,16,2]{1,2,0:T(2,128)(2,1)}), bf16[16,16,2]{1,2,0:T(2,128)(2,1)S(1)}, u32[]{:S(2)}, u32[]{:S(2)}) async-start(bf16[16,16,2]{1,2,0:T(2,128)(2,1)} %param.10), calls=%async_computation | async-start | bytes 16384 | tf_op jit(solution)/shard_map/all_to_all | solution.py:47
  29.9 291.0 %all-reduce.3.cloned.1.call-start = ((), (), s32[]{:S(2)}) async-start(), calls=%async_computation.2 | async-start | bytes 262144
  32.3 46.3 %collective-permute-start.2 = (f32[2,128,128]{2,1,0:T(8,128)S(1)}, f32[2,128,128]{2,1,0:T(8,128)S(1)}, u32[]{:S(2)}, u32[]{:S(2)}) collective-permute-start(f32[2,128,128]{2,1,0:T(8,128)S(1)} %add_select_fusion.11), channel_id=1, source_target_pairs={{0,16},{8,24},{16,32},{24,40},{32,48},{40,56},{48,64},{56,72},{64,... | collective-permute-start | bytes 393224 | tf_op jit(solution)/shard_map/ppermute | solution.py:20
  35.8 1.0 copy-start
  37.0 0.7 copy-start.4
  79.3 6.2 %collective-permute-start.3 = (f32[2,128,128]{2,1,0:T(8,128)S(1)}, f32[2,128,128]{2,1,0:T(8,128)S(1)}, u32[]{:S(2)}, u32[]{:S(2)}) collective-permute-start(f32[2,128,128]{2,1,0:T(8,128)S(1)} %add_select_fusion.10), channel_id=1, source_target_pairs={{0,32},{8,40},{16,48},{24,56},{32,64},{40,72},{48,80},{56,88},{64,... | collective-permute-start | bytes 393224 | tf_op jit(solution)/shard_map/ppermute | solution.py:20
  86.1 8.5 %collective-permute-start.4 = (f32[2,128,128]{2,1,0:T(8,128)S(1)}, f32[2,128,128]{2,1,0:T(8,128)S(1)}, u32[]{:S(2)}, u32[]{:S(2)}) collective-permute-start(f32[2,128,128]{2,1,0:T(8,128)S(1)} %add_select_fusion.9), channel_id=1, source_target_pairs={{0,64},{8,72},{16,80},{24,88},{32,96},{40,104},{48,112},{56,120},{... | collective-permute-start | bytes 393224 | tf_op jit(solution)/shard_map/ppermute | solution.py:20
  95.2 7.0 %collective-permute-start.5 = (f32[2,128,128]{2,1,0:T(8,128)S(1)}, f32[2,128,128]{2,1,0:T(8,128)S(1)}, u32[]{:S(2)}, u32[]{:S(2)}) collective-permute-start(f32[2,128,128]{2,1,0:T(8,128)S(1)} %add_select_fusion.8), channel_id=1, source_target_pairs={{0,128},{8,136},{16,144},{24,152},{32,160},{40,168},{48,176},{56,1... | collective-permute-start | bytes 393224 | tf_op jit(solution)/shard_map/ppermute | solution.py:20
  102.9 15.0 %collective-permute-start.6 = (f32[2,128,128]{2,1,0:T(8,128)S(1)}, f32[2,128,128]{2,1,0:T(8,128)S(1)}, u32[]{:S(2)}, u32[]{:S(2)}) collective-permute-start(f32[2,128,128]{2,1,0:T(8,128)S(1)} %add_select_fusion.7), channel_id=1, source_target_pairs={{0,256},{8,264},{16,272},{24,280},{32,288},{40,296},{48,304},{56,3... | collective-permute-start | bytes 393224 | tf_op jit(solution)/shard_map/ppermute | solution.py:20
  124.2 7.1 %collective-permute-start.7 = (f32[2,128,128]{2,1,0:T(8,128)S(1)}, f32[2,128,128]{2,1,0:T(8,128)}, u32[]{:S(2)}, u32[]{:S(2)}) collective-permute-start(f32[2,128,128]{2,1,0:T(8,128)S(1)} %get-tuple-element.20), channel_id=1, source_target_pairs={{8,0},{16,8},{24,16},{32,24},{40,32},{48,40},{56,48},{64,56},{72,6... | collective-permute-start | bytes 393224 | tf_op jit(solution)/shard_map/ppermute | solution.py:20
  128.4 7.2 %collective-permute-start.8 = (f32[2,128,128]{2,1,0:T(8,128)S(1)}, f32[2,128,128]{2,1,0:T(8,128)}, u32[]{:S(2)}, u32[]{:S(2)}) collective-permute-start(f32[2,128,128]{2,1,0:T(8,128)S(1)} %get-tuple-element.20), channel_id=1, source_target_pairs={{16,0},{24,8},{32,16},{40,24},{48,32},{56,40},{64,48},{72,56},{80,... | collective-permute-start | bytes 393224 | tf_op jit(solution)/shard_map/ppermute | solution.py:20
  137.2 125.9 %collective-permute-start.9 = (f32[2,128,128]{2,1,0:T(8,128)S(1)}, f32[2,128,128]{2,1,0:T(8,128)}, u32[]{:S(2)}, u32[]{:S(2)}) collective-permute-start(f32[2,128,128]{2,1,0:T(8,128)S(1)} %add_select_fusion.5), channel_id=1, source_target_pairs={{16,0},{24,8},{32,16},{40,24},{48,32},{56,40},{64,48},{72,56},{80,... | collective-permute-start | bytes 393224 | tf_op jit(solution)/shard_map/ppermute | solution.py:20
  264.7 7.2 %collective-permute-start.10 = (f32[2,128,128]{2,1,0:T(8,128)S(1)}, f32[2,128,128]{2,1,0:T(8,128)S(1)}, u32[]{:S(2)}, u32[]{:S(2)}) collective-permute-start(f32[2,128,128]{2,1,0:T(8,128)S(1)} %add_select_fusion.4), channel_id=1, source_target_pairs={{32,0},{40,8},{48,16},{56,24},{64,32},{72,40},{80,48},{88,56},{96,... | collective-permute-start | bytes 393224 | tf_op jit(solution)/shard_map/ppermute | solution.py:20
  272.6 5.7 %collective-permute-start.11 = (f32[2,128,128]{2,1,0:T(8,128)S(1)}, f32[2,128,128]{2,1,0:T(8,128)S(1)}, u32[]{:S(2)}, u32[]{:S(2)}) collective-permute-start(f32[2,128,128]{2,1,0:T(8,128)S(1)} %add_select_fusion.3), channel_id=1, source_target_pairs={{64,0},{72,8},{80,16},{88,24},{96,32},{104,40},{112,48},{120,56},{... | collective-permute-start | bytes 393224 | tf_op jit(solution)/shard_map/ppermute | solution.py:20
  278.9 50.6 %collective-permute-start.12 = (f32[2,128,128]{2,1,0:T(8,128)S(1)}, f32[2,128,128]{2,1,0:T(8,128)S(1)}, u32[]{:S(2)}, u32[]{:S(2)}) collective-permute-start(f32[2,128,128]{2,1,0:T(8,128)S(1)} %add_select_fusion.2), channel_id=1, source_target_pairs={{128,0},{136,8},{144,16},{152,24},{160,32},{168,40},{176,48},{184,... | collective-permute-start | bytes 393224 | tf_op jit(solution)/shard_map/ppermute | solution.py:20
  322.4 16.5 %all-to-all-start.1 = ((f32[2,128,2]{2,0,1:T(2,128)}), f32[2,128,2]{2,0,1:T(2,128)S(1)}, u32[]{:S(2)}, u32[]{:S(2)}) async-start(f32[2,128,2]{2,0,1:T(2,128)} %copy.154), calls=%async_computation.1 | async-start | bytes 262144 | tf_op jit(solution)/shard_map/all_to_all | solution.py:137
  330.1 10.9 %collective-permute-start.13 = (f32[2,128,128]{2,1,0:T(8,128)S(1)}, f32[2,128,128]{2,1,0:T(8,128)S(1)}, u32[]{:S(2)}, u32[]{:S(2)}) collective-permute-start(f32[2,128,128]{2,1,0:T(8,128)S(1)} %add_select_fusion.1), channel_id=1, source_target_pairs={{256,0},{264,8},{272,16},{280,24},{288,32},{296,40},{304,48},{312,... | collective-permute-start | bytes 393224 | tf_op jit(solution)/shard_map/ppermute | solution.py:20
Sparse Core Ops, SparseCore 0:
  131.5 189.3 all-reduce.2

commit v2 on v1

--- a/solution.py
+++ b/solution.py
@@ -45,8 +45,9 @@
 
 def local(queries, keys, values, feature_weight, norm_gain, doc_bounds, out_grad):
     head_groups = lax.all_to_all(feature_weight, "fsdp", split_axis=0, concat_axis=1, tiled=True)
-    weight_local = lax.all_gather(head_groups, "seq", axis=2, tiled=True)
-    head_count = weight_local.shape[0]
+    gathered = lax.all_gather(head_groups, "seq")
+    head_count, rows, _ = head_groups.shape
+    weight_local = gathered.transpose(1, 2, 0, 3).reshape(head_count, rows, -1)
     tokens_here = queries.shape[0]
     block_count = tokens_here // BLK
     block_shape = (block_count, BLK, head_count, HS)
@@ -104,7 +105,6 @@
     )
     grad_half = grad_mix.astype(jnp.bfloat16)
     gain_part = jnp.sum(grad_y * mixed_f * inverse, axis=(0, 1))
-    gain_sum = lax.psum(gain_part, "seq")
 
     state_grads = jnp.einsum(
         "bthe,bthf->bhef", qfeat, grad_half, preferred_element_type=jnp.float32
@@ -133,7 +133,12 @@
     weight_part = weight_part + jnp.einsum(
         "bhdf,bhef->hde", raw_states, state_grads, precision=HIGH
     )
-    weight_columns = lax.psum_scatter(weight_part, "seq", scatter_dimension=2, tiled=True)
+    summed = lax.psum(jnp.concatenate([weight_part, gain_part[:, None, :]], axis=1), "seq")
+    gain_sum = summed[:, HS, :]
+    column_width = HS // lax.axis_size("seq")
+    weight_columns = lax.dynamic_slice_in_dim(
+        summed[:, :HS, :], lax.axis_index("seq") * column_width, column_width, 2
+    )
     owned_grad = lax.all_to_all(weight_columns, "fsdp", split_axis=1, concat_axis=0, tiled=True)
 
     running = zero_state

time: 353 us -> 371 us (1.051)
  waiting for transfers between devices: 69.5 us -> 212 us
  blocking collectives: 163 us -> 38.6 us
    psum x0 -> x1, waiting for transfers between devices: none -> 174 us  [local(): lax.psum(jnp.concatenate([weight_part, gain_part[:, None, :]], axis=1), '...]
    psum x1 -> x0, blocking collectives: 124 us -> none  [local(): gain_sum = lax.psum(gain_part, 'seq')]
    unnamed x2 -> x1, waiting for transfers between devices: 40.1 us -> 0.02 us
    ppermute x14, waiting for transfers between devices: 21.9 us -> 37.3 us  [shifted(): return lax.ppermute(x, 'seq', pairs)]
    all_to_all x1, waiting for transfers between devices: 7.48 us -> 0.01 us  [local(): lax.all_to_all(weight_columns, 'fsdp', split_axis=1, concat_axis=0, tiled...]
  transfers between devices with their start and end apart: 17 -> 17, of which waited for: 10 -> 10; matrix products, arithmetic and copies ran while one was open for 5% -> 4% of each run, Pallas kernels for 0% -> 0%
where the time goes in v2:
time: 371 us; the launch traced here: 368 us
  waiting for transfers between devices  212 us (57%)
  starting transfers between devices  68.1 us (18%)
  blocking collectives  38.6 us (10%)
  other arithmetic  17.5 us (5%)
  between operations  14.6 us (4%)
  local copies, waits for them, and re-layouts  10.8 us (3%)
  matrix products  6.28 us (2%)
    psum x1, waiting for transfers between devices, local(): lax.psum(jnp.concatenate([weight_part, gain_part[:, None, :]], axis=1), '...  174 us
    ppermute x14, starting transfers between devices, shifted(): return lax.ppermute(x, 'seq', pairs)  50.9 us
    all_gather x1, blocking collectives, local(): gathered = lax.all_gather(head_groups, 'seq')  38.6 us
    ppermute x14, waiting for transfers between devices, shifted(): return lax.ppermute(x, 'seq', pairs)  37.3 us
    all_to_all x1, starting transfers between devices, local(): lax.all_to_all(feature_weight, 'fsdp', split_axis=0, concat_axis=1, tiled...  10 us
  transfers between devices with their start and end apart: 17, of which 10 were waited for; matrix products, arithmetic and copies ran while one was open for 4% of the time, Pallas kernels for 0%

profile of v2, /device:TPU:1, one launch (start us, length us, event | category | flops | bytes accessed | tf_op | source)
XLA Modules:
  0.0 367.7 jit_solution(9602351356460055505)
XLA Ops:
  10.2 2.0 fusion.48
  12.2 4.1 %collective-permute-start.1 = (f32[2,128,128]{2,1,0:T(8,128)S(1)}, f32[2,128,128]{2,1,0:T(8,128)S(1)}, u32[]{:S(2)}, u32[]{:S(2)}) collective-permute-start(f32[2,128,128]{2,1,0:T(8,128)S(1)} %get-tuple-element.23), channel_id=1, source_target_pairs={{0,16},{8,24},{16,32},{24,40},{32,48},{40,56},{48,64},{56,72},{64,... | collective-permute-start | bytes 393224 | tf_op jit(solution)/shard_map/ppermute | solution.py:20
  16.3 4.0 %collective-permute-start = (f32[2,128,128]{2,1,0:T(8,128)S(1)}, f32[2,128,128]{2,1,0:T(8,128)S(1)}, u32[]{:S(2)}, u32[]{:S(2)}) collective-permute-start(f32[2,128,128]{2,1,0:T(8,128)S(1)} %get-tuple-element.23), channel_id=1, source_target_pairs={{0,8},{8,16},{16,24},{24,32},{32,40},{40,48},{48,56},{56,64},{64,7... | collective-permute-start | bytes 393224 | tf_op jit(solution)/shard_map/ppermute | solution.py:20
  20.2 10.0 %all-to-all-start = ((bf16[16,16,2]{1,2,0:T(2,128)(2,1)}), bf16[16,16,2]{1,2,0:T(2,128)(2,1)S(1)}, u32[]{:S(2)}, u32[]{:S(2)}) async-start(bf16[16,16,2]{1,2,0:T(2,128)(2,1)} %param.10), calls=%async_computation | async-start | bytes 16384 | tf_op jit(solution)/shard_map/all_to_all | solution.py:47
  32.7 2.8 collective-permute-start.2
  38.3 38.6 %all_gather.7 = bf16[64,2,128,2]{2,3,1,0:T(2,128)(2,1)S(1)} all-gather(bf16[1,2,128,2]{2,3,1,0:T(2,128)(2,1)S(1)} %all_gather.6), channel_id=1, replica_groups=mesh['seq'=64,'fsdp'=8] {'seq'}, dimensions={0}, use_global_device_ids=true | all-gather | bytes 66560 | tf_op jit(solution)/shard_map/all_gather | solution.py:48
  77.7 3.3 collective-permute-start.3
  81.3 2.6 collective-permute-done.3
  84.6 6.5 %collective-permute-start.4 = (f32[2,128,128]{2,1,0:T(8,128)S(1)}, f32[2,128,128]{2,1,0:T(8,128)S(1)}, u32[]{:S(2)}, u32[]{:S(2)}) collective-permute-start(f32[2,128,128]{2,1,0:T(8,128)S(1)} %add_select_fusion.9), channel_id=1, source_target_pairs={{0,64},{8,72},{16,80},{24,88},{32,96},{40,104},{48,112},{56,120},{... | collective-permute-start | bytes 393224 | tf_op jit(solution)/shard_map/ppermute | solution.py:20
  91.4 1.7 collective-permute-done.4
  93.7 5.1 %collective-permute-start.5 = (f32[2,128,128]{2,1,0:T(8,128)S(1)}, f32[2,128,128]{2,1,0:T(8,128)S(1)}, u32[]{:S(2)}, u32[]{:S(2)}) collective-permute-start(f32[2,128,128]{2,1,0:T(8,128)S(1)} %add_select_fusion.8), channel_id=1, source_target_pairs={{0,128},{8,136},{16,144},{24,152},{32,160},{40,168},{48,176},{56,1... | collective-permute-start | bytes 393224 | tf_op jit(solution)/shard_map/ppermute | solution.py:20
  99.1 1.6 collective-permute-done.5
  101.4 13.1 %collective-permute-start.6 = (f32[2,128,128]{2,1,0:T(8,128)S(1)}, f32[2,128,128]{2,1,0:T(8,128)S(1)}, u32[]{:S(2)}, u32[]{:S(2)}) collective-permute-start(f32[2,128,128]{2,1,0:T(8,128)S(1)} %add_select_fusion.7), channel_id=1, source_target_pairs={{0,256},{8,264},{16,272},{24,280},{32,288},{40,296},{48,304},{56,3... | collective-permute-start | bytes 393224 | tf_op jit(solution)/shard_map/ppermute | solution.py:20
  114.8 1.6 collective-permute-done.6
  120.0 2.6 fusion.45
  123.9 4.2 %collective-permute-start.7 = (f32[2,128,128]{2,1,0:T(8,128)S(1)}, f32[2,128,128]{2,1,0:T(8,128)S(1)}, u32[]{:S(2)}, u32[]{:S(2)}) collective-permute-start(f32[2,128,128]{2,1,0:T(8,128)S(1)} %get-tuple-element.20), channel_id=1, source_target_pairs={{8,0},{16,8},{24,16},{32,24},{40,32},{48,40},{56,48},{64,56},{72,6... | collective-permute-start | bytes 393224 | tf_op jit(solution)/shard_map/ppermute | solution.py:20
  129.2 3.8 %collective-permute-done.7 = f32[2,128,128]{2,1,0:T(8,128)S(1)} collective-permute-done((f32[2,128,128]{2,1,0:T(8,128)S(1)}, f32[2,128,128]{2,1,0:T(8,128)S(1)}, u32[]{:S(2)}, u32[]{:S(2)}) %collective-permute-start.7) | collective-permute-done | bytes 131104 | tf_op jit(solution)/shard_map/ppermute | solution.py:20
  136.4 3.7 %collective-permute-done.9 = f32[2,128,128]{2,1,0:T(8,128)} collective-permute-done((f32[2,128,128]{2,1,0:T(8,128)S(1)}, f32[2,128,128]{2,1,0:T(8,128)}, u32[]{:S(2)}, u32[]{:S(2)}) %collective-permute-start.9) | collective-permute-done | bytes 131104 | tf_op jit(solution)/shard_map/ppermute | solution.py:20
  140.1 1.6 add_select_fusion.4
  143.8 6.4 %collective-permute-done.10 = f32[2,128,128]{2,1,0:T(8,128)S(1)} collective-permute-done((f32[2,128,128]{2,1,0:T(8,128)S(1)}, f32[2,128,128]{2,1,0:T(8,128)S(1)}, u32[]{:S(2)}, u32[]{:S(2)}) %collective-permute-start.10) | collective-permute-done | bytes 131104 | tf_op jit(solution)/shard_map/ppermute | solution.py:20
  152.8 174.5 %all-reduce.2.cloned.1.call-done = f32[2,129,128]{2,1,0:T(8,128)} async-done(((f32[2,129,128]{2,1,0:T(8,128)}), f32[2,129,128]{2,1,0:T(8,128)}) %all-reduce.2.cloned.1.call-update) | async-done | bytes 132112 | tf_op jit(solution)/shard_map/psum | solution.py:136
  329.0 7.1 %all-to-all-start.1 = ((f32[2,128,2]{2,0,1:T(2,128)}), f32[2,128,2]{2,0,1:T(2,128)S(1)}, u32[]{:S(2)}, u32[]{:S(2)}) async-start(f32[2,128,2]{2,0,1:T(2,128)} %copy.163), calls=%async_computation.1 | async-start | bytes 262144 | tf_op jit(solution)/shard_map/all_to_all | solution.py:142
  338.7 8.1 %collective-permute-done.12 = f32[2,128,128]{2,1,0:T(8,128)S(1)} collective-permute-done((f32[2,128,128]{2,1,0:T(8,128)S(1)}, f32[2,128,128]{2,1,0:T(8,128)S(1)}, u32[]{:S(2)}, u32[]{:S(2)}) %collective-permute-start.12) | collective-permute-done | bytes 131104 | tf_op jit(solution)/shard_map/ppermute | solution.py:20
  349.7 7.8 %collective-permute-done.13 = f32[2,128,128]{2,1,0:T(8,128)S(1)} collective-permute-done((f32[2,128,128]{2,1,0:T(8,128)S(1)}, f32[2,128,128]{2,1,0:T(8,128)S(1)}, u32[]{:S(2)}, u32[]{:S(2)}) %collective-permute-start.13) | collective-permute-done | bytes 131104 | tf_op jit(solution)/shard_map/ppermute | solution.py:20
  (102 shorter events, 36.3 us)
Async XLA Ops:
  8.7 1.1 copy-start.2
  12.2 24.6 %copy-start.3 = (bf16[512,256]{1,0:T(8,128)(2,1)S(1)}, bf16[512,256]{1,0:T(8,128)(2,1)}, u32[]{:S(2)}) copy-start(bf16[512,256]{1,0:T(8,128)(2,1)} %param.7) | copy-start | bytes 786436
  12.2 19.8 %collective-permute-start.1 = (f32[2,128,128]{2,1,0:T(8,128)S(1)}, f32[2,128,128]{2,1,0:T(8,128)S(1)}, u32[]{:S(2)}, u32[]{:S(2)}) collective-permute-start(f32[2,128,128]{2,1,0:T(8,128)S(1)} %get-tuple-element.23), channel_id=1, source_target_pairs={{0,16},{8,24},{16,32},{24,40},{32,48},{40,56},{48,64},{56,72},{64,... | collective-permute-start | bytes 393224 | tf_op jit(solution)/shard_map/ppermute | solution.py:20
  16.3 15.7 %collective-permute-start = (f32[2,128,128]{2,1,0:T(8,128)S(1)}, f32[2,128,128]{2,1,0:T(8,128)S(1)}, u32[]{:S(2)}, u32[]{:S(2)}) collective-permute-start(f32[2,128,128]{2,1,0:T(8,128)S(1)} %get-tuple-element.23), channel_id=1, source_target_pairs={{0,8},{8,16},{16,24},{24,32},{32,40},{40,48},{48,56},{56,64},{64,7... | collective-permute-start | bytes 393224 | tf_op jit(solution)/shard_map/ppermute | solution.py:20
  20.2 18.0 %all-to-all-start = ((bf16[16,16,2]{1,2,0:T(2,128)(2,1)}), bf16[16,16,2]{1,2,0:T(2,128)(2,1)S(1)}, u32[]{:S(2)}, u32[]{:S(2)}) async-start(bf16[16,16,2]{1,2,0:T(2,128)(2,1)} %param.10), calls=%async_computation | async-start | bytes 16384 | tf_op jit(solution)/shard_map/all_to_all | solution.py:47
  30.3 296.9 %all-reduce.2.cloned.1.call-start = ((), (), s32[]{:S(2)}) async-start(), calls=%async_computation.2 | async-start | bytes 278528 | tf_op jit(solution)/shard_map/psum | solution.py:136
  32.7 44.3 %collective-permute-start.2 = (f32[2,128,128]{2,1,0:T(8,128)S(1)}, f32[2,128,128]{2,1,0:T(8,128)S(1)}, u32[]{:S(2)}, u32[]{:S(2)}) collective-permute-start(f32[2,128,128]{2,1,0:T(8,128)S(1)} %add_select_fusion.11), channel_id=1, source_target_pairs={{0,16},{8,24},{16,32},{24,40},{32,48},{40,56},{48,64},{56,72},{64,... | collective-permute-start | bytes 393224 | tf_op jit(solution)/shard_map/ppermute | solution.py:20
  36.8 1.0 copy-start.1
  77.7 6.2 %collective-permute-start.3 = (f32[2,128,128]{2,1,0:T(8,128)S(1)}, f32[2,128,128]{2,1,0:T(8,128)S(1)}, u32[]{:S(2)}, u32[]{:S(2)}) collective-permute-start(f32[2,128,128]{2,1,0:T(8,128)S(1)} %add_select_fusion.10), channel_id=1, source_target_pairs={{0,32},{8,40},{16,48},{24,56},{32,64},{40,72},{48,80},{56,88},{64,... | collective-permute-start | bytes 393224 | tf_op jit(solution)/shard_map/ppermute | solution.py:20
  84.6 8.5 %collective-permute-start.4 = (f32[2,128,128]{2,1,0:T(8,128)S(1)}, f32[2,128,128]{2,1,0:T(8,128)S(1)}, u32[]{:S(2)}, u32[]{:S(2)}) collective-permute-start(f32[2,128,128]{2,1,0:T(8,128)S(1)} %add_select_fusion.9), channel_id=1, source_target_pairs={{0,64},{8,72},{16,80},{24,88},{32,96},{40,104},{48,112},{56,120},{... | collective-permute-start | bytes 393224 | tf_op jit(solution)/shard_map/ppermute | solution.py:20
  93.7 7.0 %collective-permute-start.5 = (f32[2,128,128]{2,1,0:T(8,128)S(1)}, f32[2,128,128]{2,1,0:T(8,128)S(1)}, u32[]{:S(2)}, u32[]{:S(2)}) collective-permute-start(f32[2,128,128]{2,1,0:T(8,128)S(1)} %add_select_fusion.8), channel_id=1, source_target_pairs={{0,128},{8,136},{16,144},{24,152},{32,160},{40,168},{48,176},{56,1... | collective-permute-start | bytes 393224 | tf_op jit(solution)/shard_map/ppermute | solution.py:20
  101.4 15.0 %collective-permute-start.6 = (f32[2,128,128]{2,1,0:T(8,128)S(1)}, f32[2,128,128]{2,1,0:T(8,128)S(1)}, u32[]{:S(2)}, u32[]{:S(2)}) collective-permute-start(f32[2,128,128]{2,1,0:T(8,128)S(1)} %add_select_fusion.7), channel_id=1, source_target_pairs={{0,256},{8,264},{16,272},{24,280},{32,288},{40,296},{48,304},{56,3... | collective-permute-start | bytes 393224 | tf_op jit(solution)/shard_map/ppermute | solution.py:20
  117.1 2.3 copy-start.4
  122.6 6.5 %collective-permute-start.8 = (f32[2,128,128]{2,1,0:T(8,128)S(1)}, f32[2,128,128]{2,1,0:T(8,128)S(1)}, u32[]{:S(2)}, u32[]{:S(2)}) collective-permute-start(f32[2,128,128]{2,1,0:T(8,128)S(1)} %get-tuple-element.20), channel_id=1, source_target_pairs={{16,0},{24,8},{32,16},{40,24},{48,32},{56,40},{64,48},{72,56},{80,... | collective-permute-start | bytes 393224 | tf_op jit(solution)/shard_map/ppermute | solution.py:20
  123.9 9.1 %collective-permute-start.7 = (f32[2,128,128]{2,1,0:T(8,128)S(1)}, f32[2,128,128]{2,1,0:T(8,128)S(1)}, u32[]{:S(2)}, u32[]{:S(2)}) collective-permute-start(f32[2,128,128]{2,1,0:T(8,128)S(1)} %get-tuple-element.20), channel_id=1, source_target_pairs={{8,0},{16,8},{24,16},{32,24},{40,32},{48,40},{56,48},{64,56},{72,6... | collective-permute-start | bytes 393224 | tf_op jit(solution)/shard_map/ppermute | solution.py:20
  133.7 6.4 %collective-permute-start.9 = (f32[2,128,128]{2,1,0:T(8,128)S(1)}, f32[2,128,128]{2,1,0:T(8,128)}, u32[]{:S(2)}, u32[]{:S(2)}) collective-permute-start(f32[2,128,128]{2,1,0:T(8,128)S(1)} %add_select_fusion.5), channel_id=1, source_target_pairs={{16,0},{24,8},{32,16},{40,24},{48,32},{56,40},{64,48},{72,56},{80,... | collective-permute-start | bytes 393224 | tf_op jit(solution)/shard_map/ppermute | solution.py:20
  141.7 8.5 %collective-permute-start.10 = (f32[2,128,128]{2,1,0:T(8,128)S(1)}, f32[2,128,128]{2,1,0:T(8,128)S(1)}, u32[]{:S(2)}, u32[]{:S(2)}) collective-permute-start(f32[2,128,128]{2,1,0:T(8,128)S(1)} %add_select_fusion.4), channel_id=1, source_target_pairs={{32,0},{40,8},{48,16},{56,24},{64,32},{72,40},{80,48},{88,56},{96,... | collective-permute-start | bytes 393224 | tf_op jit(solution)/shard_map/ppermute | solution.py:20
  150.8 185.3 %collective-permute-start.11 = (f32[2,128,128]{2,1,0:T(8,128)S(1)}, f32[2,128,128]{2,1,0:T(8,128)S(1)}, u32[]{:S(2)}, u32[]{:S(2)}) collective-permute-start(f32[2,128,128]{2,1,0:T(8,128)S(1)} %add_select_fusion.3), channel_id=1, source_target_pairs={{64,0},{72,8},{80,16},{88,24},{96,32},{104,40},{112,48},{120,56},{... | collective-permute-start | bytes 393224 | tf_op jit(solution)/shard_map/ppermute | solution.py:20
  327.2 0.9 slice-start
  329.0 19.8 %all-to-all-start.1 = ((f32[2,128,2]{2,0,1:T(2,128)}), f32[2,128,2]{2,0,1:T(2,128)S(1)}, u32[]{:S(2)}, u32[]{:S(2)}) async-start(f32[2,128,2]{2,0,1:T(2,128)} %copy.163), calls=%async_computation.1 | async-start | bytes 262144 | tf_op jit(solution)/shard_map/all_to_all | solution.py:142
  336.1 2.1 copy-start
  336.9 9.9 %collective-permute-start.12 = (f32[2,128,128]{2,1,0:T(8,128)S(1)}, f32[2,128,128]{2,1,0:T(8,128)S(1)}, u32[]{:S(2)}, u32[]{:S(2)}) collective-permute-start(f32[2,128,128]{2,1,0:T(8,128)S(1)} %add_select_fusion.2), channel_id=1, source_target_pairs={{128,0},{136,8},{144,16},{152,24},{160,32},{168,40},{176,48},{184,... | collective-permute-start | bytes 393224 | tf_op jit(solution)/shard_map/ppermute | solution.py:20
  347.5 9.9 %collective-permute-start.13 = (f32[2,128,128]{2,1,0:T(8,128)S(1)}, f32[2,128,128]{2,1,0:T(8,128)S(1)}, u32[]{:S(2)}, u32[]{:S(2)}) collective-permute-start(f32[2,128,128]{2,1,0:T(8,128)S(1)} %add_select_fusion.1), channel_id=1, source_target_pairs={{256,0},{264,8},{272,16},{280,24},{288,32},{296,40},{304,48},{312,... | collective-permute-start | bytes 393224 | tf_op jit(solution)/shard_map/ppermute | solution.py:20
  357.4 0.9 copy-start.5
  (2 other events, 1.3 us)
Sparse Core Ops, SparseCore 0:
  136.5 190.6 all-reduce.1

commit v3 on v1

--- a/solution.py
+++ b/solution.py
@@ -44,9 +44,18 @@
 
 
 def local(queries, keys, values, feature_weight, norm_gain, doc_bounds, out_grad):
-    head_groups = lax.all_to_all(feature_weight, "fsdp", split_axis=0, concat_axis=1, tiled=True)
-    weight_local = lax.all_gather(head_groups, "seq", axis=2, tiled=True)
-    head_count = weight_local.shape[0]
+    seq_count = lax.axis_size("seq")
+    fsdp_count = lax.axis_size("fsdp")
+    all_heads, rows, columns = feature_weight.shape
+    head_count = all_heads // fsdp_count
+    gathered = lax.all_gather(feature_weight, ("seq", "fsdp"))
+    weight_full = (
+        gathered.reshape(seq_count, fsdp_count, all_heads, rows, columns)
+        .transpose(2, 1, 3, 0, 4)
+        .reshape(all_heads, rows * fsdp_count, columns * seq_count)
+    )
+    group = lax.axis_index("fsdp")
+    weight_local = lax.dynamic_slice_in_dim(weight_full, group * head_count, head_count, 0)
     tokens_here = queries.shape[0]
     block_count = tokens_here // BLK
     block_shape = (block_count, BLK, head_count, HS)
@@ -104,7 +113,6 @@
     )
     grad_half = grad_mix.astype(jnp.bfloat16)
     gain_part = jnp.sum(grad_y * mixed_f * inverse, axis=(0, 1))
-    gain_sum = lax.psum(gain_part, "seq")
 
     state_grads = jnp.einsum(
         "bthe,bthf->bhef", qfeat, grad_half, preferred_element_type=jnp.float32
@@ -133,8 +141,14 @@
     weight_part = weight_part + jnp.einsum(
         "bhdf,bhef->hde", raw_states, state_grads, precision=HIGH
     )
-    weight_columns = lax.psum_scatter(weight_part, "seq", scatter_dimension=2, tiled=True)
-    owned_grad = lax.all_to_all(weight_columns, "fsdp", split_axis=1, concat_axis=0, tiled=True)
+    own_slot = jnp.concatenate([weight_part, gain_part[:, None, :]], axis=1)
+    slots = jnp.zeros((all_heads,) + own_slot.shape[1:], jnp.float32)
+    slots = lax.dynamic_update_slice_in_dim(slots, own_slot, group * head_count, 0)
+    summed = lax.psum(slots, ("seq", "fsdp"))
+    gain_sum = lax.dynamic_slice_in_dim(summed[:, HS, :], group * head_count, head_count, 0)
+    owned_grad = lax.dynamic_slice(
+        summed, (0, group * rows, place * columns), (all_heads, rows, columns)
+    )
 
     running = zero_state
     suffix_list = [zero_state] * block_count

time: 353 us -> 497 us (1.41)
  waiting for transfers between devices: 69.5 us -> 289 us
  blocking collectives: 163 us -> 83.3 us
  local copies, waits for them, and re-layouts: 11.1 us -> 21.3 us
  starting transfers between devices: 67.8 us -> 59.2 us
    psum x0 -> x1, waiting for transfers between devices: none -> 262 us  [local(): summed = lax.psum(slots, ('seq', 'fsdp'))]
    psum x1 -> x0, blocking collectives: 124 us -> none  [local(): gain_sum = lax.psum(gain_part, 'seq')]
    all_gather x1, blocking collectives: 38.9 us -> 83.3 us  [local(): gathered = lax.all_gather(feature_weight, ('seq', 'fsdp'))]
    unnamed x2 -> x1, waiting for transfers between devices: 40.1 us -> 0.02 us
    all_to_all x2 -> x0, starting transfers between devices: 17.1 us -> none  [the longest x1 10 us: local(): lax.all_to_all(feature_weight, 'fsdp', split_axis=0, concat_axis=1, tiled...]
    reshape x0 -> x2, local copies, waits for them, and re-layouts: none -> 9.74 us  [the longest x1 5.12 us: local(): weight_full = gathered.reshape(seq_count, fsdp_count, all_heads, rows, co...]
    ppermute x14, starting transfers between devices: 50.6 us -> 59.2 us  [shifted(): return lax.ppermute(x, 'seq', pairs)]
    all_to_all x2 -> x0, waiting for transfers between devices: 7.49 us -> none  [the longest x1 7.48 us: local(): lax.all_to_all(weight_columns, 'fsdp', split_axis=1, concat_axis=0, tiled...]
  transfers between devices with their start and end apart: 17 -> 15, of which waited for: 10 -> 11; matrix products, arithmetic and copies ran while one was open for 5% -> 5% of each run, Pallas kernels for 0% -> 0%
where the time goes in v3:
time: 497 us; the launch traced here: 496 us
  waiting for transfers between devices  289 us (58%)
  blocking collectives  83.3 us (17%)
  starting transfers between devices  59.2 us (12%)
  local copies, waits for them, and re-layouts  21.3 us (4%)
  other arithmetic  20.6 us (4%)
  between operations  14.7 us (3%)
  matrix products  7.25 us (1%)
    psum x1, waiting for transfers between devices, local(): summed = lax.psum(slots, ('seq', 'fsdp'))  262 us
    all_gather x1, blocking collectives, local(): gathered = lax.all_gather(feature_weight, ('seq', 'fsdp'))  83.3 us
    ppermute x14, starting transfers between devices, shifted(): return lax.ppermute(x, 'seq', pairs)  59.2 us
    ppermute x14, waiting for transfers between devices, shifted(): return lax.ppermute(x, 'seq', pairs)  27.5 us
  transfers between devices with their start and end apart: 15, of which 11 were waited for; matrix products, arithmetic and copies ran while one was open for 5% of the time, Pallas kernels for 0%

profile of v3, /device:TPU:1, one launch (start us, length us, event | category | flops | bytes accessed | tf_op | source)
XLA Modules:
  0.0 495.6 jit_solution(3536623835408504418)
XLA Ops:
  10.5 2.6 fusion.48
  13.1 4.5 collective-permute-start
  17.6 3.1 collective-permute-start.1
  20.8 83.3 %all-gather = bf16[8192,16,2]{1,2,0:T(2,128)(2,1)S(1)} all-gather(bf16[16,16,2]{1,2,0:T(2,128)(2,1)S(1)} %copy-done.18), channel_id=2, replica_groups=mesh['seq'=64,'fsdp'=8] {'seq','fsdp'}, dimensions={0}, use_global_device_ids=true | all-gather | bytes 525312 | tf_op jit(solution)/shard_map/all_gather | solution.py:51
  104.1 4.6 copy.246
  108.7 5.1 %reshape.114 = bf16[16,128,128]{1,2,0:T(8,128)(2,1)S(1)} reshape(bf16[16,8,16,64,2]{2,1,4,3,0:T(8,128)(2,1)} %bitcast.122) | data formatting | bytes 1048576 | tf_op jit(solution)/shard_map/reshape | solution.py:55
  115.8 2.7 collective-permute-start.2
  118.7 1.7 collective-permute-done.2
  121.0 5.1 %collective-permute-start.3 = (f32[2,128,128]{2,1,0:T(8,128)S(1)}, f32[2,128,128]{2,1,0:T(8,128)S(1)}, u32[]{:S(2)}, u32[]{:S(2)}) collective-permute-start(f32[2,128,128]{2,1,0:T(8,128)S(1)} %add_select_fusion.10), channel_id=1, source_target_pairs={{0,32},{8,40},{16,48},{24,56},{32,64},{40,72},{48,80},{56,88},{64,... | collective-permute-start | bytes 393224 | tf_op jit(solution)/shard_map/ppermute | solution.py:20
  128.8 6.6 %collective-permute-start.4 = (f32[2,128,128]{2,1,0:T(8,128)S(1)}, f32[2,128,128]{2,1,0:T(8,128)S(1)}, u32[]{:S(2)}, u32[]{:S(2)}) collective-permute-start(f32[2,128,128]{2,1,0:T(8,128)S(1)} %add_select_fusion.9), channel_id=1, source_target_pairs={{0,64},{8,72},{16,80},{24,88},{32,96},{40,104},{48,112},{56,120},{... | collective-permute-start | bytes 393224 | tf_op jit(solution)/shard_map/ppermute | solution.py:20
  135.7 1.6 collective-permute-done.4
  138.1 5.6 %collective-permute-start.5 = (f32[2,128,128]{2,1,0:T(8,128)S(1)}, f32[2,128,128]{2,1,0:T(8,128)S(1)}, u32[]{:S(2)}, u32[]{:S(2)}) collective-permute-start(f32[2,128,128]{2,1,0:T(8,128)S(1)} %add_select_fusion.8), channel_id=1, source_target_pairs={{0,128},{8,136},{16,144},{24,152},{32,160},{40,168},{48,176},{56,1... | collective-permute-start | bytes 393224 | tf_op jit(solution)/shard_map/ppermute | solution.py:20
  144.1 2.1 collective-permute-done.5
  146.8 11.1 %collective-permute-start.6 = (f32[2,128,128]{2,1,0:T(8,128)S(1)}, f32[2,128,128]{2,1,0:T(8,128)S(1)}, u32[]{:S(2)}, u32[]{:S(2)}) collective-permute-start(f32[2,128,128]{2,1,0:T(8,128)S(1)} %add_select_fusion.7), channel_id=1, source_target_pairs={{0,256},{8,264},{16,272},{24,280},{32,288},{40,296},{48,304},{56,3... | collective-permute-start | bytes 393224 | tf_op jit(solution)/shard_map/ppermute | solution.py:20
  163.6 3.2 fusion.45
  166.8 12.5 %collective-permute-start.7 = (f32[2,128,128]{2,1,0:T(8,128)S(1)}, f32[2,128,128]{2,1,0:T(8,128)S(1)}, u32[]{:S(2)}, u32[]{:S(2)}) collective-permute-start(f32[2,128,128]{2,1,0:T(8,128)S(1)} %get-tuple-element.44), channel_id=1, source_target_pairs={{8,0},{16,8},{24,16},{32,24},{40,32},{48,40},{56,48},{64,56},{72,6... | collective-permute-start | bytes 393224 | tf_op jit(solution)/shard_map/ppermute | solution.py:20
  182.6 3.8 collective-permute-done.8
  190.4 3.2 collective-permute-done.9
  197.4 5.0 %collective-permute-done.10 = f32[2,128,128]{2,1,0:T(8,128)} collective-permute-done((f32[2,128,128]{2,1,0:T(8,128)}, f32[2,128,128]{2,1,0:T(8,128)}, u32[]{:S(2)}, u32[]{:S(2)}) %collective-permute-start.10) | collective-permute-done | bytes 131104 | tf_op jit(solution)/shard_map/ppermute | solution.py:20
  202.4 1.6 add_select_fusion.3
  205.3 1.8 copy_bitcast_fusion.3
  207.1 2.6 collective-permute-done.11
  212.3 5.8 %collective-permute-done.12 = f32[2,128,128]{2,1,0:T(8,128)S(1)} collective-permute-done((f32[2,128,128]{2,1,0:T(8,128)S(1)}, f32[2,128,128]{2,1,0:T(8,128)S(1)}, u32[]{:S(2)}, u32[]{:S(2)}) %collective-permute-start.12) | collective-permute-done | bytes 131104 | tf_op jit(solution)/shard_map/ppermute | solution.py:20
  219.9 261.6 %all-reduce.2.cloned.1.call-done = f32[16,129,128]{2,0,1:T(8,128)} async-done(((f32[16,129,128]{2,0,1:T(8,128)}), f32[16,129,128]{2,0,1:T(8,128)}) %all-reduce.2.cloned.1.call-update) | async-done | bytes 1056784 | tf_op jit(solution)/shard_map/psum | solution.py:147
  (122 shorter events, 40.0 us)
Async XLA Ops:
  7.2 474.3 %all-reduce.2.cloned.1.call-start = ((), (), s32[]{:S(2)}) async-start(), calls=%async_computation | async-start | bytes 2113536 | tf_op jit(solution)/shard_map/psum | solution.py:147
  13.1 147.5 %copy-start.10 = (f32[1,2,128,128]{3,2,1,0:T(8,128)}, f32[1,2,128,128]{3,2,1,0:T(8,128)S(1)}, u32[]{:S(2)}) copy-start(f32[1,2,128,128]{3,2,1,0:T(8,128)S(1)} %get-tuple-element.48) | copy-start | bytes 393220
  13.1 101.9 %collective-permute-start = (f32[2,128,128]{2,1,0:T(8,128)S(1)}, f32[2,128,128]{2,1,0:T(8,128)S(1)}, u32[]{:S(2)}, u32[]{:S(2)}) collective-permute-start(f32[2,128,128]{2,1,0:T(8,128)S(1)} %get-tuple-element.47), channel_id=1, source_target_pairs={{0,8},{8,16},{16,24},{24,32},{32,40},{40,48},{48,56},{56,64},{64,7... | collective-permute-start | bytes 393224 | tf_op jit(solution)/shard_map/ppermute | solution.py:20
  17.6 97.4 %collective-permute-start.1 = (f32[2,128,128]{2,1,0:T(8,128)S(1)}, f32[2,128,128]{2,1,0:T(8,128)S(1)}, u32[]{:S(2)}, u32[]{:S(2)}) collective-permute-start(f32[2,128,128]{2,1,0:T(8,128)S(1)} %get-tuple-element.47), channel_id=1, source_target_pairs={{0,16},{8,24},{16,32},{24,40},{32,48},{40,56},{48,64},{56,72},{64,... | collective-permute-start | bytes 393224 | tf_op jit(solution)/shard_map/ppermute | solution.py:20
  114.0 21.4 %copy-start.1 = (bf16[4,128,2,128]{1,3,0,2:T(8,128)(2,1)}, bf16[4,128,2,128]{1,3,0,2:T(8,128)(2,1)S(1)}, u32[]{:S(2)}) copy-start(bf16[4,128,2,128]{1,3,0,2:T(8,128)(2,1)S(1)} %fusion.11) | copy-start | bytes 786436
  115.8 4.7 collective-permute-start.2
  121.0 7.1 %collective-permute-start.3 = (f32[2,128,128]{2,1,0:T(8,128)S(1)}, f32[2,128,128]{2,1,0:T(8,128)S(1)}, u32[]{:S(2)}, u32[]{:S(2)}) collective-permute-start(f32[2,128,128]{2,1,0:T(8,128)S(1)} %add_select_fusion.10), channel_id=1, source_target_pairs={{0,32},{8,40},{16,48},{24,56},{32,64},{40,72},{48,80},{56,88},{64,... | collective-permute-start | bytes 393224 | tf_op jit(solution)/shard_map/ppermute | solution.py:20
  128.8 8.5 %collective-permute-start.4 = (f32[2,128,128]{2,1,0:T(8,128)S(1)}, f32[2,128,128]{2,1,0:T(8,128)S(1)}, u32[]{:S(2)}, u32[]{:S(2)}) collective-permute-start(f32[2,128,128]{2,1,0:T(8,128)S(1)} %add_select_fusion.9), channel_id=1, source_target_pairs={{0,64},{8,72},{16,80},{24,88},{32,96},{40,104},{48,112},{56,120},{... | collective-permute-start | bytes 393224 | tf_op jit(solution)/shard_map/ppermute | solution.py:20
  135.7 24.8 %copy-start.4 = (bf16[4,2,128,128]{3,2,1,0:T(8,128)(2,1)}, bf16[4,2,128,128]{3,2,1,0:T(8,128)(2,1)S(1)}, u32[]{:S(2)}) copy-start(bf16[4,2,128,128]{3,2,1,0:T(8,128)(2,1)S(1)} %fusion.1) | copy-start | bytes 786436
  138.1 22.5 %copy-start.12 = (f32[1,2,128,128]{3,2,1,0:T(8,128)S(1)}, f32[1,2,128,128]{3,2,1,0:T(8,128)}, u32[]{:S(2)}) copy-start(f32[1,2,128,128]{3,2,1,0:T(8,128)} %get-tuple-element.49) | copy-start | bytes 393220
  138.1 22.5 %copy-start.13 = (f32[1,2,128,128]{3,2,1,0:T(8,128)S(1)}, f32[1,2,128,128]{3,2,1,0:T(8,128)}, u32[]{:S(2)}) copy-start(f32[1,2,128,128]{3,2,1,0:T(8,128)} %get-tuple-element.50) | copy-start | bytes 393220
  138.1 8.1 %collective-permute-start.5 = (f32[2,128,128]{2,1,0:T(8,128)S(1)}, f32[2,128,128]{2,1,0:T(8,128)S(1)}, u32[]{:S(2)}, u32[]{:S(2)}) collective-permute-start(f32[2,128,128]{2,1,0:T(8,128)S(1)} %add_select_fusion.8), channel_id=1, source_target_pairs={{0,128},{8,136},{16,144},{24,152},{32,160},{40,168},{48,176},{56,1... | collective-permute-start | bytes 393224 | tf_op jit(solution)/shard_map/ppermute | solution.py:20
  146.8 13.0 %collective-permute-start.6 = (f32[2,128,128]{2,1,0:T(8,128)S(1)}, f32[2,128,128]{2,1,0:T(8,128)S(1)}, u32[]{:S(2)}, u32[]{:S(2)}) collective-permute-start(f32[2,128,128]{2,1,0:T(8,128)S(1)} %add_select_fusion.7), channel_id=1, source_target_pairs={{0,256},{8,264},{16,272},{24,280},{32,288},{40,296},{48,304},{56,3... | collective-permute-start | bytes 393224 | tf_op jit(solution)/shard_map/ppermute | solution.py:20
  166.8 15.8 %collective-permute-start.7 = (f32[2,128,128]{2,1,0:T(8,128)S(1)}, f32[2,128,128]{2,1,0:T(8,128)S(1)}, u32[]{:S(2)}, u32[]{:S(2)}) collective-permute-start(f32[2,128,128]{2,1,0:T(8,128)S(1)} %get-tuple-element.44), channel_id=1, source_target_pairs={{8,0},{16,8},{24,16},{32,24},{40,32},{48,40},{56,48},{64,56},{72,6... | collective-permute-start | bytes 393224 | tf_op jit(solution)/shard_map/ppermute | solution.py:20
  179.3 7.1 %collective-permute-start.8 = (f32[2,128,128]{2,1,0:T(8,128)S(1)}, f32[2,128,128]{2,1,0:T(8,128)S(1)}, u32[]{:S(2)}, u32[]{:S(2)}) collective-permute-start(f32[2,128,128]{2,1,0:T(8,128)S(1)} %get-tuple-element.44), channel_id=1, source_target_pairs={{16,0},{24,8},{32,16},{40,24},{48,32},{56,40},{64,48},{72,56},{80,... | collective-permute-start | bytes 393224 | tf_op jit(solution)/shard_map/ppermute | solution.py:20
  187.1 6.6 %collective-permute-start.9 = (f32[2,128,128]{2,1,0:T(8,128)S(1)}, f32[2,128,128]{2,1,0:T(8,128)S(1)}, u32[]{:S(2)}, u32[]{:S(2)}) collective-permute-start(f32[2,128,128]{2,1,0:T(8,128)S(1)} %add_select_fusion.5), channel_id=1, source_target_pairs={{16,0},{24,8},{32,16},{40,24},{48,32},{56,40},{64,48},{72,56},{80,... | collective-permute-start | bytes 393224 | tf_op jit(solution)/shard_map/ppermute | solution.py:20
  194.9 7.5 %collective-permute-start.10 = (f32[2,128,128]{2,1,0:T(8,128)}, f32[2,128,128]{2,1,0:T(8,128)}, u32[]{:S(2)}, u32[]{:S(2)}) collective-permute-start(f32[2,128,128]{2,1,0:T(8,128)} %add_select_fusion.4), channel_id=1, source_target_pairs={{32,0},{40,8},{48,16},{56,24},{64,32},{72,40},{80,48},{88,56},{96,... | collective-permute-start | bytes 393224 | tf_op jit(solution)/shard_map/ppermute | solution.py:20
  203.9 5.7 %collective-permute-start.11 = (f32[2,128,128]{2,1,0:T(8,128)S(1)}, f32[2,128,128]{2,1,0:T(8,128)S(1)}, u32[]{:S(2)}, u32[]{:S(2)}) collective-permute-start(f32[2,128,128]{2,1,0:T(8,128)S(1)} %add_select_fusion.3), channel_id=1, source_target_pairs={{64,0},{72,8},{80,16},{88,24},{96,32},{104,40},{112,48},{120,56},{... | collective-permute-start | bytes 393224 | tf_op jit(solution)/shard_map/ppermute | solution.py:20
  207.1 278.2 %copy-start.3 = (bf16[4,128,2,128]{1,3,0,2:T(8,128)(2,1)S(1)}, bf16[4,128,2,128]{1,3,0,2:T(8,128)(2,1)}, u32[]{:S(2)}) copy-start(bf16[4,128,2,128]{1,3,0,2:T(8,128)(2,1)} %copy-done.1) | copy-start | bytes 786436
  207.1 278.2 %copy-start.14 = (f32[1,2,128,128]{3,2,1,0:T(8,128)S(1)}, f32[1,2,128,128]{3,2,1,0:T(8,128)}, u32[]{:S(2)}) copy-start(f32[1,2,128,128]{3,2,1,0:T(8,128)} %get-tuple-element.46) | copy-start | bytes 393220
  207.1 278.2 %copy-start.16 = (f32[1,2,128,128]{3,2,1,0:T(8,128)S(1)}, f32[1,2,128,128]{3,2,1,0:T(8,128)}, u32[]{:S(2)}) copy-start(f32[1,2,128,128]{3,2,1,0:T(8,128)} %copy-done.15) | copy-start | bytes 393220
  210.3 7.7 %collective-permute-start.12 = (f32[2,128,128]{2,1,0:T(8,128)S(1)}, f32[2,128,128]{2,1,0:T(8,128)S(1)}, u32[]{:S(2)}, u32[]{:S(2)}) collective-permute-start(f32[2,128,128]{2,1,0:T(8,128)S(1)} %add_select_fusion.2), channel_id=1, source_target_pairs={{128,0},{136,8},{144,16},{152,24},{160,32},{168,40},{176,48},{184,... | collective-permute-start | bytes 393224 | tf_op jit(solution)/shard_map/ppermute | solution.py:20
  212.2 273.0 %copy-start.17 = (f32[1,2,128,128]{3,2,1,0:T(8,128)}, f32[1,2,128,128]{3,2,1,0:T(8,128)S(1)}, u32[]{:S(2)}) copy-start(f32[1,2,128,128]{3,2,1,0:T(8,128)S(1)} %fusion.46) | copy-start | bytes 393220
  218.6 265.9 %collective-permute-start.13 = (f32[2,128,128]{2,1,0:T(8,128)S(1)}, f32[2,128,128]{2,1,0:T(8,128)S(1)}, u32[]{:S(2)}, u32[]{:S(2)}) collective-permute-start(f32[2,128,128]{2,1,0:T(8,128)S(1)} %add_select_fusion.1), channel_id=1, source_target_pairs={{256,0},{264,8},{272,16},{280,24},{288,32},{296,40},{304,48},{312,... | collective-permute-start | bytes 393224 | tf_op jit(solution)/shard_map/ppermute | solution.py:20
  (12 other events, 108.6 us)
Sparse Core Ops, SparseCore 0:
  197.5 283.9 all-reduce.1

commit v4 on v1

--- a/solution.py
+++ b/solution.py
@@ -37,6 +37,42 @@
     return state
 
 
+def exchanged(x, bit):
+    count = lax.axis_size("seq")
+    return lax.ppermute(x, "seq", [(i, i ^ bit) for i in range(count)])
+
+
+def gathered_columns(piece):
+    count = lax.axis_size("seq")
+    place = lax.axis_index("seq")
+    bit = 1
+    while bit < count:
+        other = exchanged(piece, bit)
+        upper = (place & bit) > 0
+        piece = jnp.where(
+            upper, jnp.concatenate([other, piece], -1), jnp.concatenate([piece, other], -1)
+        )
+        bit *= 2
+    return piece
+
+
+def summed_columns(part, extra):
+    count = lax.axis_size("seq")
+    place = lax.axis_index("seq")
+    bit = count // 2
+    while bit >= 1:
+        half = part.shape[-1] // 2
+        low, high = part[..., :half], part[..., half:]
+        upper = (place & bit) > 0
+        kept = jnp.where(upper, high, low)
+        sent = jnp.where(upper, low, high)
+        got = exchanged(jnp.concatenate([sent, extra[..., None]], -1), bit)
+        part = kept + got[..., :half]
+        extra = extra + got[..., half]
+        bit //= 2
+    return part, extra
+
+
 def project(rows, weight):
     return jnp.einsum("bthd,hde->bthe", rows, weight, preferred_element_type=jnp.float32).astype(
         jnp.bfloat16
@@ -45,7 +81,7 @@
 
 def local(queries, keys, values, feature_weight, norm_gain, doc_bounds, out_grad):
     head_groups = lax.all_to_all(feature_weight, "fsdp", split_axis=0, concat_axis=1, tiled=True)
-    weight_local = lax.all_gather(head_groups, "seq", axis=2, tiled=True)
+    weight_local = gathered_columns(head_groups)
     head_count = weight_local.shape[0]
     tokens_here = queries.shape[0]
     block_count = tokens_here // BLK
@@ -104,7 +140,6 @@
     )
     grad_half = grad_mix.astype(jnp.bfloat16)
     gain_part = jnp.sum(grad_y * mixed_f * inverse, axis=(0, 1))
-    gain_sum = lax.psum(gain_part, "seq")
 
     state_grads = jnp.einsum(
         "bthe,bthf->bhef", qfeat, grad_half, preferred_element_type=jnp.float32
@@ -133,7 +168,7 @@
     weight_part = weight_part + jnp.einsum(
         "bhdf,bhef->hde", raw_states, state_grads, precision=HIGH
     )
-    weight_columns = lax.psum_scatter(weight_part, "seq", scatter_dimension=2, tiled=True)
+    weight_columns, gain_sum = summed_columns(weight_part, gain_part)
     owned_grad = lax.all_to_all(weight_columns, "fsdp", split_axis=1, concat_axis=0, tiled=True)
 
     running = zero_state

time: 353 us -> 202 us (0.57)
  the two profiles are of different devices: /device:TPU:1 before, /device:TPU:30 now
where the time goes in v4:
time: 202 us; the launch traced here: 201 us
  starting transfers between devices  97.4 us (48%)
  waiting for transfers between devices  66.7 us (33%)
  other arithmetic  20.1 us (10%)
  local copies, waits for them, and re-layouts  9.12 us (5%)
  matrix products  6.29 us (3%)
    ppermute x14, starting transfers between devices, shifted(): return lax.ppermute(x, 'seq', pairs)  47.5 us
    ppermute x14, waiting for transfers between devices, shifted(): return lax.ppermute(x, 'seq', pairs)  42.2 us
    ppermute x12, starting transfers between devices, exchanged(): return lax.ppermute(x, 'seq', [(i, i ^ bit) for i in range(count)])  36.2 us
    ppermute x12, waiting for transfers between devices, exchanged(): return lax.ppermute(x, 'seq', [(i, i ^ bit) for i in range(count)])  19.6 us
    all_to_all x1, starting transfers between devices, local(): lax.all_to_all(feature_weight, 'fsdp', split_axis=0, concat_axis=1, tiled...  10.3 us
    select_n x10, other arithmetic, carried_in(): state = jnp.where(opens(lo, hi), state, far + state)  6.5 us
    all_to_all x1, waiting for transfers between devices, local(): lax.all_to_all(feature_weight, 'fsdp', split_axis=0, concat_axis=1, tiled...  4.84 us
  transfers between devices with their start and end apart: 28, of which 17 were waited for; matrix products, arithmetic and copies ran while one was open for 11% of the time, Pallas kernels for 0%

profile of v4, /device:TPU:30, one launch (start us, length us, event | category | flops | bytes accessed | tf_op | source)
XLA Modules:
  0.0 201.1 jit_solution(11539877025684564286)
XLA Ops:
  0.6 10.3 %all-to-all-start = ((bf16[16,16,2]{1,2,0:T(2,128)(2,1)}), bf16[16,16,2]{1,2,0:T(2,128)(2,1)S(1)}, u32[]{:S(2)}, u32[]{:S(2)}) async-start(bf16[16,16,2]{1,2,0:T(2,128)(2,1)} %param.10), calls=%async_computation | async-start | bytes 16384 | tf_op jit(solution)/shard_map/all_to_all | solution.py:83
  13.8 4.8 %all-to-all-done = bf16[16,16,2]{1,2,0:T(2,128)(2,1)S(1)} async-done(((bf16[16,16,2]{1,2,0:T(2,128)(2,1)}), bf16[16,16,2]{1,2,0:T(2,128)(2,1)S(1)}, u32[]{:S(2)}, u32[]{:S(2)}) %all-to-all-start) | async-done | bytes 1056 | tf_op jit(solution)/shard_map/all_to_all | solution.py:83
  22.7 4.6 %collective-permute-start.1 = (f32[2,128,128]{2,1,0:T(8,128)S(1)}, f32[2,128,128]{2,1,0:T(8,128)S(1)}, u32[]{:S(2)}, u32[]{:S(2)}) collective-permute-start(f32[2,128,128]{2,1,0:T(8,128)S(1)} %get-tuple-element.23), channel_id=1, source_target_pairs={{0,16},{8,24},{16,32},{24,40},{32,48},{40,56},{48,64},{56,72},{64,... | collective-permute-start | bytes 393224 | tf_op jit(solution)/shard_map/ppermute | solution.py:20
  32.2 2.8 %collective-permute-done.8 = bf16[2,128,4]{1,2,0:T(4,128)(2,1)S(1)} collective-permute-done((bf16[2,128,4]{1,2,0:T(4,128)(2,1)S(1)}, bf16[2,128,4]{1,2,0:T(4,128)(2,1)S(1)}, u32[]{:S(2)}, u32[]{:S(2)}) %collective-permute-start.8) | collective-permute-done | bytes 2080 | tf_op jit(solution)/shard_map/ppermute | solution.py:42
  37.7 4.2 %collective-permute-done.9 = bf16[2,128,8]{1,2,0:T(8,128)(2,1)S(1)} collective-permute-done((bf16[2,128,8]{1,2,0:T(8,128)(2,1)S(1)}, bf16[2,128,8]{1,2,0:T(8,128)(2,1)S(1)}, u32[]{:S(2)}, u32[]{:S(2)}) %collective-permute-start.9) | collective-permute-done | bytes 4128 | tf_op jit(solution)/shard_map/ppermute | solution.py:42
  44.8 2.7 %collective-permute-done.10 = bf16[2,128,16]{1,2,0:T(8,128)(2,1)S(1)} collective-permute-done((bf16[2,128,16]{1,2,0:T(8,128)(2,1)S(1)}, bf16[2,128,16]{1,2,0:T(8,128)(2,1)S(1)}, u32[]{:S(2)}, u32[]{:S(2)}) %collective-permute-start.10) | collective-permute-done | bytes 8224 | tf_op jit(solution)/shard_map/ppermute | solution.py:42
  50.1 4.2 %collective-permute-start.2 = (f32[2,128,128]{2,1,0:T(8,128)S(1)}, f32[2,128,128]{2,1,0:T(8,128)S(1)}, u32[]{:S(2)}, u32[]{:S(2)}) collective-permute-start(f32[2,128,128]{2,1,0:T(8,128)S(1)} %add_select_fusion.11), channel_id=1, source_target_pairs={{0,16},{8,24},{16,32},{24,40},{32,48},{40,56},{48,64},{56,72},{64,... | collective-permute-start | bytes 393224 | tf_op jit(solution)/shard_map/ppermute | solution.py:20
  59.3 5.9 %collective-permute-start.3 = (f32[2,128,128]{2,1,0:T(8,128)S(1)}, f32[2,128,128]{2,1,0:T(8,128)S(1)}, u32[]{:S(2)}, u32[]{:S(2)}) collective-permute-start(f32[2,128,128]{2,1,0:T(8,128)S(1)} %add_select_fusion.10), channel_id=1, source_target_pairs={{0,32},{8,40},{16,48},{24,56},{32,64},{40,72},{48,80},{56,88},{64,... | collective-permute-start | bytes 393224 | tf_op jit(solution)/shard_map/ppermute | solution.py:20
  69.0 4.6 %collective-permute-start.4 = (f32[2,128,128]{2,1,0:T(8,128)S(1)}, f32[2,128,128]{2,1,0:T(8,128)S(1)}, u32[]{:S(2)}, u32[]{:S(2)}) collective-permute-start(f32[2,128,128]{2,1,0:T(8,128)S(1)} %add_select_fusion.9), channel_id=1, source_target_pairs={{0,64},{8,72},{16,80},{24,88},{32,96},{40,104},{48,112},{56,120},{... | collective-permute-start | bytes 393224 | tf_op jit(solution)/shard_map/ppermute | solution.py:20
  73.8 2.9 %collective-permute-done.4 = f32[2,128,128]{2,1,0:T(8,128)S(1)} collective-permute-done((f32[2,128,128]{2,1,0:T(8,128)S(1)}, f32[2,128,128]{2,1,0:T(8,128)S(1)}, u32[]{:S(2)}, u32[]{:S(2)}) %collective-permute-start.4) | collective-permute-done | bytes 131104 | tf_op jit(solution)/shard_map/ppermute | solution.py:20
  77.3 4.4 %collective-permute-start.5 = (f32[2,128,128]{2,1,0:T(8,128)S(1)}, f32[2,128,128]{2,1,0:T(8,128)S(1)}, u32[]{:S(2)}, u32[]{:S(2)}) collective-permute-start(f32[2,128,128]{2,1,0:T(8,128)S(1)} %add_select_fusion.8), channel_id=1, source_target_pairs={{0,128},{8,136},{16,144},{24,152},{32,160},{40,168},{48,176},{56,1... | collective-permute-start | bytes 393224 | tf_op jit(solution)/shard_map/ppermute | solution.py:20
  82.0 3.0 %collective-permute-done.5 = f32[2,128,128]{2,1,0:T(8,128)S(1)} collective-permute-done((f32[2,128,128]{2,1,0:T(8,128)S(1)}, f32[2,128,128]{2,1,0:T(8,128)S(1)}, u32[]{:S(2)}, u32[]{:S(2)}) %collective-permute-start.5) | collective-permute-done | bytes 131104 | tf_op jit(solution)/shard_map/ppermute | solution.py:20
  85.7 6.7 %collective-permute-start.6 = (f32[2,128,128]{2,1,0:T(8,128)S(1)}, f32[2,128,128]{2,1,0:T(8,128)S(1)}, u32[]{:S(2)}, u32[]{:S(2)}) collective-permute-start(f32[2,128,128]{2,1,0:T(8,128)S(1)} %add_select_fusion.7), channel_id=1, source_target_pairs={{0,256},{8,264},{16,272},{24,280},{32,288},{40,296},{48,304},{56,3... | collective-permute-start | bytes 393224 | tf_op jit(solution)/shard_map/ppermute | solution.py:20
  99.6 8.4 %collective-permute-start.20 = (f32[2,128,65]{1,2,0:T(8,128)S(1)}, f32[2,128,65]{1,2,0:T(8,128)S(1)}, u32[]{:S(2)}, u32[]{:S(2)}) collective-permute-start(f32[2,128,65]{1,2,0:T(8,128)S(1)} %pad_maximum_fusion), channel_id=1, source_target_pairs={{0,256},{8,264},{16,272},{24,280},{32,288},{40,296},{48,304},{56,3... | collective-permute-start | bytes 199688 | tf_op jit(solution)/shard_map/ppermute | solution.py:42
  110.6 2.8 %collective-permute-start.14 = (f32[2,128,128]{2,1,0:T(8,128)S(1)}, f32[2,128,128]{2,1,0:T(8,128)}, u32[]{:S(2)}, u32[]{:S(2)}) collective-permute-start(f32[2,128,128]{2,1,0:T(8,128)S(1)} %get-tuple-element.20), channel_id=1, source_target_pairs={{16,0},{24,8},{32,16},{40,24},{48,32},{56,40},{64,48},{72,56},{80,... | collective-permute-start | bytes 393224 | tf_op jit(solution)/shard_map/ppermute | solution.py:20
  116.1 7.4 %collective-permute-start.21 = (f32[2,128,33]{1,0,2:T(2,128)}, f32[2,128,33]{1,0,2:T(2,128)}, u32[]{:S(2)}, u32[]{:S(2)}) collective-permute-start(f32[2,128,33]{1,0,2:T(2,128)} %pad_maximum_fusion.1), channel_id=1, source_target_pairs={{0,128},{8,136},{16,144},{24,152},{32,160},{40,168},{48,176},{56,1... | collective-permute-start | bytes 101384 | tf_op jit(solution)/shard_map/ppermute | solution.py:42
  130.2 2.9 %collective-permute-done.22 = f32[2,128,17]{1,0,2:T(2,128)S(1)} collective-permute-done((f32[2,128,17]{1,0,2:T(2,128)S(1)}, f32[2,128,17]{1,0,2:T(2,128)S(1)}, u32[]{:S(2)}, u32[]{:S(2)}) %collective-permute-start.22) | collective-permute-done | bytes 17440 | tf_op jit(solution)/shard_map/ppermute | solution.py:42
  135.8 4.4 %collective-permute-done.23 = f32[2,128,9]{1,0,2:T(2,128)S(1)} collective-permute-done((f32[2,128,9]{1,0,2:T(2,128)S(1)}, f32[2,128,9]{1,0,2:T(2,128)S(1)}, u32[]{:S(2)}, u32[]{:S(2)}) %collective-permute-start.23) | collective-permute-done | bytes 9248 | tf_op jit(solution)/shard_map/ppermute | solution.py:42
  144.5 3.2 %collective-permute-start.15 = (f32[2,128,128]{2,1,0:T(8,128)S(1)}, f32[2,128,128]{2,1,0:T(8,128)S(1)}, u32[]{:S(2)}, u32[]{:S(2)}) collective-permute-start(f32[2,128,128]{2,1,0:T(8,128)S(1)} %add_select_fusion.5), channel_id=1, source_target_pairs={{16,0},{24,8},{32,16},{40,24},{48,32},{56,40},{64,48},{72,56},{80,... | collective-permute-start | bytes 393224 | tf_op jit(solution)/shard_map/ppermute | solution.py:20
  147.8 6.9 %collective-permute-done.15 = f32[2,128,128]{2,1,0:T(8,128)S(1)} collective-permute-done((f32[2,128,128]{2,1,0:T(8,128)S(1)}, f32[2,128,128]{2,1,0:T(8,128)S(1)}, u32[]{:S(2)}, u32[]{:S(2)}) %collective-permute-start.15) | collective-permute-done | bytes 131104 | tf_op jit(solution)/shard_map/ppermute | solution.py:20
  159.3 6.6 %collective-permute-done.16 = f32[2,128,128]{2,1,0:T(8,128)S(1)} collective-permute-done((f32[2,128,128]{2,1,0:T(8,128)S(1)}, f32[2,128,128]{2,1,0:T(8,128)S(1)}, u32[]{:S(2)}, u32[]{:S(2)}) %collective-permute-start.16) | collective-permute-done | bytes 131104 | tf_op jit(solution)/shard_map/ppermute | solution.py:20
  169.2 3.4 %all-to-all-start.1 = ((f32[2,128,2]{0,2,1:T(2,128)}), f32[2,128,2]{0,2,1:T(2,128)S(1)}, u32[]{:S(2)}, u32[]{:S(2)}) async-start(f32[2,128,2]{0,2,1:T(2,128)} %copy.183), calls=%async_computation.1 | async-start | bytes 262144 | tf_op jit(solution)/shard_map/all_to_all | solution.py:172
  178.8 7.6 %collective-permute-done.18 = f32[2,128,128]{2,1,0:T(8,128)S(1)} collective-permute-done((f32[2,128,128]{2,1,0:T(8,128)S(1)}, f32[2,128,128]{2,1,0:T(8,128)S(1)}, u32[]{:S(2)}, u32[]{:S(2)}) %collective-permute-start.18) | collective-permute-done | bytes 131104 | tf_op jit(solution)/shard_map/ppermute | solution.py:20
  189.3 8.6 %collective-permute-done.19 = f32[2,128,128]{2,1,0:T(8,128)S(1)} collective-permute-done((f32[2,128,128]{2,1,0:T(8,128)S(1)}, f32[2,128,128]{2,1,0:T(8,128)S(1)}, u32[]{:S(2)}, u32[]{:S(2)}) %collective-permute-start.19) | collective-permute-done | bytes 131104 | tf_op jit(solution)/shard_map/ppermute | solution.py:20
  (140 shorter events, 76.2 us)
Async XLA Ops:
  0.6 18.1 %all-to-all-start = ((bf16[16,16,2]{1,2,0:T(2,128)(2,1)}), bf16[16,16,2]{1,2,0:T(2,128)(2,1)S(1)}, u32[]{:S(2)}, u32[]{:S(2)}) async-start(bf16[16,16,2]{1,2,0:T(2,128)(2,1)} %param.10), calls=%async_computation | async-start | bytes 16384 | tf_op jit(solution)/shard_map/all_to_all | solution.py:83
  18.8 10.7 %collective-permute-start.7 = (bf16[2,128,2]{1,2,0:T(2,128)(2,1)S(1)}, bf16[2,128,2]{1,2,0:T(2,128)(2,1)S(1)}, u32[]{:S(2)}, u32[]{:S(2)}) collective-permute-start(bf16[2,128,2]{1,2,0:T(2,128)(2,1)S(1)} %all_to_all.23), channel_id=1, source_target_pairs={{0,8},{8,0},{16,24},{24,16},{32,40},{40,32},{48,56},{56,48},{64,72... | collective-permute-start | bytes 3080 | tf_op jit(solution)/shard_map/ppermute | solution.py:42
  22.7 26.8 %collective-permute-start.1 = (f32[2,128,128]{2,1,0:T(8,128)S(1)}, f32[2,128,128]{2,1,0:T(8,128)S(1)}, u32[]{:S(2)}, u32[]{:S(2)}) collective-permute-start(f32[2,128,128]{2,1,0:T(8,128)S(1)} %get-tuple-element.23), channel_id=1, source_target_pairs={{0,16},{8,24},{16,32},{24,40},{32,48},{40,56},{48,64},{56,72},{64,... | collective-permute-start | bytes 393224 | tf_op jit(solution)/shard_map/ppermute | solution.py:20
  27.3 22.1 %collective-permute-start = (f32[2,128,128]{2,1,0:T(8,128)S(1)}, f32[2,128,128]{2,1,0:T(8,128)S(1)}, u32[]{:S(2)}, u32[]{:S(2)}) collective-permute-start(f32[2,128,128]{2,1,0:T(8,128)S(1)} %get-tuple-element.23), channel_id=1, source_target_pairs={{0,8},{8,16},{16,24},{24,32},{32,40},{40,48},{48,56},{56,64},{64,7... | collective-permute-start | bytes 393224 | tf_op jit(solution)/shard_map/ppermute | solution.py:20
  47.5 8.9 %collective-permute-start.11 = (bf16[2,128,32]{1,2,0:T(8,128)(2,1)S(1)}, bf16[2,128,32]{1,2,0:T(8,128)(2,1)S(1)}, u32[]{:S(2)}, u32[]{:S(2)}) collective-permute-start(bf16[2,128,32]{1,2,0:T(8,128)(2,1)S(1)} %maximum_select_fusion.2), channel_id=1, source_target_pairs={{0,128},{8,136},{16,144},{24,152},{32,160},{40,168},{48,176},{56,1... | collective-permute-start | bytes 49160 | tf_op jit(solution)/shard_map/ppermute | solution.py:42
  50.1 8.5 %collective-permute-start.2 = (f32[2,128,128]{2,1,0:T(8,128)S(1)}, f32[2,128,128]{2,1,0:T(8,128)S(1)}, u32[]{:S(2)}, u32[]{:S(2)}) collective-permute-start(f32[2,128,128]{2,1,0:T(8,128)S(1)} %add_select_fusion.11), channel_id=1, source_target_pairs={{0,16},{8,24},{16,32},{24,40},{32,48},{40,56},{48,64},{56,72},{64,... | collective-permute-start | bytes 393224 | tf_op jit(solution)/shard_map/ppermute | solution.py:20
  56.5 9.7 %collective-permute-start.12 = (bf16[2,128,64]{1,2,0:T(8,128)(2,1)S(1)}, bf16[2,128,64]{1,2,0:T(8,128)(2,1)S(1)}, u32[]{:S(2)}, u32[]{:S(2)}) collective-permute-start(bf16[2,128,64]{1,2,0:T(8,128)(2,1)S(1)} %maximum_select_fusion.1), channel_id=1, source_target_pairs={{0,256},{8,264},{16,272},{24,280},{32,288},{40,296},{48,304},{56,3... | collective-permute-start | bytes 98312 | tf_op jit(solution)/shard_map/ppermute | solution.py:42
  59.3 9.0 %collective-permute-start.3 = (f32[2,128,128]{2,1,0:T(8,128)S(1)}, f32[2,128,128]{2,1,0:T(8,128)S(1)}, u32[]{:S(2)}, u32[]{:S(2)}) collective-permute-start(f32[2,128,128]{2,1,0:T(8,128)S(1)} %add_select_fusion.10), channel_id=1, source_target_pairs={{0,32},{8,40},{16,48},{24,56},{32,64},{40,72},{48,80},{56,88},{64,... | collective-permute-start | bytes 393224 | tf_op jit(solution)/shard_map/ppermute | solution.py:20
  69.0 7.7 %collective-permute-start.4 = (f32[2,128,128]{2,1,0:T(8,128)S(1)}, f32[2,128,128]{2,1,0:T(8,128)S(1)}, u32[]{:S(2)}, u32[]{:S(2)}) collective-permute-start(f32[2,128,128]{2,1,0:T(8,128)S(1)} %add_select_fusion.9), channel_id=1, source_target_pairs={{0,64},{8,72},{16,80},{24,88},{32,96},{40,104},{48,112},{56,120},{... | collective-permute-start | bytes 393224 | tf_op jit(solution)/shard_map/ppermute | solution.py:20
  77.3 7.8 %collective-permute-start.5 = (f32[2,128,128]{2,1,0:T(8,128)S(1)}, f32[2,128,128]{2,1,0:T(8,128)S(1)}, u32[]{:S(2)}, u32[]{:S(2)}) collective-permute-start(f32[2,128,128]{2,1,0:T(8,128)S(1)} %add_select_fusion.8), channel_id=1, source_target_pairs={{0,128},{8,136},{16,144},{24,152},{32,160},{40,168},{48,176},{56,1... | collective-permute-start | bytes 393224 | tf_op jit(solution)/shard_map/ppermute | solution.py:20
  85.7 9.2 %collective-permute-start.6 = (f32[2,128,128]{2,1,0:T(8,128)S(1)}, f32[2,128,128]{2,1,0:T(8,128)S(1)}, u32[]{:S(2)}, u32[]{:S(2)}) collective-permute-start(f32[2,128,128]{2,1,0:T(8,128)S(1)} %add_select_fusion.7), channel_id=1, source_target_pairs={{0,256},{8,264},{16,272},{24,280},{32,288},{40,296},{48,304},{56,3... | collective-permute-start | bytes 393224 | tf_op jit(solution)/shard_map/ppermute | solution.py:20
  99.6 15.7 %collective-permute-start.20 = (f32[2,128,65]{1,2,0:T(8,128)S(1)}, f32[2,128,65]{1,2,0:T(8,128)S(1)}, u32[]{:S(2)}, u32[]{:S(2)}) collective-permute-start(f32[2,128,65]{1,2,0:T(8,128)S(1)} %pad_maximum_fusion), channel_id=1, source_target_pairs={{0,256},{8,264},{16,272},{24,280},{32,288},{40,296},{48,304},{56,3... | collective-permute-start | bytes 199688 | tf_op jit(solution)/shard_map/ppermute | solution.py:42
  110.6 32.3 %collective-permute-start.14 = (f32[2,128,128]{2,1,0:T(8,128)S(1)}, f32[2,128,128]{2,1,0:T(8,128)}, u32[]{:S(2)}, u32[]{:S(2)}) collective-permute-start(f32[2,128,128]{2,1,0:T(8,128)S(1)} %get-tuple-element.20), channel_id=1, source_target_pairs={{16,0},{24,8},{32,16},{40,24},{48,32},{56,40},{64,48},{72,56},{80,... | collective-permute-start | bytes 393224 | tf_op jit(solution)/shard_map/ppermute | solution.py:20
  113.4 29.6 %collective-permute-start.13 = (f32[2,128,128]{2,1,0:T(8,128)S(1)}, f32[2,128,128]{2,1,0:T(8,128)}, u32[]{:S(2)}, u32[]{:S(2)}) collective-permute-start(f32[2,128,128]{2,1,0:T(8,128)S(1)} %get-tuple-element.20), channel_id=1, source_target_pairs={{8,0},{16,8},{24,16},{32,24},{40,32},{48,40},{56,48},{64,56},{72,6... | collective-permute-start | bytes 393224 | tf_op jit(solution)/shard_map/ppermute | solution.py:20
  116.1 9.8 %collective-permute-start.21 = (f32[2,128,33]{1,0,2:T(2,128)}, f32[2,128,33]{1,0,2:T(2,128)}, u32[]{:S(2)}, u32[]{:S(2)}) collective-permute-start(f32[2,128,33]{1,0,2:T(2,128)} %pad_maximum_fusion.1), channel_id=1, source_target_pairs={{0,128},{8,136},{16,144},{24,152},{32,160},{40,168},{48,176},{56,1... | collective-permute-start | bytes 101384 | tf_op jit(solution)/shard_map/ppermute | solution.py:42
  133.1 7.1 %collective-permute-start.23 = (f32[2,128,9]{1,0,2:T(2,128)S(1)}, f32[2,128,9]{1,0,2:T(2,128)S(1)}, u32[]{:S(2)}, u32[]{:S(2)}) collective-permute-start(f32[2,128,9]{1,0,2:T(2,128)S(1)} %pad_maximum_fusion.3), channel_id=1, source_target_pairs={{0,32},{8,40},{16,48},{24,56},{32,0},{40,8},{48,16},{56,24},{64,96... | collective-permute-start | bytes 27656 | tf_op jit(solution)/shard_map/ppermute | solution.py:42
  140.3 7.5 %collective-permute-start.24 = (f32[2,128,5]{1,0,2:T(2,128)S(1)}, f32[2,128,5]{1,0,2:T(2,128)S(1)}, u32[]{:S(2)}, u32[]{:S(2)}) collective-permute-start(f32[2,128,5]{1,0,2:T(2,128)S(1)} %pad_maximum_fusion.4), channel_id=1, source_target_pairs={{0,16},{8,24},{16,0},{24,8},{32,48},{40,56},{48,32},{56,40},{64,80... | collective-permute-start | bytes 15368 | tf_op jit(solution)/shard_map/ppermute | solution.py:42
  144.5 10.2 %collective-permute-start.15 = (f32[2,128,128]{2,1,0:T(8,128)S(1)}, f32[2,128,128]{2,1,0:T(8,128)S(1)}, u32[]{:S(2)}, u32[]{:S(2)}) collective-permute-start(f32[2,128,128]{2,1,0:T(8,128)S(1)} %add_select_fusion.5), channel_id=1, source_target_pairs={{16,0},{24,8},{32,16},{40,24},{48,32},{56,40},{64,48},{72,56},{80,... | collective-permute-start | bytes 393224 | tf_op jit(solution)/shard_map/ppermute | solution.py:20
  155.4 10.5 %collective-permute-start.16 = (f32[2,128,128]{2,1,0:T(8,128)S(1)}, f32[2,128,128]{2,1,0:T(8,128)S(1)}, u32[]{:S(2)}, u32[]{:S(2)}) collective-permute-start(f32[2,128,128]{2,1,0:T(8,128)S(1)} %add_select_fusion.4), channel_id=1, source_target_pairs={{32,0},{40,8},{48,16},{56,24},{64,32},{72,40},{80,48},{88,56},{96,... | collective-permute-start | bytes 393224 | tf_op jit(solution)/shard_map/ppermute | solution.py:20
  157.3 11.0 %collective-permute-start.25 = (f32[2,128,3]{1,0,2:T(2,128)S(1)}, f32[2,128,3]{1,0,2:T(2,128)S(1)}, u32[]{:S(2)}, u32[]{:S(2)}) collective-permute-start(f32[2,128,3]{1,0,2:T(2,128)S(1)} %pad_maximum_fusion.5), channel_id=1, source_target_pairs={{0,8},{8,0},{16,24},{24,16},{32,40},{40,32},{48,56},{56,48},{64,72... | collective-permute-start | bytes 9224 | tf_op jit(solution)/shard_map/ppermute | solution.py:42
  166.4 8.6 %collective-permute-start.17 = (f32[2,128,128]{2,1,0:T(8,128)S(1)}, f32[2,128,128]{2,1,0:T(8,128)S(1)}, u32[]{:S(2)}, u32[]{:S(2)}) collective-permute-start(f32[2,128,128]{2,1,0:T(8,128)S(1)} %add_select_fusion.3), channel_id=1, source_target_pairs={{64,0},{72,8},{80,16},{88,24},{96,32},{104,40},{112,48},{120,56},{... | collective-permute-start | bytes 393224 | tf_op jit(solution)/shard_map/ppermute | solution.py:20
  169.2 19.3 %all-to-all-start.1 = ((f32[2,128,2]{0,2,1:T(2,128)}), f32[2,128,2]{0,2,1:T(2,128)S(1)}, u32[]{:S(2)}, u32[]{:S(2)}) async-start(f32[2,128,2]{0,2,1:T(2,128)} %copy.183), calls=%async_computation.1 | async-start | bytes 262144 | tf_op jit(solution)/shard_map/all_to_all | solution.py:172
  175.7 10.8 %collective-permute-start.18 = (f32[2,128,128]{2,1,0:T(8,128)S(1)}, f32[2,128,128]{2,1,0:T(8,128)S(1)}, u32[]{:S(2)}, u32[]{:S(2)}) collective-permute-start(f32[2,128,128]{2,1,0:T(8,128)S(1)} %add_select_fusion.2), channel_id=1, source_target_pairs={{128,0},{136,8},{144,16},{152,24},{160,32},{168,40},{176,48},{184,... | collective-permute-start | bytes 393224 | tf_op jit(solution)/shard_map/ppermute | solution.py:20
  187.2 10.8 %collective-permute-start.19 = (f32[2,128,128]{2,1,0:T(8,128)S(1)}, f32[2,128,128]{2,1,0:T(8,128)S(1)}, u32[]{:S(2)}, u32[]{:S(2)}) collective-permute-start(f32[2,128,128]{2,1,0:T(8,128)S(1)} %add_select_fusion.1), channel_id=1, source_target_pairs={{256,0},{264,8},{272,16},{280,24},{288,32},{296,40},{304,48},{312,... | collective-permute-start | bytes 393224 | tf_op jit(solution)/shard_map/ppermute | solution.py:20
  (9 other events, 49.8 us)

commit v5 on v1

--- a/solution.py
+++ b/solution.py
@@ -11,8 +11,13 @@
 HIGH = lax.Precision.HIGHEST
 
 
+RADIX = 4
+
+
 def shifted(x, dist, backward):
     count = lax.axis_size("seq")
+    if dist >= count:
+        return jnp.zeros_like(x)
     if backward:
         pairs = [(i, i - dist) for i in range(dist, count)]
     else:
@@ -24,17 +29,64 @@
     count = lax.axis_size("seq")
     place = lax.axis_index("seq")
     sign = 1 if backward else -1
-    near = shifted(aggregate, 1, backward)
-    far = shifted(aggregate, 2, backward)
-    one = place + sign
-    state = jnp.where(opens(one, one), near, far + near)
-    covered = 2
+
+    def span(dist, width):
+        first = place + sign * dist
+        last = place + sign * (dist + width - 1)
+        return (last, first) if sign < 0 else (first, last)
+
+    pieces = [shifted(aggregate, m, backward) for m in range(1, RADIX + 1)]
+    state = pieces[-1]
+    for m in range(RADIX - 1, 0, -1):
+        state = jnp.where(opens(*span(m, 1)), pieces[m - 1], state + pieces[m - 1])
+    covered = RADIX
     while covered < count:
-        far = shifted(state, covered, backward)
-        lo, hi = (place + 1, place + covered) if backward else (place - covered, place - 1)
-        state = jnp.where(opens(lo, hi), state, far + state)
-        covered *= 2
+        pieces = [shifted(state, m * covered, backward) for m in range(1, RADIX)]
+        merged = pieces[-1]
+        for m in range(RADIX - 2, 0, -1):
+            merged = jnp.where(opens(*span(m * covered + 1, covered)), pieces[m - 1], merged + pieces[m - 1])
+        state = jnp.where(opens(*span(1, covered)), state, merged + state)
+        covered *= RADIX
     return state
+
+
+def exchanged(x, mask):
+    count = lax.axis_size("seq")
+    return lax.ppermute(x, "seq", [(i, i ^ mask) for i in range(count)])
+
+
+def gathered_columns(piece):
+    count = lax.axis_size("seq")
+    place = lax.axis_index("seq")
+    base = 1
+    while base < count:
+        digit = (place // base) % RADIX
+        got = [piece] + [exchanged(piece, m * base) for m in range(1, RADIX)]
+        piece = jnp.concatenate(
+            [lax.select_n(digit ^ v, *got) for v in range(RADIX)], -1
+        )
+        base *= RADIX
+    return piece
+
+
+def summed_columns(part, extra):
+    count = lax.axis_size("seq")
+    place = lax.axis_index("seq")
+    base = count // RADIX
+    while base >= 1:
+        width = part.shape[-1] // RADIX
+        quarters = [part[..., v * width:(v + 1) * width] for v in range(RADIX)]
+        digit = (place // base) % RADIX
+        part = lax.select_n(digit, *quarters)
+        total = extra
+        for m in range(1, RADIX):
+            sent = lax.select_n(digit ^ m, *quarters)
+            got = exchanged(jnp.concatenate([sent, extra[..., None]], -1), m * base)
+            part = part + got[..., :width]
+            total = total + got[..., width]
+        extra = total
+        base //= RADIX
+    return part, extra
 
 
 def project(rows, weight):
@@ -45,7 +97,7 @@
 
 def local(queries, keys, values, feature_weight, norm_gain, doc_bounds, out_grad):
     head_groups = lax.all_to_all(feature_weight, "fsdp", split_axis=0, concat_axis=1, tiled=True)
-    weight_local = lax.all_gather(head_groups, "seq", axis=2, tiled=True)
+    weight_local = gathered_columns(head_groups)
     head_count = weight_local.shape[0]
     tokens_here = queries.shape[0]
     block_count = tokens_here // BLK
@@ -104,7 +156,6 @@
     )
     grad_half = grad_mix.astype(jnp.bfloat16)
     gain_part = jnp.sum(grad_y * mixed_f * inverse, axis=(0, 1))
-    gain_sum = lax.psum(gain_part, "seq")
 
     state_grads = jnp.einsum(
         "bthe,bthf->bhef", qfeat, grad_half, preferred_element_type=jnp.float32
@@ -133,7 +184,7 @@
     weight_part = weight_part + jnp.einsum(
         "bhdf,bhef->hde", raw_states, state_grads, precision=HIGH
     )
-    weight_columns = lax.psum_scatter(weight_part, "seq", scatter_dimension=2, tiled=True)
+    weight_columns, gain_sum = summed_columns(weight_part, gain_part)
     owned_grad = lax.all_to_all(weight_columns, "fsdp", split_axis=1, concat_axis=0, tiled=True)
 
     running = zero_state

time: 353 us -> 236 us (0.67)
  the two profiles are of different devices: /device:TPU:1 before, /device:TPU:23 now
where the time goes in v5:
time: 236 us; the launch traced here: 234 us
  starting transfers between devices  143 us (61%)
  waiting for transfers between devices  43.6 us (18%)
  other arithmetic  28.5 us (12%)
  local copies, waits for them, and re-layouts  11.4 us (5%)
  matrix products  6.32 us (3%)
    ppermute x20, starting transfers between devices, shifted(): return lax.ppermute(x, 'seq', pairs)  65.9 us
    ppermute x18, starting transfers between devices, exchanged(): return lax.ppermute(x, 'seq', [(i, i ^ mask) for i in range(count)])  63.6 us
    ppermute x20, waiting for transfers between devices, shifted(): return lax.ppermute(x, 'seq', pairs)  34.7 us
    all_to_all x1, starting transfers between devices, local(): lax.all_to_all(feature_weight, 'fsdp', split_axis=0, concat_axis=1, tiled...  10 us
    select_n x4, other arithmetic, carried_in(): state = jnp.where(opens(*span(1, covered)), state, merged + state)  7.57 us
    select_n x2, other arithmetic, carried_in(): state = jnp.where(opens(*span(m, 1)), pieces[m - 1], state + pieces[m - 1])  5.73 us
  transfers between devices with their start and end apart: 40, of which 14 were waited for; matrix products, arithmetic and copies ran while one was open for 9% of the time, Pallas kernels for 0%

profile of v5, /device:TPU:23, one launch (start us, length us, event | category | flops | bytes accessed | tf_op | source)
XLA Modules:
  0.0 234.4 jit_solution(4057065130259121568)
XLA Ops:
  5.5 4.0 %collective-permute-start.3 = (f32[2,128,128]{2,1,0:T(8,128)S(1)}, f32[2,128,128]{2,1,0:T(8,128)S(1)}, u32[]{:S(2)}, u32[]{:S(2)}) collective-permute-start(f32[2,128,128]{2,1,0:T(8,128)S(1)} %get-tuple-element.30), channel_id=1, source_target_pairs={{0,32},{8,40},{16,48},{24,56},{32,64},{40,72},{48,80},{56,88},{64,... | collective-permute-start | bytes 393224 | tf_op jit(solution)/shard_map/ppermute | solution.py:25
  9.5 4.6 %collective-permute-start.2 = (f32[2,128,128]{2,1,0:T(8,128)S(1)}, f32[2,128,128]{2,1,0:T(8,128)}, u32[]{:S(2)}, u32[]{:S(2)}) collective-permute-start(f32[2,128,128]{2,1,0:T(8,128)S(1)} %get-tuple-element.30), channel_id=1, source_target_pairs={{0,24},{8,32},{16,40},{24,48},{32,56},{40,64},{48,72},{56,80},{64,... | collective-permute-start | bytes 393224 | tf_op jit(solution)/shard_map/ppermute | solution.py:25
  14.1 10.0 %all-to-all-start = ((bf16[16,16,2]{1,2,0:T(2,128)(2,1)}), bf16[16,16,2]{1,2,0:T(2,128)(2,1)S(1)}, u32[]{:S(2)}, u32[]{:S(2)}) async-start(bf16[16,16,2]{1,2,0:T(2,128)(2,1)} %param.10), calls=%async_computation | async-start | bytes 16384 | tf_op jit(solution)/shard_map/all_to_all | solution.py:99
  26.4 4.3 %all-to-all-done = bf16[16,16,2]{1,2,0:T(2,128)(2,1)S(1)} async-done(((bf16[16,16,2]{1,2,0:T(2,128)(2,1)}), bf16[16,16,2]{1,2,0:T(2,128)(2,1)S(1)}, u32[]{:S(2)}, u32[]{:S(2)}) %all-to-all-start) | async-done | bytes 1056 | tf_op jit(solution)/shard_map/all_to_all | solution.py:99
  33.4 4.0 %collective-permute-start.12 = (bf16[2,128,2]{2,1,0:T(8,128)(2,1)S(1)}, bf16[2,128,2]{2,1,0:T(8,128)(2,1)S(1)}, u32[]{:S(2)}, u32[]{:S(2)}) collective-permute-start(bf16[2,128,2]{2,1,0:T(8,128)(2,1)S(1)} %bitcast.120), channel_id=1, source_target_pairs={{0,24},{8,16},{16,8},{24,0},{32,56},{40,48},{48,40},{56,32},{64,88... | collective-permute-start | bytes 3080 | tf_op jit(solution)/shard_map/ppermute | solution.py:55
  40.7 4.1 %collective-permute-start.15 = (bf16[2,128,8]{2,1,0:T(8,128)(2,1)S(1)}, bf16[2,128,8]{2,1,0:T(8,128)(2,1)S(1)}, u32[]{:S(2)}, u32[]{:S(2)}) collective-permute-start(bf16[2,128,8]{2,1,0:T(8,128)(2,1)S(1)} %pad_maximum_fusion.9), channel_id=1, source_target_pairs={{0,96},{8,104},{16,112},{24,120},{32,64},{40,72},{48,80},{56,88},{... | collective-permute-start | bytes 12296 | tf_op jit(solution)/shard_map/ppermute | solution.py:55
  47.1 4.6 %collective-permute-start.13 = (bf16[2,128,8]{2,1,0:T(8,128)(2,1)S(1)}, bf16[2,128,8]{2,1,0:T(8,128)(2,1)S(1)}, u32[]{:S(2)}, u32[]{:S(2)}) collective-permute-start(bf16[2,128,8]{2,1,0:T(8,128)(2,1)S(1)} %pad_maximum_fusion.9), channel_id=1, source_target_pairs={{0,32},{8,40},{16,48},{24,56},{32,0},{40,8},{48,16},{56,24},{64,96... | collective-permute-start | bytes 12296 | tf_op jit(solution)/shard_map/ppermute | solution.py:55
  53.8 3.6 %collective-permute-start.18 = (bf16[2,128,32]{2,1,0:T(8,128)(2,1)S(1)}, bf16[2,128,32]{2,1,0:T(8,128)(2,1)S(1)}, u32[]{:S(2)}, u32[]{:S(2)}) collective-permute-start(bf16[2,128,32]{2,1,0:T(8,128)(2,1)S(1)} %pad_maximum_fusion.10), channel_id=1, source_target_pairs={{0,384},{8,392},{16,400},{24,408},{32,416},{40,424},{48,432},{56,4... | collective-permute-start | bytes 49160 | tf_op jit(solution)/shard_map/ppermute | solution.py:55
  59.9 5.3 %collective-permute-start.16 = (bf16[2,128,32]{2,1,0:T(8,128)(2,1)S(1)}, bf16[2,128,32]{2,1,0:T(8,128)(2,1)S(1)}, u32[]{:S(2)}, u32[]{:S(2)}) collective-permute-start(bf16[2,128,32]{2,1,0:T(8,128)(2,1)S(1)} %pad_maximum_fusion.10), channel_id=1, source_target_pairs={{0,128},{8,136},{16,144},{24,152},{32,160},{40,168},{48,176},{56,1... | collective-permute-start | bytes 49160 | tf_op jit(solution)/shard_map/ppermute | solution.py:55
  67.3 5.0 %collective-permute-start.1 = (f32[2,128,128]{2,1,0:T(8,128)S(1)}, f32[2,128,128]{2,1,0:T(8,128)S(1)}, u32[]{:S(2)}, u32[]{:S(2)}) collective-permute-start(f32[2,128,128]{2,1,0:T(8,128)S(1)} %get-tuple-element.30), channel_id=1, source_target_pairs={{0,16},{8,24},{16,32},{24,40},{32,48},{40,56},{48,64},{56,72},{64,... | collective-permute-start | bytes 393224 | tf_op jit(solution)/shard_map/ppermute | solution.py:25
  72.3 5.8 %collective-permute-start = (f32[2,128,128]{2,1,0:T(8,128)S(1)}, f32[2,128,128]{2,1,0:T(8,128)S(1)}, u32[]{:S(2)}, u32[]{:S(2)}) collective-permute-start(f32[2,128,128]{2,1,0:T(8,128)S(1)} %get-tuple-element.30), channel_id=1, source_target_pairs={{0,8},{8,16},{16,24},{24,32},{32,40},{40,48},{48,56},{56,64},{64,7... | collective-permute-start | bytes 393224 | tf_op jit(solution)/shard_map/ppermute | solution.py:25
  87.9 4.4 %collective-permute-start.4 = (f32[2,128,128]{2,1,0:T(8,128)S(1)}, f32[2,128,128]{2,1,0:T(8,128)S(1)}, u32[]{:S(2)}, u32[]{:S(2)}) collective-permute-start(f32[2,128,128]{2,1,0:T(8,128)S(1)} %add_select_fusion.15), channel_id=1, source_target_pairs={{0,32},{8,40},{16,48},{24,56},{32,64},{40,72},{48,80},{56,88},{64,... | collective-permute-start | bytes 393224 | tf_op jit(solution)/shard_map/ppermute | solution.py:25
  103.6 5.0 %collective-permute-done.7 = f32[2,128,128]{2,1,0:T(8,128)S(1)} collective-permute-done((f32[2,128,128]{2,1,0:T(8,128)S(1)}, f32[2,128,128]{2,1,0:T(8,128)S(1)}, u32[]{:S(2)}, u32[]{:S(2)}) %collective-permute-start.7) | collective-permute-done | bytes 131104 | tf_op jit(solution)/shard_map/ppermute | solution.py:25
  117.0 4.2 %collective-permute-start.29 = (f32[2,128,33]{2,1,0:T(8,128)}, f32[2,128,33]{2,1,0:T(8,128)S(1)}, u32[]{:S(2)}, u32[]{:S(2)}) collective-permute-start(f32[2,128,33]{2,1,0:T(8,128)} %get-tuple-element.66), channel_id=1, source_target_pairs={{0,128},{8,136},{16,144},{24,152},{32,160},{40,168},{48,176},{56,1... | collective-permute-start | bytes 101384 | tf_op jit(solution)/shard_map/ppermute | solution.py:55
  121.2 6.2 %collective-permute-start.30 = (f32[2,128,33]{2,1,0:T(8,128)}, f32[2,128,33]{2,1,0:T(8,128)S(1)}, u32[]{:S(2)}, u32[]{:S(2)}) collective-permute-start(f32[2,128,33]{2,1,0:T(8,128)} %get-tuple-element.67), channel_id=1, source_target_pairs={{0,256},{8,264},{16,272},{24,280},{32,288},{40,296},{48,304},{56,3... | collective-permute-start | bytes 101384 | tf_op jit(solution)/shard_map/ppermute | solution.py:55
  132.7 8.3 %collective-permute-start.22 = (f32[2,128,128]{2,1,0:T(8,128)}, f32[2,128,128]{2,1,0:T(8,128)}, u32[]{:S(2)}, u32[]{:S(2)}) collective-permute-start(f32[2,128,128]{2,1,0:T(8,128)} %get-tuple-element.26), channel_id=1, source_target_pairs={{32,0},{40,8},{48,16},{56,24},{64,32},{72,40},{80,48},{88,56},{96,... | collective-permute-start | bytes 393224 | tf_op jit(solution)/shard_map/ppermute | solution.py:25
  141.0 6.5 %collective-permute-start.21 = (f32[2,128,128]{2,1,0:T(8,128)}, f32[2,128,128]{2,1,0:T(8,128)}, u32[]{:S(2)}, u32[]{:S(2)}) collective-permute-start(f32[2,128,128]{2,1,0:T(8,128)} %get-tuple-element.26), channel_id=1, source_target_pairs={{24,0},{32,8},{40,16},{48,24},{56,32},{64,40},{72,48},{80,56},{88,... | collective-permute-start | bytes 393224 | tf_op jit(solution)/shard_map/ppermute | solution.py:25
  156.1 5.2 %collective-permute-start.34 = (f32[2,128,9]{2,1,0:T(8,128)S(1)}, f32[2,128,9]{2,1,0:T(8,128)S(1)}, u32[]{:S(2)}, u32[]{:S(2)}) collective-permute-start(f32[2,128,9]{2,1,0:T(8,128)S(1)} %get-tuple-element.63), channel_id=1, source_target_pairs={{0,96},{8,104},{16,112},{24,120},{32,64},{40,72},{48,80},{56,88},{... | collective-permute-start | bytes 27656 | tf_op jit(solution)/shard_map/ppermute | solution.py:55
  165.5 5.2 %collective-permute-start.35 = (f32[2,128,3]{2,1,0:T(8,128)S(1)}, f32[2,128,3]{2,1,0:T(8,128)S(1)}, u32[]{:S(2)}, u32[]{:S(2)}) collective-permute-start(f32[2,128,3]{2,1,0:T(8,128)S(1)} %get-tuple-element.56), channel_id=1, source_target_pairs={{0,8},{8,0},{16,24},{24,16},{32,40},{40,32},{48,56},{56,48},{64,72... | collective-permute-start | bytes 9224 | tf_op jit(solution)/shard_map/ppermute | solution.py:55
  182.7 3.4 %all-to-all-start.1 = ((f32[2,128,2]{2,0,1:T(2,128)}), f32[2,128,2]{2,0,1:T(2,128)S(1)}, u32[]{:S(2)}, u32[]{:S(2)}) async-start(f32[2,128,2]{2,0,1:T(2,128)} %copy.805), calls=%async_computation.1 | async-start | bytes 262144 | tf_op jit(solution)/shard_map/all_to_all | solution.py:188
  195.2 4.3 %collective-permute-start.23 = (f32[2,128,128]{2,1,0:T(8,128)S(1)}, f32[2,128,128]{2,1,0:T(8,128)S(1)}, u32[]{:S(2)}, u32[]{:S(2)}) collective-permute-start(f32[2,128,128]{2,1,0:T(8,128)S(1)} %add_select_fusion.6), channel_id=1, source_target_pairs={{32,0},{40,8},{48,16},{56,24},{64,32},{72,40},{80,48},{88,56},{96,... | collective-permute-start | bytes 393224 | tf_op jit(solution)/shard_map/ppermute | solution.py:25
  200.0 5.5 %collective-permute-done.25 = f32[2,128,128]{2,1,0:T(8,128)S(1)} collective-permute-done((f32[2,128,128]{2,1,0:T(8,128)S(1)}, f32[2,128,128]{2,1,0:T(8,128)S(1)}, u32[]{:S(2)}, u32[]{:S(2)}) %collective-permute-start.25) | collective-permute-done | bytes 131104 | tf_op jit(solution)/shard_map/ppermute | solution.py:25
  214.7 9.5 %collective-permute-done.27 = f32[2,128,128]{2,1,0:T(8,128)S(1)} collective-permute-done((f32[2,128,128]{2,1,0:T(8,128)S(1)}, f32[2,128,128]{2,1,0:T(8,128)S(1)}, u32[]{:S(2)}, u32[]{:S(2)}) %collective-permute-start.27) | collective-permute-done | bytes 131104 | tf_op jit(solution)/shard_map/ppermute | solution.py:25
  224.2 5.9 %collective-permute-done.26 = f32[2,128,128]{2,1,0:T(8,128)S(1)} collective-permute-done((f32[2,128,128]{2,1,0:T(8,128)S(1)}, f32[2,128,128]{2,1,0:T(8,128)S(1)}, u32[]{:S(2)}, u32[]{:S(2)}) %collective-permute-start.26) | collective-permute-done | bytes 131104 | tf_op jit(solution)/shard_map/ppermute | solution.py:25
  (176 shorter events, 103.8 us)
Async XLA Ops:
  5.5 73.5 %collective-permute-start.3 = (f32[2,128,128]{2,1,0:T(8,128)S(1)}, f32[2,128,128]{2,1,0:T(8,128)S(1)}, u32[]{:S(2)}, u32[]{:S(2)}) collective-permute-start(f32[2,128,128]{2,1,0:T(8,128)S(1)} %get-tuple-element.30), channel_id=1, source_target_pairs={{0,32},{8,40},{16,48},{24,56},{32,64},{40,72},{48,80},{56,88},{64,... | collective-permute-start | bytes 393224 | tf_op jit(solution)/shard_map/ppermute | solution.py:25
  9.5 69.4 %collective-permute-start.2 = (f32[2,128,128]{2,1,0:T(8,128)S(1)}, f32[2,128,128]{2,1,0:T(8,128)}, u32[]{:S(2)}, u32[]{:S(2)}) collective-permute-start(f32[2,128,128]{2,1,0:T(8,128)S(1)} %get-tuple-element.30), channel_id=1, source_target_pairs={{0,24},{8,32},{16,40},{24,48},{32,56},{40,64},{48,72},{56,80},{64,... | collective-permute-start | bytes 393224 | tf_op jit(solution)/shard_map/ppermute | solution.py:25
  14.1 16.6 %all-to-all-start = ((bf16[16,16,2]{1,2,0:T(2,128)(2,1)}), bf16[16,16,2]{1,2,0:T(2,128)(2,1)S(1)}, u32[]{:S(2)}, u32[]{:S(2)}) async-start(bf16[16,16,2]{1,2,0:T(2,128)(2,1)} %param.10), calls=%async_computation | async-start | bytes 16384 | tf_op jit(solution)/shard_map/all_to_all | solution.py:99
  40.7 11.9 %collective-permute-start.15 = (bf16[2,128,8]{2,1,0:T(8,128)(2,1)S(1)}, bf16[2,128,8]{2,1,0:T(8,128)(2,1)S(1)}, u32[]{:S(2)}, u32[]{:S(2)}) collective-permute-start(bf16[2,128,8]{2,1,0:T(8,128)(2,1)S(1)} %pad_maximum_fusion.9), channel_id=1, source_target_pairs={{0,96},{8,104},{16,112},{24,120},{32,64},{40,72},{48,80},{56,88},{... | collective-permute-start | bytes 12296 | tf_op jit(solution)/shard_map/ppermute | solution.py:55
  53.8 13.6 %collective-permute-start.18 = (bf16[2,128,32]{2,1,0:T(8,128)(2,1)S(1)}, bf16[2,128,32]{2,1,0:T(8,128)(2,1)S(1)}, u32[]{:S(2)}, u32[]{:S(2)}) collective-permute-start(bf16[2,128,32]{2,1,0:T(8,128)(2,1)S(1)} %pad_maximum_fusion.10), channel_id=1, source_target_pairs={{0,384},{8,392},{16,400},{24,408},{32,416},{40,424},{48,432},{56,4... | collective-permute-start | bytes 49160 | tf_op jit(solution)/shard_map/ppermute | solution.py:55
  57.4 14.9 %collective-permute-start.17 = (bf16[2,128,32]{2,1,0:T(8,128)(2,1)S(1)}, bf16[2,128,32]{2,1,0:T(8,128)(2,1)S(1)}, u32[]{:S(2)}, u32[]{:S(2)}) collective-permute-start(bf16[2,128,32]{2,1,0:T(8,128)(2,1)S(1)} %pad_maximum_fusion.10), channel_id=1, source_target_pairs={{0,256},{8,264},{16,272},{24,280},{32,288},{40,296},{48,304},{56,3... | collective-permute-start | bytes 49160 | tf_op jit(solution)/shard_map/ppermute | solution.py:55
  59.9 18.3 %collective-permute-start.16 = (bf16[2,128,32]{2,1,0:T(8,128)(2,1)S(1)}, bf16[2,128,32]{2,1,0:T(8,128)(2,1)S(1)}, u32[]{:S(2)}, u32[]{:S(2)}) collective-permute-start(bf16[2,128,32]{2,1,0:T(8,128)(2,1)S(1)} %pad_maximum_fusion.10), channel_id=1, source_target_pairs={{0,128},{8,136},{16,144},{24,152},{32,160},{40,168},{48,176},{56,1... | collective-permute-start | bytes 49160 | tf_op jit(solution)/shard_map/ppermute | solution.py:55
  67.3 11.6 %collective-permute-start.1 = (f32[2,128,128]{2,1,0:T(8,128)S(1)}, f32[2,128,128]{2,1,0:T(8,128)S(1)}, u32[]{:S(2)}, u32[]{:S(2)}) collective-permute-start(f32[2,128,128]{2,1,0:T(8,128)S(1)} %get-tuple-element.30), channel_id=1, source_target_pairs={{0,16},{8,24},{16,32},{24,40},{32,48},{40,56},{48,64},{56,72},{64,... | collective-permute-start | bytes 393224 | tf_op jit(solution)/shard_map/ppermute | solution.py:25
  82.9 9.6 %collective-permute-start.6 = (f32[2,128,128]{2,1,0:T(8,128)S(1)}, f32[2,128,128]{2,1,0:T(8,128)S(1)}, u32[]{:S(2)}, u32[]{:S(2)}) collective-permute-start(f32[2,128,128]{2,1,0:T(8,128)S(1)} %add_select_fusion.15), channel_id=1, source_target_pairs={{0,96},{8,104},{16,112},{24,120},{32,128},{40,136},{48,144},{56,15... | collective-permute-start | bytes 393224 | tf_op jit(solution)/shard_map/ppermute | solution.py:25
  117.0 30.9 %collective-permute-start.29 = (f32[2,128,33]{2,1,0:T(8,128)}, f32[2,128,33]{2,1,0:T(8,128)S(1)}, u32[]{:S(2)}, u32[]{:S(2)}) collective-permute-start(f32[2,128,33]{2,1,0:T(8,128)} %get-tuple-element.66), channel_id=1, source_target_pairs={{0,128},{8,136},{16,144},{24,152},{32,160},{40,168},{48,176},{56,1... | collective-permute-start | bytes 101384 | tf_op jit(solution)/shard_map/ppermute | solution.py:55
  121.2 26.7 %collective-permute-start.30 = (f32[2,128,33]{2,1,0:T(8,128)}, f32[2,128,33]{2,1,0:T(8,128)S(1)}, u32[]{:S(2)}, u32[]{:S(2)}) collective-permute-start(f32[2,128,33]{2,1,0:T(8,128)} %get-tuple-element.67), channel_id=1, source_target_pairs={{0,256},{8,264},{16,272},{24,280},{32,288},{40,296},{48,304},{56,3... | collective-permute-start | bytes 101384 | tf_op jit(solution)/shard_map/ppermute | solution.py:55
  127.3 20.5 %collective-permute-start.31 = (f32[2,128,33]{2,1,0:T(8,128)}, f32[2,128,33]{2,1,0:T(8,128)}, u32[]{:S(2)}, u32[]{:S(2)}) collective-permute-start(f32[2,128,33]{2,1,0:T(8,128)} %get-tuple-element.68), channel_id=1, source_target_pairs={{0,384},{8,392},{16,400},{24,408},{32,416},{40,424},{48,432},{56,4... | collective-permute-start | bytes 101384 | tf_op jit(solution)/shard_map/ppermute | solution.py:55
  132.7 53.9 %collective-permute-start.22 = (f32[2,128,128]{2,1,0:T(8,128)}, f32[2,128,128]{2,1,0:T(8,128)}, u32[]{:S(2)}, u32[]{:S(2)}) collective-permute-start(f32[2,128,128]{2,1,0:T(8,128)} %get-tuple-element.26), channel_id=1, source_target_pairs={{32,0},{40,8},{48,16},{56,24},{64,32},{72,40},{80,48},{88,56},{96,... | collective-permute-start | bytes 393224 | tf_op jit(solution)/shard_map/ppermute | solution.py:25
  141.0 45.6 %collective-permute-start.21 = (f32[2,128,128]{2,1,0:T(8,128)}, f32[2,128,128]{2,1,0:T(8,128)}, u32[]{:S(2)}, u32[]{:S(2)}) collective-permute-start(f32[2,128,128]{2,1,0:T(8,128)} %get-tuple-element.26), channel_id=1, source_target_pairs={{24,0},{32,8},{40,16},{48,24},{56,32},{64,40},{72,48},{80,56},{88,... | collective-permute-start | bytes 393224 | tf_op jit(solution)/shard_map/ppermute | solution.py:25
  151.5 10.8 %collective-permute-start.32 = (f32[2,128,9]{2,1,0:T(8,128)S(1)}, f32[2,128,9]{2,1,0:T(8,128)S(1)}, u32[]{:S(2)}, u32[]{:S(2)}) collective-permute-start(f32[2,128,9]{2,1,0:T(8,128)S(1)} %get-tuple-element.61), channel_id=1, source_target_pairs={{0,32},{8,40},{16,48},{24,56},{32,0},{40,8},{48,16},{56,24},{64,96... | collective-permute-start | bytes 27656 | tf_op jit(solution)/shard_map/ppermute | solution.py:55
  165.5 11.3 %collective-permute-start.35 = (f32[2,128,3]{2,1,0:T(8,128)S(1)}, f32[2,128,3]{2,1,0:T(8,128)S(1)}, u32[]{:S(2)}, u32[]{:S(2)}) collective-permute-start(f32[2,128,3]{2,1,0:T(8,128)S(1)} %get-tuple-element.56), channel_id=1, source_target_pairs={{0,8},{8,0},{16,24},{24,16},{32,40},{40,32},{48,56},{56,48},{64,72... | collective-permute-start | bytes 9224 | tf_op jit(solution)/shard_map/ppermute | solution.py:55
  170.7 9.1 %collective-permute-start.36 = (f32[2,128,3]{2,1,0:T(8,128)S(1)}, f32[2,128,3]{2,1,0:T(8,128)S(1)}, u32[]{:S(2)}, u32[]{:S(2)}) collective-permute-start(f32[2,128,3]{2,1,0:T(8,128)S(1)} %get-tuple-element.57), channel_id=1, source_target_pairs={{0,16},{8,24},{16,0},{24,8},{32,48},{40,56},{48,32},{56,40},{64,80... | collective-permute-start | bytes 9224 | tf_op jit(solution)/shard_map/ppermute | solution.py:55
  176.9 9.7 %collective-permute-start.20 = (f32[2,128,128]{2,1,0:T(8,128)}, f32[2,128,128]{2,1,0:T(8,128)S(1)}, u32[]{:S(2)}, u32[]{:S(2)}) collective-permute-start(f32[2,128,128]{2,1,0:T(8,128)} %get-tuple-element.26), channel_id=1, source_target_pairs={{16,0},{24,8},{32,16},{40,24},{48,32},{56,40},{64,48},{72,56},{80,... | collective-permute-start | bytes 393224 | tf_op jit(solution)/shard_map/ppermute | solution.py:25
  182.7 31.1 %all-to-all-start.1 = ((f32[2,128,2]{2,0,1:T(2,128)}), f32[2,128,2]{2,0,1:T(2,128)S(1)}, u32[]{:S(2)}, u32[]{:S(2)}) async-start(f32[2,128,2]{2,0,1:T(2,128)} %copy.805), calls=%async_computation.1 | async-start | bytes 262144 | tf_op jit(solution)/shard_map/all_to_all | solution.py:188
  191.3 14.3 %collective-permute-start.25 = (f32[2,128,128]{2,1,0:T(8,128)S(1)}, f32[2,128,128]{2,1,0:T(8,128)S(1)}, u32[]{:S(2)}, u32[]{:S(2)}) collective-permute-start(f32[2,128,128]{2,1,0:T(8,128)S(1)} %add_select_fusion.6), channel_id=1, source_target_pairs={{96,0},{104,8},{112,16},{120,24},{128,32},{136,40},{144,48},{152,5... | collective-permute-start | bytes 393224 | tf_op jit(solution)/shard_map/ppermute | solution.py:25
  193.2 12.4 %collective-permute-start.24 = (f32[2,128,128]{2,1,0:T(8,128)S(1)}, f32[2,128,128]{2,1,0:T(8,128)S(1)}, u32[]{:S(2)}, u32[]{:S(2)}) collective-permute-start(f32[2,128,128]{2,1,0:T(8,128)S(1)} %add_select_fusion.6), channel_id=1, source_target_pairs={{64,0},{72,8},{80,16},{88,24},{96,32},{104,40},{112,48},{120,56},{... | collective-permute-start | bytes 393224 | tf_op jit(solution)/shard_map/ppermute | solution.py:25
  195.2 12.9 %collective-permute-start.23 = (f32[2,128,128]{2,1,0:T(8,128)S(1)}, f32[2,128,128]{2,1,0:T(8,128)S(1)}, u32[]{:S(2)}, u32[]{:S(2)}) collective-permute-start(f32[2,128,128]{2,1,0:T(8,128)S(1)} %add_select_fusion.6), channel_id=1, source_target_pairs={{32,0},{40,8},{48,16},{56,24},{64,32},{72,40},{80,48},{88,56},{96,... | collective-permute-start | bytes 393224 | tf_op jit(solution)/shard_map/ppermute | solution.py:25
  210.6 13.6 %collective-permute-start.27 = (f32[2,128,128]{2,1,0:T(8,128)S(1)}, f32[2,128,128]{2,1,0:T(8,128)S(1)}, u32[]{:S(2)}, u32[]{:S(2)}) collective-permute-start(f32[2,128,128]{2,1,0:T(8,128)S(1)} %add_select_fusion.3), channel_id=1, source_target_pairs={{256,0},{264,8},{272,16},{280,24},{288,32},{296,40},{304,48},{312,... | collective-permute-start | bytes 393224 | tf_op jit(solution)/shard_map/ppermute | solution.py:25
  211.9 18.2 %collective-permute-start.26 = (f32[2,128,128]{2,1,0:T(8,128)S(1)}, f32[2,128,128]{2,1,0:T(8,128)S(1)}, u32[]{:S(2)}, u32[]{:S(2)}) collective-permute-start(f32[2,128,128]{2,1,0:T(8,128)S(1)} %add_select_fusion.3), channel_id=1, source_target_pairs={{128,0},{136,8},{144,16},{152,24},{160,32},{168,40},{176,48},{184,... | collective-permute-start | bytes 393224 | tf_op jit(solution)/shard_map/ppermute | solution.py:25
  (33 other events, 467.7 us)

commit v6 on v4

--- a/solution.py
+++ b/solution.py
@@ -9,42 +9,62 @@
 
 epsilon = 1.0
 HIGH = lax.Precision.HIGHEST
+OUTER = "seq_row"
+INNER = "seq_col"
 
 
 def shifted(x, dist, backward):
-    count = lax.axis_size("seq")
+    count = lax.axis_size((OUTER, INNER))
     if backward:
         pairs = [(i, i - dist) for i in range(dist, count)]
     else:
         pairs = [(i, i + dist) for i in range(count - dist)]
-    return lax.ppermute(x, "seq", pairs)
-
-
-def carried_in(aggregate, opens, backward):
-    count = lax.axis_size("seq")
-    place = lax.axis_index("seq")
-    sign = 1 if backward else -1
-    near = shifted(aggregate, 1, backward)
-    far = shifted(aggregate, 2, backward)
-    one = place + sign
-    state = jnp.where(opens(one, one), near, far + near)
-    covered = 2
-    while covered < count:
-        far = shifted(state, covered, backward)
-        lo, hi = (place + 1, place + covered) if backward else (place - covered, place - 1)
-        state = jnp.where(opens(lo, hi), state, far + state)
-        covered *= 2
-    return state
+    return lax.ppermute(x, (OUTER, INNER), pairs)
+
+
+def masked_sum(mask, stacked):
+    return jnp.sum(jnp.where(mask[:, None, None, None], stacked, 0.0), 0)
+
+
+def carried_in(aggregate, last_open, backward):
+    inner = lax.axis_size(INNER)
+    outer = lax.axis_size(OUTER)
+    col = lax.axis_index(INNER)
+    row = lax.axis_index(OUTER)
+    place = row * inner + col
+    near = place + 1 if backward else place - 1
+    bound = last_open(near)
+    cols = jnp.arange(inner)
+    rows = jnp.arange(outer)
+    in_row = lax.all_gather(aggregate, INNER)
+    if backward:
+        mine = (cols > col) & (row * inner + cols <= bound)
+        row_bound = last_open(row * inner)
+        carry = (row * inner + cols <= row_bound)
+    else:
+        mine = (cols < col) & (row * inner + cols >= bound)
+        row_bound = last_open(row * inner + inner - 1)
+        carry = (row * inner + cols >= row_bound)
+    local_sum = masked_sum(mine, in_row)
+    row_part = masked_sum(carry, in_row)
+    across = lax.all_gather(row_part, OUTER)
+    bound_row = bound // inner
+    if backward:
+        take = (rows > row) & (rows <= bound_row)
+    else:
+        take = (rows < row) & (rows >= bound_row)
+    far_sum = masked_sum(take, across)
+    return local_sum + far_sum
 
 
 def exchanged(x, bit):
-    count = lax.axis_size("seq")
-    return lax.ppermute(x, "seq", [(i, i ^ bit) for i in range(count)])
+    count = lax.axis_size((OUTER, INNER))
+    return lax.ppermute(x, (OUTER, INNER), [(i, i ^ bit) for i in range(count)])
 
 
 def gathered_columns(piece):
-    count = lax.axis_size("seq")
-    place = lax.axis_index("seq")
+    count = lax.axis_size((OUTER, INNER))
+    place = lax.axis_index((OUTER, INNER))
     bit = 1
     while bit < count:
         other = exchanged(piece, bit)
@@ -57,8 +77,8 @@
 
 
 def summed_columns(part, extra):
-    count = lax.axis_size("seq")
-    place = lax.axis_index("seq")
+    count = lax.axis_size((OUTER, INNER))
+    place = lax.axis_index((OUTER, INNER))
     bit = count // 2
     while bit >= 1:
         half = part.shape[-1] // 2
@@ -90,12 +110,16 @@
     key_blocks = keys.reshape(block_shape)
     value_blocks = values.reshape(block_shape)
 
-    place = lax.axis_index("seq")
+    place = lax.axis_index((OUTER, INNER))
     starts = doc_bounds[:, 0]
     start_device = starts // block_count
 
-    def opens(lo, hi):
-        return jnp.any((start_device >= lo) & (start_device <= hi))
+    def last_open(device):
+        return jnp.max(jnp.where(start_device <= device, start_device, 0))
+
+    def next_open(device):
+        count = lax.axis_size((OUTER, INNER))
+        return jnp.min(jnp.where(start_device >= device, start_device, count - 1))
 
     block_ids = place * block_count + jnp.arange(block_count, dtype=jnp.int32)
     starts_here = jnp.any(starts[None, :] == block_ids[:, None], axis=1)
@@ -113,7 +137,7 @@
         held = jnp.where(starts_here[position], zero_state, running)
         prefix_list.append(held)
         running = held + raw_updates[position]
-    entering = carried_in(running, opens, False)
+    entering = carried_in(running, last_open, False)
     raw_states = jnp.stack(prefix_list) + jnp.where(
         reach_left[:, None, None, None], entering[None], 0.0
     )
@@ -176,7 +200,7 @@
     for position in reversed(range(block_count)):
         suffix_list[position] = running
         running = jnp.where(starts_here[position], zero_state, running + state_grads[position])
-    leaving = carried_in(running, opens, True)
+    leaving = carried_in(running, next_open, True)
     suffix = jnp.stack(suffix_list) + jnp.where(
         reach_right[:, None, None, None], leaving[None], 0.0
     )
@@ -198,7 +222,7 @@
     key_grad = jnp.einsum(
         "bthe,hde->bthd", kfeat_grad, weight_local, preferred_element_type=jnp.float32
     ).astype(jnp.bfloat16)
-    factor = (lax.axis_size("seq") * tokens_here) ** (-0.5)
+    factor = (lax.axis_size((OUTER, INNER)) * tokens_here) ** (-0.5)
     flat_shape = (tokens_here, head_count * HS)
     return (
         mixed.reshape(flat_shape),
@@ -220,17 +244,31 @@
         P(),
         P("seq", "fsdp"),
     )
+    seq_count, fsdp_count = mesh.devices.shape
+    inner = 8 if seq_count % 8 == 0 else seq_count
+    split = jax.sharding.Mesh(
+        mesh.devices.reshape(seq_count // inner, inner, fsdp_count), (OUTER, INNER, "fsdp")
+    )
+    seq = (OUTER, INNER)
+
+    def respec(spec):
+        return P(*[seq if part == "seq" else part for part in spec])
+
+    placed = tuple(respec(p) for p in placed)
     return jax.shard_map(
         local,
-        mesh=mesh,
+        mesh=split,
         in_specs=placed,
-        out_specs=(
-            P("seq", "fsdp"),
-            P("seq", "fsdp"),
-            P("seq", "fsdp"),
-            P("seq", "fsdp"),
-            P(None, "fsdp", "seq"),
-            P("fsdp", None),
+        out_specs=tuple(
+            respec(p)
+            for p in (
+                P("seq", "fsdp"),
+                P("seq", "fsdp"),
+                P("seq", "fsdp"),
+                P("seq", "fsdp"),
+                P(None, "fsdp", "seq"),
+                P("fsdp", None),
+            )
         ),
         check_vma=False,
     )

time: 202 us -> 199 us (0.985)
  the two profiles are of different devices: /device:TPU:30 before, /device:TPU:4 now
where the time goes in v6:
time: 199 us; the launch traced here: 197 us
  waiting for transfers between devices  76.3 us (38%)
  starting transfers between devices  61.1 us (31%)
  other arithmetic  20.5 us (10%)
  between operations  19.7 us (10%)
  local copies, waits for them, and re-layouts  13.6 us (7%)
  matrix products  6.28 us (3%)
    ppermute x12, starting transfers between devices, exchanged(): return lax.ppermute(x, (OUTER, INNER), [(i, i ^ bit) for i in range(count)])  43.6 us
    all_gather x2, waiting for transfers between devices, carried_in(): across = lax.all_gather(row_part, OUTER)  36.5 us
    ppermute x12, waiting for transfers between devices, exchanged(): return lax.ppermute(x, (OUTER, INNER), [(i, i ^ bit) for i in range(count)])  13.1 us
    all_gather x2, waiting for transfers between devices, carried_in(): in_row = lax.all_gather(aggregate, INNER)  10.7 us
    all_to_all x1, starting transfers between devices, local(): lax.all_to_all(feature_weight, 'fsdp', split_axis=0, concat_axis=1, tiled...  10.3 us
    all_to_all x1, waiting for transfers between devices, local(): lax.all_to_all(weight_columns, 'fsdp', split_axis=1, concat_axis=0, tiled...  8.27 us
    unnamed x34, local copies, waits for them, and re-layouts  8.23 us
    all_to_all x1, waiting for transfers between devices, local(): lax.all_to_all(feature_weight, 'fsdp', split_axis=0, concat_axis=1, tiled...  7.69 us
  transfers between devices with their start and end apart: 18, of which 12 were waited for; matrix products, arithmetic and copies ran while one was open for 10% of the time, Pallas kernels for 0%

profile of v6, /device:TPU:4, one launch (start us, length us, event | category | flops | bytes accessed | tf_op | source)
XLA Modules:
  0.0 197.4 jit_solution(10712466576853152778)
XLA Ops:
  10.2 2.6 %slice_add_fusion.3 = (f32[1,2,128,128]{3,2,1,0:T(8,128)}, f32[1,2,128,128]{3,2,1,0:T(8,128)S(1)}, f32[1,2,128,128]{3,2,1,0:T(8,128)S(1)}, f32[1,2,128,128]{3,2,1,0:T(8,128)}) fusion(f32[4,2,128,128]{3,2,1,0:T(8,128)S(1)} %fusion.26, pred[]{:T(512)} %bitcast.3, pred[]{:T(512)} %bitcast.2, pred[]{:T(512)} %bitcast.1), kind=kLoop, calls=%fused_computation.85 | loop fusion | flops 196608 | bytes 1048579 | tf_op jit(solution)/shard_map/add | solution.py:139
  12.9 10.3 %all-to-all-start = ((bf16[16,16,2]{1,2,0:T(2,128)(2,1)}), bf16[16,16,2]{1,2,0:T(2,128)(2,1)S(1)}, u32[]{:S(2)}, u32[]{:S(2)}) async-start(bf16[16,16,2]{1,2,0:T(2,128)(2,1)} %param.10), calls=%async_computation | async-start | bytes 16384 | tf_op jit(solution)/shard_map/all_to_all | solution.py:103
  23.2 7.7 %all-to-all-done = bf16[16,16,2]{1,2,0:T(2,128)(2,1)S(1)} async-done(((bf16[16,16,2]{1,2,0:T(2,128)(2,1)}), bf16[16,16,2]{1,2,0:T(2,128)(2,1)S(1)}, u32[]{:S(2)}, u32[]{:S(2)}) %all-to-all-start) | async-done | bytes 1056 | tf_op jit(solution)/shard_map/all_to_all | solution.py:103
  34.1 3.1 %collective-permute-start.1 = (bf16[2,128,4]{1,2,0:T(4,128)(2,1)S(1)}, bf16[2,128,4]{1,2,0:T(4,128)(2,1)S(1)}, u32[]{:S(2)}, u32[]{:S(2)}) collective-permute-start(bf16[2,128,4]{1,2,0:T(4,128)(2,1)S(1)} %maximum_select_fusion.5), channel_id=1, source_target_pairs={{0,16},{8,24},{16,0},{24,8},{32,48},{40,56},{48,32},{56,40},{64,80... | collective-permute-start | bytes 6152 | tf_op jit(solution)/shard_map/ppermute | solution.py:62
  39.6 2.4 %collective-permute-start.2 = (bf16[2,128,8]{1,2,0:T(8,128)(2,1)S(1)}, bf16[2,128,8]{1,2,0:T(8,128)(2,1)S(1)}, u32[]{:S(2)}, u32[]{:S(2)}) collective-permute-start(bf16[2,128,8]{1,2,0:T(8,128)(2,1)S(1)} %maximum_select_fusion.4), channel_id=1, source_target_pairs={{0,32},{8,40},{16,48},{24,56},{32,0},{40,8},{48,16},{56,24},{64,96... | collective-permute-start | bytes 12296 | tf_op jit(solution)/shard_map/ppermute | solution.py:62
  42.0 3.2 %all-gather.7.cloned.1.call-done = f32[8,2,128,128]{3,2,1,0:T(8,128)} async-done(((f32[1,2,128,128]{3,2,1,0:T(8,128)}), f32[8,2,128,128]{3,2,1,0:T(8,128)}) %all-gather.7.cloned.1.call-update) | async-done | bytes 1048592 | tf_op jit(solution)/shard_map/all_gather | solution.py:39
  45.2 2.1 %select_reduce_fusion.4 = (f32[2,128,128]{2,1,0:T(8,128)}, f32[2,128,128]{2,1,0:T(8,128)S(1)}) fusion(f32[8,2,128,128]{3,2,1,0:T(8,128)} %all-gather.7.cloned.1.call-done, pred[8]{0:T(512)(128)(4,1)S(1)} %get-tuple-element.39, pred[8]{0:T(512)(128)(4,1)S(1)} %get-tuple-element.38), kind=kLoop, calls=%fused_computation.36 | loop fusion | flops 983040 | bytes 1310736 | tf_op jit(solution)/shard_map/reduce_sum | solution.py:26
  48.2 3.0 %collective-permute-start.3 = (bf16[2,128,16]{1,2,0:T(8,128)(2,1)S(1)}, bf16[2,128,16]{1,2,0:T(8,128)(2,1)S(1)}, u32[]{:S(2)}, u32[]{:S(2)}) collective-permute-start(bf16[2,128,16]{1,2,0:T(8,128)(2,1)S(1)} %maximum_select_fusion.3), channel_id=1, source_target_pairs={{0,64},{8,72},{16,80},{24,88},{32,96},{40,104},{48,112},{56,120},{... | collective-permute-start | bytes 24584 | tf_op jit(solution)/shard_map/ppermute | solution.py:62
  53.8 3.9 %collective-permute-start.4 = (bf16[2,128,32]{1,2,0:T(8,128)(2,1)S(1)}, bf16[2,128,32]{1,2,0:T(8,128)(2,1)S(1)}, u32[]{:S(2)}, u32[]{:S(2)}) collective-permute-start(bf16[2,128,32]{1,2,0:T(8,128)(2,1)S(1)} %maximum_select_fusion.2), channel_id=1, source_target_pairs={{0,128},{8,136},{16,144},{24,152},{32,160},{40,168},{48,176},{56,1... | collective-permute-start | bytes 49160 | tf_op jit(solution)/shard_map/ppermute | solution.py:62
  60.3 7.2 %collective-permute-start.5 = (bf16[2,128,64]{1,2,0:T(8,128)(2,1)S(1)}, bf16[2,128,64]{1,2,0:T(8,128)(2,1)S(1)}, u32[]{:S(2)}, u32[]{:S(2)}) collective-permute-start(bf16[2,128,64]{1,2,0:T(8,128)(2,1)S(1)} %maximum_select_fusion.1), channel_id=1, source_target_pairs={{0,256},{8,264},{16,272},{24,280},{32,288},{40,296},{48,304},{56,3... | collective-permute-start | bytes 98312 | tf_op jit(solution)/shard_map/ppermute | solution.py:62
  71.5 18.1 %all-gather.11.cloned.1.call-done = f32[16,128,128]{2,1,0:T(8,128)} async-done(((f32[2,128,128]{2,1,0:T(8,128)}), f32[16,128,128]{2,1,0:T(8,128)}) %all-gather.11.cloned.1.call-update) | async-done | bytes 1048592 | tf_op jit(solution)/shard_map/all_gather | solution.py:50
  96.7 5.5 %collective-permute-start.6 = (f32[2,128,65]{1,2,0:T(8,128)S(1)}, f32[2,128,65]{1,2,0:T(8,128)S(1)}, u32[]{:S(2)}, u32[]{:S(2)}) collective-permute-start(f32[2,128,65]{1,2,0:T(8,128)S(1)} %pad_maximum_fusion), channel_id=1, source_target_pairs={{0,256},{8,264},{16,272},{24,280},{32,288},{40,296},{48,304},{56,3... | collective-permute-start | bytes 199688 | tf_op jit(solution)/shard_map/ppermute | solution.py:62
  102.2 4.7 %collective-permute-done.6 = f32[2,128,65]{1,2,0:T(8,128)S(1)} collective-permute-done((f32[2,128,65]{1,2,0:T(8,128)S(1)}, f32[2,128,65]{1,2,0:T(8,128)S(1)}, u32[]{:S(2)}, u32[]{:S(2)}) %collective-permute-start.6) | collective-permute-done | bytes 66592 | tf_op jit(solution)/shard_map/ppermute | solution.py:62
  107.1 4.5 %collective-permute-start.7 = (f32[2,128,33]{1,0,2:T(2,128)S(1)}, f32[2,128,33]{1,0,2:T(2,128)S(1)}, u32[]{:S(2)}, u32[]{:S(2)}) collective-permute-start(f32[2,128,33]{1,0,2:T(2,128)S(1)} %pad_maximum_fusion.1), channel_id=1, source_target_pairs={{0,128},{8,136},{16,144},{24,152},{32,160},{40,168},{48,176},{56,1... | collective-permute-start | bytes 101384 | tf_op jit(solution)/shard_map/ppermute | solution.py:62
  111.7 3.3 %fusion.46 = (f32[1,2,128,128]{3,2,1,0:T(8,128)}, f32[1,2,128,128]{3,2,1,0:T(8,128)S(1)}, f32[1,2,128,128]{3,2,1,0:T(8,128)}) fusion(f32[4,2,128,128]{3,2,1,0:T(8,128)S(1)} %fusion.38, pred[]{:T(512)} %bitcast.24, pred[]{:T(512)} %bitcast.1, pred[]{:T(512)} %bitcast.2, pred[]{:T(512)} %bitcast.3), kind=kLoop, calls=%fused_computation.79 | loop fusion | flops 229376 | bytes 917508 | tf_op jit(solution)/shard_map/jit(_where)/select_n | solution.py:202
  115.1 2.7 %collective-permute-start.8 = (f32[2,128,17]{1,0,2:T(2,128)S(1)}, f32[2,128,17]{1,0,2:T(2,128)S(1)}, u32[]{:S(2)}, u32[]{:S(2)}) collective-permute-start(f32[2,128,17]{1,0,2:T(2,128)S(1)} %pad_maximum_fusion.2), channel_id=1, source_target_pairs={{0,64},{8,72},{16,80},{24,88},{32,96},{40,104},{48,112},{56,120},{... | collective-permute-start | bytes 52232 | tf_op jit(solution)/shard_map/ppermute | solution.py:62
  121.8 2.3 %collective-permute-start.9 = (f32[2,128,9]{1,0,2:T(2,128)S(1)}, f32[2,128,9]{1,0,2:T(2,128)S(1)}, u32[]{:S(2)}, u32[]{:S(2)}) collective-permute-start(f32[2,128,9]{1,0,2:T(2,128)S(1)} %pad_maximum_fusion.3), channel_id=1, source_target_pairs={{0,32},{8,40},{16,48},{24,56},{32,0},{40,8},{48,16},{56,24},{64,96... | collective-permute-start | bytes 27656 | tf_op jit(solution)/shard_map/ppermute | solution.py:62
  124.2 4.7 %collective-permute-done.9 = f32[2,128,9]{1,0,2:T(2,128)S(1)} collective-permute-done((f32[2,128,9]{1,0,2:T(2,128)S(1)}, f32[2,128,9]{1,0,2:T(2,128)S(1)}, u32[]{:S(2)}, u32[]{:S(2)}) %collective-permute-start.9) | collective-permute-done | bytes 9248 | tf_op jit(solution)/shard_map/ppermute | solution.py:62
  128.9 4.9 %collective-permute-start.10 = (f32[2,128,5]{1,0,2:T(2,128)S(1)}, f32[2,128,5]{1,0,2:T(2,128)S(1)}, u32[]{:S(2)}, u32[]{:S(2)}) collective-permute-start(f32[2,128,5]{1,0,2:T(2,128)S(1)} %pad_maximum_fusion.4), channel_id=1, source_target_pairs={{0,16},{8,24},{16,0},{24,8},{32,48},{40,56},{48,32},{56,40},{64,80... | collective-permute-start | bytes 15368 | tf_op jit(solution)/shard_map/ppermute | solution.py:62
  133.8 7.5 %all-gather.9.cloned.1.call-done = f32[8,2,128,128]{3,2,1,0:T(8,128)} async-done(((f32[1,2,128,128]{3,2,1,0:T(8,128)}), f32[8,2,128,128]{3,2,1,0:T(8,128)}) %all-gather.9.cloned.1.call-update) | async-done | bytes 1048592 | tf_op jit(solution)/shard_map/all_gather | solution.py:39
  144.3 2.1 %collective-permute-start.11 = (f32[2,128,3]{1,0,2:T(2,128)S(1)}, f32[2,128,3]{1,0,2:T(2,128)S(1)}, u32[]{:S(2)}, u32[]{:S(2)}) collective-permute-start(f32[2,128,3]{1,0,2:T(2,128)S(1)} %pad_maximum_fusion.5), channel_id=1, source_target_pairs={{0,8},{8,0},{16,24},{24,16},{32,40},{40,32},{48,56},{56,48},{64,72... | collective-permute-start | bytes 9224 | tf_op jit(solution)/shard_map/ppermute | solution.py:62
  149.8 7.0 %all-to-all-start.1 = ((f32[2,128,2]{0,2,1:T(2,128)}), f32[2,128,2]{0,2,1:T(2,128)S(1)}, u32[]{:S(2)}, u32[]{:S(2)}) async-start(f32[2,128,2]{0,2,1:T(2,128)} %copy.183), calls=%async_computation.1 | async-start | bytes 262144 | tf_op jit(solution)/shard_map/all_to_all | solution.py:196
  158.1 8.3 %all-to-all-done.1 = f32[2,128,2]{0,2,1:T(2,128)S(1)} async-done(((f32[2,128,2]{0,2,1:T(2,128)}), f32[2,128,2]{0,2,1:T(2,128)S(1)}, u32[]{:S(2)}, u32[]{:S(2)}) %all-to-all-start.1) | async-done | bytes 2080 | tf_op jit(solution)/shard_map/all_to_all | solution.py:196
  167.2 18.3 %all-gather.13.cloned.1.call-done = f32[16,128,128]{2,1,0:T(8,128)} async-done(((f32[2,128,128]{2,1,0:T(8,128)}), f32[16,128,128]{2,1,0:T(8,128)}) %all-gather.13.cloned.1.call-update) | async-done | bytes 1048592 | tf_op jit(solution)/shard_map/all_gather | solution.py:50
  (144 shorter events, 38.1 us)
Async XLA Ops:
  7.2 38.0 %all-gather.7.cloned.1.call-start = ((), (), s32[]{:S(2)}) async-start(), calls=%async_computation.2 | async-start | bytes 1179648 | tf_op jit(solution)/shard_map/all_gather | solution.py:39
  8.8 1.1 copy-start.1
  12.8 78.2 %copy-start.3 = (f32[1,2,128,128]{3,2,1,0:T(8,128)}, f32[1,2,128,128]{3,2,1,0:T(8,128)S(1)}, u32[]{:S(2)}) copy-start(f32[1,2,128,128]{3,2,1,0:T(8,128)S(1)} %get-tuple-element.20) | copy-start | bytes 393220
  12.8 78.2 %copy-start.5 = (f32[1,2,128,128]{3,2,1,0:T(8,128)}, f32[1,2,128,128]{3,2,1,0:T(8,128)S(1)}, u32[]{:S(2)}) copy-start(f32[1,2,128,128]{3,2,1,0:T(8,128)S(1)} %get-tuple-element.21) | copy-start | bytes 393220
  12.9 18.1 %all-to-all-start = ((bf16[16,16,2]{1,2,0:T(2,128)(2,1)}), bf16[16,16,2]{1,2,0:T(2,128)(2,1)S(1)}, u32[]{:S(2)}, u32[]{:S(2)}) async-start(bf16[16,16,2]{1,2,0:T(2,128)(2,1)} %param.10), calls=%async_computation | async-start | bytes 16384 | tf_op jit(solution)/shard_map/all_to_all | solution.py:103
  23.2 66.4 %all-gather.11.cloned.1.call-start = ((), (), s32[]{:S(2)}) async-start(), calls=%async_computation.4 | async-start | bytes 1179648 | tf_op jit(solution)/shard_map/all_gather | solution.py:50
  31.0 3.0 %collective-permute-start = (bf16[2,128,2]{1,2,0:T(2,128)(2,1)S(1)}, bf16[2,128,2]{1,2,0:T(2,128)(2,1)S(1)}, u32[]{:S(2)}, u32[]{:S(2)}) collective-permute-start(bf16[2,128,2]{1,2,0:T(2,128)(2,1)S(1)} %all_to_all.23), channel_id=1, source_target_pairs={{0,8},{8,0},{16,24},{24,16},{32,40},{40,32},{48,56},{56,48},{64,72... | collective-permute-start | bytes 3080 | tf_op jit(solution)/shard_map/ppermute | solution.py:62
  34.1 5.5 %collective-permute-start.1 = (bf16[2,128,4]{1,2,0:T(4,128)(2,1)S(1)}, bf16[2,128,4]{1,2,0:T(4,128)(2,1)S(1)}, u32[]{:S(2)}, u32[]{:S(2)}) collective-permute-start(bf16[2,128,4]{1,2,0:T(4,128)(2,1)S(1)} %maximum_select_fusion.5), channel_id=1, source_target_pairs={{0,16},{8,24},{16,0},{24,8},{32,48},{40,56},{48,32},{56,40},{64,80... | collective-permute-start | bytes 6152 | tf_op jit(solution)/shard_map/ppermute | solution.py:62
  39.6 8.7 %collective-permute-start.2 = (bf16[2,128,8]{1,2,0:T(8,128)(2,1)S(1)}, bf16[2,128,8]{1,2,0:T(8,128)(2,1)S(1)}, u32[]{:S(2)}, u32[]{:S(2)}) collective-permute-start(bf16[2,128,8]{1,2,0:T(8,128)(2,1)S(1)} %maximum_select_fusion.4), channel_id=1, source_target_pairs={{0,32},{8,40},{16,48},{24,56},{32,0},{40,8},{48,16},{56,24},{64,96... | collective-permute-start | bytes 12296 | tf_op jit(solution)/shard_map/ppermute | solution.py:62
  47.3 20.9 %copy-start.2 = (bf16[512,256]{1,0:T(8,128)(2,1)S(1)}, bf16[512,256]{1,0:T(8,128)(2,1)}, u32[]{:S(2)}) copy-start(bf16[512,256]{1,0:T(8,128)(2,1)} %param.7) | copy-start | bytes 786436
  47.3 94.0 %all-gather.9.cloned.1.call-start = ((), (), s32[]{:S(2)}) async-start(), calls=%async_computation.3 | async-start | bytes 1179648 | tf_op jit(solution)/shard_map/all_gather | solution.py:39
  48.2 5.5 %collective-permute-start.3 = (bf16[2,128,16]{1,2,0:T(8,128)(2,1)S(1)}, bf16[2,128,16]{1,2,0:T(8,128)(2,1)S(1)}, u32[]{:S(2)}, u32[]{:S(2)}) collective-permute-start(bf16[2,128,16]{1,2,0:T(8,128)(2,1)S(1)} %maximum_select_fusion.3), channel_id=1, source_target_pairs={{0,64},{8,72},{16,80},{24,88},{32,96},{40,104},{48,112},{56,120},{... | collective-permute-start | bytes 24584 | tf_op jit(solution)/shard_map/ppermute | solution.py:62
  53.8 6.5 %collective-permute-start.4 = (bf16[2,128,32]{1,2,0:T(8,128)(2,1)S(1)}, bf16[2,128,32]{1,2,0:T(8,128)(2,1)S(1)}, u32[]{:S(2)}, u32[]{:S(2)}) collective-permute-start(bf16[2,128,32]{1,2,0:T(8,128)(2,1)S(1)} %maximum_select_fusion.2), channel_id=1, source_target_pairs={{0,128},{8,136},{16,144},{24,152},{32,160},{40,168},{48,176},{56,1... | collective-permute-start | bytes 49160 | tf_op jit(solution)/shard_map/ppermute | solution.py:62
  60.3 10.0 %collective-permute-start.5 = (bf16[2,128,64]{1,2,0:T(8,128)(2,1)S(1)}, bf16[2,128,64]{1,2,0:T(8,128)(2,1)S(1)}, u32[]{:S(2)}, u32[]{:S(2)}) collective-permute-start(bf16[2,128,64]{1,2,0:T(8,128)(2,1)S(1)} %maximum_select_fusion.1), channel_id=1, source_target_pairs={{0,256},{8,264},{16,272},{24,280},{32,288},{40,296},{48,304},{56,3... | collective-permute-start | bytes 98312 | tf_op jit(solution)/shard_map/ppermute | solution.py:62
  91.9 3.0 %copy-start.9 = (f32[1,2,128,128]{3,2,1,0:T(8,128)}, f32[1,2,128,128]{3,2,1,0:T(8,128)S(1)}, u32[]{:S(2)}) copy-start(f32[1,2,128,128]{3,2,1,0:T(8,128)S(1)} %stack.6) | copy-start | bytes 393220
  94.7 1.0 copy-start.6
  96.7 10.3 %collective-permute-start.6 = (f32[2,128,65]{1,2,0:T(8,128)S(1)}, f32[2,128,65]{1,2,0:T(8,128)S(1)}, u32[]{:S(2)}, u32[]{:S(2)}) collective-permute-start(f32[2,128,65]{1,2,0:T(8,128)S(1)} %pad_maximum_fusion), channel_id=1, source_target_pairs={{0,256},{8,264},{16,272},{24,280},{32,288},{40,296},{48,304},{56,3... | collective-permute-start | bytes 199688 | tf_op jit(solution)/shard_map/ppermute | solution.py:62
  107.1 7.9 %collective-permute-start.7 = (f32[2,128,33]{1,0,2:T(2,128)S(1)}, f32[2,128,33]{1,0,2:T(2,128)S(1)}, u32[]{:S(2)}, u32[]{:S(2)}) collective-permute-start(f32[2,128,33]{1,0,2:T(2,128)S(1)} %pad_maximum_fusion.1), channel_id=1, source_target_pairs={{0,128},{8,136},{16,144},{24,152},{32,160},{40,168},{48,176},{56,1... | collective-permute-start | bytes 101384 | tf_op jit(solution)/shard_map/ppermute | solution.py:62
  115.0 70.5 %all-gather.13.cloned.1.call-start = ((), (), s32[]{:S(2)}) async-start(), calls=%async_computation.5 | async-start | bytes 1179648 | tf_op jit(solution)/shard_map/all_gather | solution.py:50
  115.1 6.6 %collective-permute-start.8 = (f32[2,128,17]{1,0,2:T(2,128)S(1)}, f32[2,128,17]{1,0,2:T(2,128)S(1)}, u32[]{:S(2)}, u32[]{:S(2)}) collective-permute-start(f32[2,128,17]{1,0,2:T(2,128)S(1)} %pad_maximum_fusion.2), channel_id=1, source_target_pairs={{0,64},{8,72},{16,80},{24,88},{32,96},{40,104},{48,112},{56,120},{... | collective-permute-start | bytes 52232 | tf_op jit(solution)/shard_map/ppermute | solution.py:62
  121.8 7.1 %collective-permute-start.9 = (f32[2,128,9]{1,0,2:T(2,128)S(1)}, f32[2,128,9]{1,0,2:T(2,128)S(1)}, u32[]{:S(2)}, u32[]{:S(2)}) collective-permute-start(f32[2,128,9]{1,0,2:T(2,128)S(1)} %pad_maximum_fusion.3), channel_id=1, source_target_pairs={{0,32},{8,40},{16,48},{24,56},{32,0},{40,8},{48,16},{56,24},{64,96... | collective-permute-start | bytes 27656 | tf_op jit(solution)/shard_map/ppermute | solution.py:62
  128.9 14.8 %collective-permute-start.10 = (f32[2,128,5]{1,0,2:T(2,128)S(1)}, f32[2,128,5]{1,0,2:T(2,128)S(1)}, u32[]{:S(2)}, u32[]{:S(2)}) collective-permute-start(f32[2,128,5]{1,0,2:T(2,128)S(1)} %pad_maximum_fusion.4), channel_id=1, source_target_pairs={{0,16},{8,24},{16,0},{24,8},{32,48},{40,56},{48,32},{56,40},{64,80... | collective-permute-start | bytes 15368 | tf_op jit(solution)/shard_map/ppermute | solution.py:62
  144.3 4.6 %collective-permute-start.11 = (f32[2,128,3]{1,0,2:T(2,128)S(1)}, f32[2,128,3]{1,0,2:T(2,128)S(1)}, u32[]{:S(2)}, u32[]{:S(2)}) collective-permute-start(f32[2,128,3]{1,0,2:T(2,128)S(1)} %pad_maximum_fusion.5), channel_id=1, source_target_pairs={{0,8},{8,0},{16,24},{24,16},{32,40},{40,32},{48,56},{56,48},{64,72... | collective-permute-start | bytes 9224 | tf_op jit(solution)/shard_map/ppermute | solution.py:62
  149.8 16.6 %all-to-all-start.1 = ((f32[2,128,2]{0,2,1:T(2,128)}), f32[2,128,2]{0,2,1:T(2,128)S(1)}, u32[]{:S(2)}, u32[]{:S(2)}) async-start(f32[2,128,2]{0,2,1:T(2,128)} %copy.183), calls=%async_computation.1 | async-start | bytes 262144 | tf_op jit(solution)/shard_map/all_to_all | solution.py:196
  (9 other events, 7.5 us)
Sparse Core Ops, SparseCore 0:
  13.0 32.1 all-gather.6
  47.8 41.7 all-gather.10
  115.1 26.1 all-gather.8
  143.8 41.6 all-gather.12

commit v7 on v6

--- a/solution.py
+++ b/solution.py
@@ -36,7 +36,7 @@
     bound = last_open(near)
     cols = jnp.arange(inner)
     rows = jnp.arange(outer)
-    in_row = lax.all_gather(aggregate, INNER)
+    in_row = lax.all_gather(aggregate.astype(jnp.bfloat16), INNER).astype(jnp.float32)
     if backward:
         mine = (cols > col) & (row * inner + cols <= bound)
         row_bound = last_open(row * inner)
@@ -47,7 +47,7 @@
         carry = (row * inner + cols >= row_bound)
     local_sum = masked_sum(mine, in_row)
     row_part = masked_sum(carry, in_row)
-    across = lax.all_gather(row_part, OUTER)
+    across = lax.all_gather(row_part.astype(jnp.bfloat16), OUTER).astype(jnp.float32)
     bound_row = bound // inner
     if backward:
         take = (rows > row) & (rows <= bound_row)

time: 199 us -> 203 us (1.020)
  the two profiles are of different devices: /device:TPU:4 before, /device:TPU:1 now
where the time goes in v7:
time: 203 us; the launch traced here: 202 us
  blocking collectives  73.4 us (36%)
  starting transfers between devices  69.4 us (34%)
  waiting for transfers between devices  24.4 us (12%)
  other arithmetic  12 us (6%)
  local copies, waits for them, and re-layouts  10.4 us (5%)
  matrix products  6.34 us (3%)
  between operations  6.32 us (3%)
    ppermute x12, starting transfers between devices, exchanged(): return lax.ppermute(x, (OUTER, INNER), [(i, i ^ bit) for i in range(count)])  51.6 us
    all_gather x2, blocking collectives, carried_in(): lax.all_gather(row_part.astype(jnp.bfloat16), OUTER).astype(jnp.float32)  40.9 us
    all_gather x2, blocking collectives, carried_in(): lax.all_gather(aggregate.astype(jnp.bfloat16), INNER).astype(jnp.float32)  32.6 us
    ppermute x12, waiting for transfers between devices, exchanged(): return lax.ppermute(x, (OUTER, INNER), [(i, i ^ bit) for i in range(count)])  16.5 us
    all_to_all x1, starting transfers between devices, local(): lax.all_to_all(feature_weight, 'fsdp', split_axis=0, concat_axis=1, tiled...  10.9 us
    all_to_all x1, waiting for transfers between devices, local(): lax.all_to_all(weight_columns, 'fsdp', split_axis=1, concat_axis=0, tiled...  7.89 us
    all_to_all x1, starting transfers between devices, local(): lax.all_to_all(weight_columns, 'fsdp', split_axis=1, concat_axis=0, tiled...  6.93 us
    unnamed x14, local copies, waits for them, and re-layouts  5.16 us
  transfers between devices with their start and end apart: 14, of which 9 were waited for; matrix products, arithmetic and copies ran while one was open for 10% of the time, Pallas kernels for 0%

profile of v7, /device:TPU:1, one launch (start us, length us, event | category | flops | bytes accessed | tf_op | source)
XLA Modules:
  0.0 202.2 jit_solution(14828175544442528136)
XLA Ops:
  0.6 10.9 %all-to-all-start = ((bf16[16,16,2]{1,2,0:T(2,128)(2,1)}), bf16[16,16,2]{1,2,0:T(2,128)(2,1)S(1)}, u32[]{:S(2)}, u32[]{:S(2)}) async-start(bf16[16,16,2]{1,2,0:T(2,128)(2,1)} %param.10), calls=%async_computation | async-start | bytes 16384 | tf_op jit(solution)/shard_map/all_to_all | solution.py:103
  16.4 14.3 %all_gather.16 = bf16[8,2,128,128]{3,2,1,0:T(8,128)(2,1)S(1)} all-gather(bf16[1,2,128,128]{3,2,1,0:T(8,128)(2,1)S(1)} %get-tuple-element.19), channel_id=1, replica_groups=mesh['seq_row'=8,'seq_col'=8,'fsdp'=8] {'seq_col'}, dimensions={0}, use_global_device_ids=true | all-gather | bytes 589824 | tf_op jit(solution)/shard_map/all_gather | solution.py:39
  32.9 20.9 %all-gather = bf16[16,128,128]{2,1,0:T(8,128)(2,1)S(1)} all-gather(bf16[2,128,128]{2,1,0:T(8,128)(2,1)S(1)} %get-tuple-element.10), channel_id=2, replica_groups=mesh['seq_row'=8,'seq_col'=8,'fsdp'=8] {'seq_row'}, dimensions={0}, use_global_device_ids=true | all-gather | bytes 589824 | tf_op jit(solution)/shard_map/all_gather | solution.py:50
  54.6 8.1 %collective-permute-start = (bf16[2,128,2]{1,2,0:T(2,128)(2,1)S(1)}, bf16[2,128,2]{1,2,0:T(2,128)(2,1)S(1)}, u32[]{:S(2)}, u32[]{:S(2)}) collective-permute-start(bf16[2,128,2]{1,2,0:T(2,128)(2,1)S(1)} %all_to_all.23), channel_id=1, source_target_pairs={{0,8},{8,0},{16,24},{24,16},{32,40},{40,32},{48,56},{56,48},{64,72... | collective-permute-start | bytes 3080 | tf_op jit(solution)/shard_map/ppermute | solution.py:62
  65.7 2.8 %collective-permute-start.1 = (bf16[2,128,4]{1,2,0:T(4,128)(2,1)S(1)}, bf16[2,128,4]{1,2,0:T(4,128)(2,1)S(1)}, u32[]{:S(2)}, u32[]{:S(2)}) collective-permute-start(bf16[2,128,4]{1,2,0:T(4,128)(2,1)S(1)} %maximum_select_fusion.5), channel_id=1, source_target_pairs={{0,16},{8,24},{16,0},{24,8},{32,48},{40,56},{48,32},{56,40},{64,80... | collective-permute-start | bytes 6152 | tf_op jit(solution)/shard_map/ppermute | solution.py:62
  70.0 3.8 %collective-permute-start.2 = (bf16[2,128,8]{1,2,0:T(8,128)(2,1)S(1)}, bf16[2,128,8]{1,2,0:T(8,128)(2,1)S(1)}, u32[]{:S(2)}, u32[]{:S(2)}) collective-permute-start(bf16[2,128,8]{1,2,0:T(8,128)(2,1)S(1)} %maximum_select_fusion.4), channel_id=1, source_target_pairs={{0,32},{8,40},{16,48},{24,56},{32,0},{40,8},{48,16},{56,24},{64,96... | collective-permute-start | bytes 12296 | tf_op jit(solution)/shard_map/ppermute | solution.py:62
  75.9 2.3 %collective-permute-start.3 = (bf16[2,128,16]{1,2,0:T(8,128)(2,1)S(1)}, bf16[2,128,16]{1,2,0:T(8,128)(2,1)S(1)}, u32[]{:S(2)}, u32[]{:S(2)}) collective-permute-start(bf16[2,128,16]{1,2,0:T(8,128)(2,1)S(1)} %maximum_select_fusion.3), channel_id=1, source_target_pairs={{0,64},{8,72},{16,80},{24,88},{32,96},{40,104},{48,112},{56,120},{... | collective-permute-start | bytes 24584 | tf_op jit(solution)/shard_map/ppermute | solution.py:62
  78.2 2.1 %collective-permute-done.3 = bf16[2,128,16]{1,2,0:T(8,128)(2,1)S(1)} collective-permute-done((bf16[2,128,16]{1,2,0:T(8,128)(2,1)S(1)}, bf16[2,128,16]{1,2,0:T(8,128)(2,1)S(1)}, u32[]{:S(2)}, u32[]{:S(2)}) %collective-permute-start.3) | collective-permute-done | bytes 8224 | tf_op jit(solution)/shard_map/ppermute | solution.py:62
  80.3 3.9 %collective-permute-start.4 = (bf16[2,128,32]{1,2,0:T(8,128)(2,1)S(1)}, bf16[2,128,32]{1,2,0:T(8,128)(2,1)S(1)}, u32[]{:S(2)}, u32[]{:S(2)}) collective-permute-start(bf16[2,128,32]{1,2,0:T(8,128)(2,1)S(1)} %maximum_select_fusion.2), channel_id=1, source_target_pairs={{0,128},{8,136},{16,144},{24,152},{32,160},{40,168},{48,176},{56,1... | collective-permute-start | bytes 49160 | tf_op jit(solution)/shard_map/ppermute | solution.py:62
  88.4 4.0 %collective-permute-start.5 = (bf16[2,128,64]{1,2,0:T(8,128)(2,1)S(1)}, bf16[2,128,64]{1,2,0:T(8,128)(2,1)S(1)}, u32[]{:S(2)}, u32[]{:S(2)}) collective-permute-start(bf16[2,128,64]{1,2,0:T(8,128)(2,1)S(1)} %maximum_select_fusion.1), channel_id=1, source_target_pairs={{0,256},{8,264},{16,272},{24,280},{32,288},{40,296},{48,304},{56,3... | collective-permute-start | bytes 98312 | tf_op jit(solution)/shard_map/ppermute | solution.py:62
  94.6 2.4 %collective-permute-done.5 = bf16[2,128,64]{1,2,0:T(8,128)(2,1)S(1)} collective-permute-done((bf16[2,128,64]{1,2,0:T(8,128)(2,1)S(1)}, bf16[2,128,64]{1,2,0:T(8,128)(2,1)S(1)}, u32[]{:S(2)}, u32[]{:S(2)}) %collective-permute-start.5) | collective-permute-done | bytes 32800 | tf_op jit(solution)/shard_map/ppermute | solution.py:62
  102.1 4.0 %collective-permute-start.6 = (f32[2,128,65]{1,2,0:T(8,128)S(1)}, f32[2,128,65]{1,2,0:T(8,128)S(1)}, u32[]{:S(2)}, u32[]{:S(2)}) collective-permute-start(f32[2,128,65]{1,2,0:T(8,128)S(1)} %pad_maximum_fusion), channel_id=1, source_target_pairs={{0,256},{8,264},{16,272},{24,280},{32,288},{40,296},{48,304},{56,3... | collective-permute-start | bytes 199688 | tf_op jit(solution)/shard_map/ppermute | solution.py:62
  106.2 2.6 %fusion.53 = (bf16[1,2,128,128]{3,2,1,0:T(8,128)(2,1)S(1)}, f32[1,2,128,128]{3,2,1,0:T(8,128)S(1)}, f32[1,2,128,128]{3,2,1,0:T(8,128)S(1)}) fusion(f32[4,2,128,128]{3,2,1,0:T(8,128)S(1)} %fusion.44, pred[]{:T(512)} %bitcast.24, pred[]{:T(512)} %bitcast.1, pred[]{:T(512)} %bitcast.2, pred[]{:T(512)} %bitcast.3), kind=kLoop, calls=%fused_computation.86 | loop fusion | flops 262144 | bytes 851972 | tf_op jit(solution)/shard_map/convert_element_type | solution.py:39
  109.5 18.3 %all_gather.18 = bf16[8,2,128,128]{3,2,1,0:T(8,128)(2,1)S(1)} all-gather(bf16[1,2,128,128]{3,2,1,0:T(8,128)(2,1)S(1)} %get-tuple-element.16), channel_id=1, replica_groups=mesh['seq_row'=8,'seq_col'=8,'fsdp'=8] {'seq_col'}, dimensions={0}, use_global_device_ids=true | all-gather | bytes 589824 | tf_op jit(solution)/shard_map/all_gather | solution.py:39
  128.1 20.0 %all-gather.1 = bf16[16,128,128]{2,1,0:T(8,128)(2,1)S(1)} all-gather(bf16[2,128,128]{2,1,0:T(8,128)(2,1)S(1)} %get-tuple-element.8), channel_id=3, replica_groups=mesh['seq_row'=8,'seq_col'=8,'fsdp'=8] {'seq_row'}, dimensions={0}, use_global_device_ids=true | all-gather | bytes 589824 | tf_op jit(solution)/shard_map/all_gather | solution.py:50
  148.5 2.8 %collective-permute-start.7 = (f32[2,128,33]{1,0,2:T(2,128)S(1)}, f32[2,128,33]{1,0,2:T(2,128)S(1)}, u32[]{:S(2)}, u32[]{:S(2)}) collective-permute-start(f32[2,128,33]{1,0,2:T(2,128)S(1)} %pad_maximum_fusion.1), channel_id=1, source_target_pairs={{0,128},{8,136},{16,144},{24,152},{32,160},{40,168},{48,176},{56,1... | collective-permute-start | bytes 101384 | tf_op jit(solution)/shard_map/ppermute | solution.py:62
  151.6 2.4 %collective-permute-done.7 = f32[2,128,33]{1,0,2:T(2,128)S(1)} collective-permute-done((f32[2,128,33]{1,0,2:T(2,128)S(1)}, f32[2,128,33]{1,0,2:T(2,128)S(1)}, u32[]{:S(2)}, u32[]{:S(2)}) %collective-permute-start.7) | collective-permute-done | bytes 33824 | tf_op jit(solution)/shard_map/ppermute | solution.py:62
  156.3 2.3 %collective-permute-done.8 = f32[2,128,17]{1,0,2:T(2,128)S(1)} collective-permute-done((f32[2,128,17]{1,0,2:T(2,128)S(1)}, f32[2,128,17]{1,0,2:T(2,128)S(1)}, u32[]{:S(2)}, u32[]{:S(2)}) %collective-permute-start.8) | collective-permute-done | bytes 17440 | tf_op jit(solution)/shard_map/ppermute | solution.py:62
  158.7 3.1 %collective-permute-start.9 = (f32[2,128,9]{1,0,2:T(2,128)S(1)}, f32[2,128,9]{1,0,2:T(2,128)S(1)}, u32[]{:S(2)}, u32[]{:S(2)}) collective-permute-start(f32[2,128,9]{1,0,2:T(2,128)S(1)} %pad_maximum_fusion.3), channel_id=1, source_target_pairs={{0,32},{8,40},{16,48},{24,56},{32,0},{40,8},{48,16},{56,24},{64,96... | collective-permute-start | bytes 27656 | tf_op jit(solution)/shard_map/ppermute | solution.py:62
  162.1 2.5 %collective-permute-done.9 = f32[2,128,9]{1,0,2:T(2,128)S(1)} collective-permute-done((f32[2,128,9]{1,0,2:T(2,128)S(1)}, f32[2,128,9]{1,0,2:T(2,128)S(1)}, u32[]{:S(2)}, u32[]{:S(2)}) %collective-permute-start.9) | collective-permute-done | bytes 9248 | tf_op jit(solution)/shard_map/ppermute | solution.py:62
  164.7 2.6 %collective-permute-start.10 = (f32[2,128,5]{1,0,2:T(2,128)S(1)}, f32[2,128,5]{1,0,2:T(2,128)S(1)}, u32[]{:S(2)}, u32[]{:S(2)}) collective-permute-start(f32[2,128,5]{1,0,2:T(2,128)S(1)} %pad_maximum_fusion.4), channel_id=1, source_target_pairs={{0,16},{8,24},{16,0},{24,8},{32,48},{40,56},{48,32},{56,40},{64,80... | collective-permute-start | bytes 15368 | tf_op jit(solution)/shard_map/ppermute | solution.py:62
  169.1 12.2 %collective-permute-start.11 = (f32[2,128,3]{1,0,2:T(2,128)S(1)}, f32[2,128,3]{1,0,2:T(2,128)S(1)}, u32[]{:S(2)}, u32[]{:S(2)}) collective-permute-start(f32[2,128,3]{1,0,2:T(2,128)S(1)} %pad_maximum_fusion.5), channel_id=1, source_target_pairs={{0,8},{8,0},{16,24},{24,16},{32,40},{40,32},{48,56},{56,48},{64,72... | collective-permute-start | bytes 9224 | tf_op jit(solution)/shard_map/ppermute | solution.py:62
  186.0 6.9 %all-to-all-start.1 = ((f32[2,128,2]{0,2,1:T(2,128)}), f32[2,128,2]{0,2,1:T(2,128)S(1)}, u32[]{:S(2)}, u32[]{:S(2)}) async-start(f32[2,128,2]{0,2,1:T(2,128)} %copy.183), calls=%async_computation.1 | async-start | bytes 262144 | tf_op jit(solution)/shard_map/all_to_all | solution.py:196
  193.5 7.9 %all-to-all-done.1 = f32[2,128,2]{0,2,1:T(2,128)S(1)} async-done(((f32[2,128,2]{0,2,1:T(2,128)}), f32[2,128,2]{0,2,1:T(2,128)S(1)}, u32[]{:S(2)}, u32[]{:S(2)}) %all-to-all-start.1) | async-done | bytes 2080 | tf_op jit(solution)/shard_map/all_to_all | solution.py:196
  (116 shorter events, 32.8 us)
Async XLA Ops:
  0.6 53.9 %all-to-all-start = ((bf16[16,16,2]{1,2,0:T(2,128)(2,1)}), bf16[16,16,2]{1,2,0:T(2,128)(2,1)S(1)}, u32[]{:S(2)}, u32[]{:S(2)}) async-start(bf16[16,16,2]{1,2,0:T(2,128)(2,1)} %param.10), calls=%async_computation | async-start | bytes 16384 | tf_op jit(solution)/shard_map/all_to_all | solution.py:103
  11.5 0.7 copy-start.3
  13.0 1.1 copy-start.1
  54.6 11.0 %collective-permute-start = (bf16[2,128,2]{1,2,0:T(2,128)(2,1)S(1)}, bf16[2,128,2]{1,2,0:T(2,128)(2,1)S(1)}, u32[]{:S(2)}, u32[]{:S(2)}) collective-permute-start(bf16[2,128,2]{1,2,0:T(2,128)(2,1)S(1)} %all_to_all.23), channel_id=1, source_target_pairs={{0,8},{8,0},{16,24},{24,16},{32,40},{40,32},{48,56},{56,48},{64,72... | collective-permute-start | bytes 3080 | tf_op jit(solution)/shard_map/ppermute | solution.py:62
  65.7 4.3 %collective-permute-start.1 = (bf16[2,128,4]{1,2,0:T(4,128)(2,1)S(1)}, bf16[2,128,4]{1,2,0:T(4,128)(2,1)S(1)}, u32[]{:S(2)}, u32[]{:S(2)}) collective-permute-start(bf16[2,128,4]{1,2,0:T(4,128)(2,1)S(1)} %maximum_select_fusion.5), channel_id=1, source_target_pairs={{0,16},{8,24},{16,0},{24,8},{32,48},{40,56},{48,32},{56,40},{64,80... | collective-permute-start | bytes 6152 | tf_op jit(solution)/shard_map/ppermute | solution.py:62
  70.0 5.9 %collective-permute-start.2 = (bf16[2,128,8]{1,2,0:T(8,128)(2,1)S(1)}, bf16[2,128,8]{1,2,0:T(8,128)(2,1)S(1)}, u32[]{:S(2)}, u32[]{:S(2)}) collective-permute-start(bf16[2,128,8]{1,2,0:T(8,128)(2,1)S(1)} %maximum_select_fusion.4), channel_id=1, source_target_pairs={{0,32},{8,40},{16,48},{24,56},{32,0},{40,8},{48,16},{56,24},{64,96... | collective-permute-start | bytes 12296 | tf_op jit(solution)/shard_map/ppermute | solution.py:62
  73.8 19.3 %copy-start.2 = (bf16[512,256]{1,0:T(8,128)(2,1)S(1)}, bf16[512,256]{1,0:T(8,128)(2,1)}, u32[]{:S(2)}) copy-start(bf16[512,256]{1,0:T(8,128)(2,1)} %param.7) | copy-start | bytes 786436
  75.9 4.4 %collective-permute-start.3 = (bf16[2,128,16]{1,2,0:T(8,128)(2,1)S(1)}, bf16[2,128,16]{1,2,0:T(8,128)(2,1)S(1)}, u32[]{:S(2)}, u32[]{:S(2)}) collective-permute-start(bf16[2,128,16]{1,2,0:T(8,128)(2,1)S(1)} %maximum_select_fusion.3), channel_id=1, source_target_pairs={{0,64},{8,72},{16,80},{24,88},{32,96},{40,104},{48,112},{56,120},{... | collective-permute-start | bytes 24584 | tf_op jit(solution)/shard_map/ppermute | solution.py:62
  80.3 8.1 %collective-permute-start.4 = (bf16[2,128,32]{1,2,0:T(8,128)(2,1)S(1)}, bf16[2,128,32]{1,2,0:T(8,128)(2,1)S(1)}, u32[]{:S(2)}, u32[]{:S(2)}) collective-permute-start(bf16[2,128,32]{1,2,0:T(8,128)(2,1)S(1)} %maximum_select_fusion.2), channel_id=1, source_target_pairs={{0,128},{8,136},{16,144},{24,152},{32,160},{40,168},{48,176},{56,1... | collective-permute-start | bytes 49160 | tf_op jit(solution)/shard_map/ppermute | solution.py:62
  88.4 8.6 %collective-permute-start.5 = (bf16[2,128,64]{1,2,0:T(8,128)(2,1)S(1)}, bf16[2,128,64]{1,2,0:T(8,128)(2,1)S(1)}, u32[]{:S(2)}, u32[]{:S(2)}) collective-permute-start(bf16[2,128,64]{1,2,0:T(8,128)(2,1)S(1)} %maximum_select_fusion.1), channel_id=1, source_target_pairs={{0,256},{8,264},{16,272},{24,280},{32,288},{40,296},{48,304},{56,3... | collective-permute-start | bytes 98312 | tf_op jit(solution)/shard_map/ppermute | solution.py:62
  92.4 0.7 copy-start.4
  93.1 1.0 copy-start
  102.1 46.1 %collective-permute-start.6 = (f32[2,128,65]{1,2,0:T(8,128)S(1)}, f32[2,128,65]{1,2,0:T(8,128)S(1)}, u32[]{:S(2)}, u32[]{:S(2)}) collective-permute-start(f32[2,128,65]{1,2,0:T(8,128)S(1)} %pad_maximum_fusion), channel_id=1, source_target_pairs={{0,256},{8,264},{16,272},{24,280},{32,288},{40,296},{48,304},{56,3... | collective-permute-start | bytes 199688 | tf_op jit(solution)/shard_map/ppermute | solution.py:62
  148.5 5.6 %collective-permute-start.7 = (f32[2,128,33]{1,0,2:T(2,128)S(1)}, f32[2,128,33]{1,0,2:T(2,128)S(1)}, u32[]{:S(2)}, u32[]{:S(2)}) collective-permute-start(f32[2,128,33]{1,0,2:T(2,128)S(1)} %pad_maximum_fusion.1), channel_id=1, source_target_pairs={{0,128},{8,136},{16,144},{24,152},{32,160},{40,168},{48,176},{56,1... | collective-permute-start | bytes 101384 | tf_op jit(solution)/shard_map/ppermute | solution.py:62
  154.1 4.5 %collective-permute-start.8 = (f32[2,128,17]{1,0,2:T(2,128)S(1)}, f32[2,128,17]{1,0,2:T(2,128)S(1)}, u32[]{:S(2)}, u32[]{:S(2)}) collective-permute-start(f32[2,128,17]{1,0,2:T(2,128)S(1)} %pad_maximum_fusion.2), channel_id=1, source_target_pairs={{0,64},{8,72},{16,80},{24,88},{32,96},{40,104},{48,112},{56,120},{... | collective-permute-start | bytes 52232 | tf_op jit(solution)/shard_map/ppermute | solution.py:62
  158.7 5.9 %collective-permute-start.9 = (f32[2,128,9]{1,0,2:T(2,128)S(1)}, f32[2,128,9]{1,0,2:T(2,128)S(1)}, u32[]{:S(2)}, u32[]{:S(2)}) collective-permute-start(f32[2,128,9]{1,0,2:T(2,128)S(1)} %pad_maximum_fusion.3), channel_id=1, source_target_pairs={{0,32},{8,40},{16,48},{24,56},{32,0},{40,8},{48,16},{56,24},{64,96... | collective-permute-start | bytes 27656 | tf_op jit(solution)/shard_map/ppermute | solution.py:62
  164.7 4.4 %collective-permute-start.10 = (f32[2,128,5]{1,0,2:T(2,128)S(1)}, f32[2,128,5]{1,0,2:T(2,128)S(1)}, u32[]{:S(2)}, u32[]{:S(2)}) collective-permute-start(f32[2,128,5]{1,0,2:T(2,128)S(1)} %pad_maximum_fusion.4), channel_id=1, source_target_pairs={{0,16},{8,24},{16,0},{24,8},{32,48},{40,56},{48,32},{56,40},{64,80... | collective-permute-start | bytes 15368 | tf_op jit(solution)/shard_map/ppermute | solution.py:62
  169.1 16.1 %collective-permute-start.11 = (f32[2,128,3]{1,0,2:T(2,128)S(1)}, f32[2,128,3]{1,0,2:T(2,128)S(1)}, u32[]{:S(2)}, u32[]{:S(2)}) collective-permute-start(f32[2,128,3]{1,0,2:T(2,128)S(1)} %pad_maximum_fusion.5), channel_id=1, source_target_pairs={{0,8},{8,0},{16,24},{24,16},{32,40},{40,32},{48,56},{56,48},{64,72... | collective-permute-start | bytes 9224 | tf_op jit(solution)/shard_map/ppermute | solution.py:62
  186.0 15.4 %all-to-all-start.1 = ((f32[2,128,2]{0,2,1:T(2,128)}), f32[2,128,2]{0,2,1:T(2,128)S(1)}, u32[]{:S(2)}, u32[]{:S(2)}) async-start(f32[2,128,2]{0,2,1:T(2,128)} %copy.183), calls=%async_computation.1 | async-start | bytes 262144 | tf_op jit(solution)/shard_map/all_to_all | solution.py:196

commit v8 on v7

--- a/solution.py
+++ b/solution.py
@@ -26,7 +26,7 @@
     return jnp.sum(jnp.where(mask[:, None, None, None], stacked, 0.0), 0)
 
 
-def carried_in(aggregate, last_open, backward):
+def carried_in(aggregate, last_open, backward, kind, extra=None):
     inner = lax.axis_size(INNER)
     outer = lax.axis_size(OUTER)
     col = lax.axis_index(INNER)
@@ -36,7 +36,15 @@
     bound = last_open(near)
     cols = jnp.arange(inner)
     rows = jnp.arange(outer)
-    in_row = lax.all_gather(aggregate.astype(jnp.bfloat16), INNER).astype(jnp.float32)
+    width = aggregate.shape[-1]
+    sent = aggregate.astype(kind)
+    if extra is not None:
+        sent = jnp.concatenate([sent, extra.astype(kind)], -1)
+    in_row = lax.all_gather(sent, INNER)
+    if extra is not None:
+        row_extra = jnp.moveaxis(in_row[..., width:], 0, -2)
+        row_extra = row_extra.reshape(row_extra.shape[:-2] + (-1,))
+    in_row = in_row[..., :width].astype(jnp.float32)
     if backward:
         mine = (cols > col) & (row * inner + cols <= bound)
         row_bound = last_open(row * inner)
@@ -47,13 +55,22 @@
         carry = (row * inner + cols >= row_bound)
     local_sum = masked_sum(mine, in_row)
     row_part = masked_sum(carry, in_row)
-    across = lax.all_gather(row_part.astype(jnp.bfloat16), OUTER).astype(jnp.float32)
+    sent = row_part.astype(kind)
+    if extra is not None:
+        sent = jnp.concatenate([sent, row_extra.astype(kind)], -1)
+    across = lax.all_gather(sent, OUTER)
+    if extra is not None:
+        all_extra = jnp.moveaxis(across[..., width:], 0, -2)
+        all_extra = all_extra.reshape(all_extra.shape[:-2] + (-1,))
+    across = across[..., :width].astype(jnp.float32)
     bound_row = bound // inner
     if backward:
         take = (rows > row) & (rows <= bound_row)
     else:
         take = (rows < row) & (rows >= bound_row)
     far_sum = masked_sum(take, across)
+    if extra is not None:
+        return local_sum + far_sum, all_extra
     return local_sum + far_sum
 
 
@@ -101,8 +118,7 @@
 
 def local(queries, keys, values, feature_weight, norm_gain, doc_bounds, out_grad):
     head_groups = lax.all_to_all(feature_weight, "fsdp", split_axis=0, concat_axis=1, tiled=True)
-    weight_local = gathered_columns(head_groups)
-    head_count = weight_local.shape[0]
+    head_count = head_groups.shape[0]
     tokens_here = queries.shape[0]
     block_count = tokens_here // BLK
     block_shape = (block_count, BLK, head_count, HS)
@@ -137,7 +153,9 @@
         held = jnp.where(starts_here[position], zero_state, running)
         prefix_list.append(held)
         running = held + raw_updates[position]
-    entering = carried_in(running, last_open, False)
+    entering, weight_local = carried_in(
+        running, last_open, False, jnp.bfloat16, extra=head_groups
+    )
     raw_states = jnp.stack(prefix_list) + jnp.where(
         reach_left[:, None, None, None], entering[None], 0.0
     )
@@ -200,7 +218,7 @@
     for position in reversed(range(block_count)):
         suffix_list[position] = running
         running = jnp.where(starts_here[position], zero_state, running + state_grads[position])
-    leaving = carried_in(running, next_open, True)
+    leaving = carried_in(running, next_open, True, jnp.float32)
     suffix = jnp.stack(suffix_list) + jnp.where(
         reach_right[:, None, None, None], leaving[None], 0.0
     )

time: 203 us -> 188 us (0.926)
  the two profiles are of different devices: /device:TPU:1 before, /device:TPU:2 now
where the time goes in v8:
time: 188 us; the launch traced here: 187 us
  blocking collectives  40.3 us (21%)
  starting transfers between devices  39.7 us (21%)
  waiting for transfers between devices  36.8 us (20%)
  other arithmetic  22.3 us (12%)
  local copies, waits for them, and re-layouts  21.3 us (11%)
  between operations  20.2 us (11%)
  matrix products  6.07 us (3%)
    all_gather x1, blocking collectives, carried_in(): across = lax.all_gather(sent, OUTER)  27.1 us
    ppermute x6, starting transfers between devices, exchanged(): return lax.ppermute(x, (OUTER, INNER), [(i, i ^ bit) for i in range(count)])  22.2 us
    all_gather x1, waiting for transfers between devices, carried_in(): across = lax.all_gather(sent, OUTER)  16.5 us
    all_gather x1, blocking collectives, carried_in(): in_row = lax.all_gather(sent, INNER)  13.2 us
    all_to_all x1, starting transfers between devices, local(): lax.all_to_all(feature_weight, 'fsdp', split_axis=0, concat_axis=1, tiled...  10.3 us
    unnamed x48, local copies, waits for them, and re-layouts  9.98 us
    all_to_all x1, waiting for transfers between devices, local(): lax.all_to_all(weight_columns, 'fsdp', split_axis=1, concat_axis=0, tiled...  7.61 us
    all_to_all x1, starting transfers between devices, local(): lax.all_to_all(weight_columns, 'fsdp', split_axis=1, concat_axis=0, tiled...  7.08 us
  transfers between devices with their start and end apart: 10, of which 5 were waited for; matrix products, arithmetic and copies ran while one was open for 16% of the time, Pallas kernels for 0%

profile of v8, /device:TPU:2, one launch (start us, length us, event | category | flops | bytes accessed | tf_op | source)
XLA Modules:
  0.0 186.7 jit_solution(474595400535619929)
XLA Ops:
  7.2 10.3 %all-to-all-start = ((bf16[16,16,2]{1,2,0:T(2,128)(2,1)}), bf16[16,16,2]{1,2,0:T(2,128)(2,1)S(1)}, u32[]{:S(2)}, u32[]{:S(2)}) async-start(bf16[16,16,2]{1,2,0:T(2,128)(2,1)} %param.10), calls=%async_computation | async-start | bytes 16384 | tf_op jit(solution)/shard_map/all_to_all | solution.py:120
  27.2 2.0 %fusion.51 = (bf16[2,128,128]{1,2,0:T(8,128)(2,1)S(1)}, f32[1,2,128,128]{2,3,1,0:T(8,128)S(1)}, f32[1,2,128,128]{2,3,1,0:T(8,128)S(1)}, f32[1,2,128,128]{2,3,1,0:T(8,128)S(1)}) fusion(f32[4,2,128,128]{2,3,1,0:T(8,128)S(1)} %fusion.32, pred[]{:T(512)} %bitcast.3, pred[]{:T(512)} %bitcast.2, pred[]{:T(512)} %bitcast.1), kind=kLoop, calls=%fused_computation.93 | loop fusion | flops 229376 | bytes 983043 | tf_op jit(solution)/shard_map/convert_element_type | solution.py:40
  31.5 13.2 %all-gather = bf16[16,128,130]{1,2,0:T(8,128)(2,1)S(1)} all-gather(bf16[2,128,130]{1,2,0:T(8,128)(2,1)S(1)} %pad_maximum_fusion.2), channel_id=2, replica_groups=mesh['seq_row'=8,'seq_col'=8,'fsdp'=8] {'seq_col'}, dimensions={0}, use_global_device_ids=true | all-gather | bytes 599040 | tf_op jit(solution)/shard_map/all_gather | solution.py:43
  44.8 1.5 fusion.17
  46.4 27.1 %all-gather.1 = bf16[16,128,144]{1,2,0:T(8,128)(2,1)S(1)} all-gather(bf16[2,128,144]{1,2,0:T(8,128)(2,1)S(1)} %copy.313), channel_id=3, replica_groups=mesh['seq_row'=8,'seq_col'=8,'fsdp'=8] {'seq_row'}, dimensions={0}, use_global_device_ids=true | all-gather | bytes 663552 | tf_op jit(solution)/shard_map/all_gather | solution.py:61
  80.1 6.3 %collective-permute-start = (f32[2,128,65]{1,2,0:T(8,128)S(1)}, f32[2,128,65]{1,2,0:T(8,128)S(1)}, u32[]{:S(2)}, u32[]{:S(2)}) collective-permute-start(f32[2,128,65]{1,2,0:T(8,128)S(1)} %pad_maximum_fusion.1), channel_id=1, source_target_pairs={{0,256},{8,264},{16,272},{24,280},{32,288},{40,296},{48,304},{56,3... | collective-permute-start | bytes 199688 | tf_op jit(solution)/shard_map/ppermute | solution.py:79
  86.9 3.5 %collective-permute-done = f32[2,128,65]{1,2,0:T(8,128)S(1)} collective-permute-done((f32[2,128,65]{1,2,0:T(8,128)S(1)}, f32[2,128,65]{1,2,0:T(8,128)S(1)}, u32[]{:S(2)}, u32[]{:S(2)}) %collective-permute-start) | collective-permute-done | bytes 66592 | tf_op jit(solution)/shard_map/ppermute | solution.py:79
  91.1 5.0 %collective-permute-start.1 = (f32[2,128,33]{1,0,2:T(2,128)S(1)}, f32[2,128,33]{1,0,2:T(2,128)S(1)}, u32[]{:S(2)}, u32[]{:S(2)}) collective-permute-start(f32[2,128,33]{1,0,2:T(2,128)S(1)} %pad_maximum_fusion.3), channel_id=1, source_target_pairs={{0,128},{8,136},{16,144},{24,152},{32,160},{40,168},{48,176},{56,1... | collective-permute-start | bytes 101384 | tf_op jit(solution)/shard_map/ppermute | solution.py:79
  96.1 3.3 %add_select_fusion = (f32[1,2,128,128]{2,3,1,0:T(8,128)S(1)}, f32[1,2,128,128]{2,3,1,0:T(8,128)}, f32[1,2,128,128]{2,3,1,0:T(8,128)}) fusion(f32[1,2,128,128]{2,3,1,0:T(8,128)S(1)} %copy.414, pred[]{:T(512)} %bitcast.31, f32[1,2,128,128]{2,3,1,0:T(8,128)S(1)} %copy.413, pred[]{:T(512)} %bitcast.1, f32[1,2,128,128]{2,3,1,0:T(8,128)S(1)} %copy.412, ...), kind=kLoop, calls=%fused_computation.87 | loop fusion | flops 229376 | bytes 917508 | tf_op jit(solution)/shard_map/jit(_where)/select_n | solution.py:220
  100.3 1.9 %collective-permute-start.2 = (f32[2,128,17]{1,0,2:T(2,128)S(1)}, f32[2,128,17]{1,0,2:T(2,128)S(1)}, u32[]{:S(2)}, u32[]{:S(2)}) collective-permute-start(f32[2,128,17]{1,0,2:T(2,128)S(1)} %pad_maximum_fusion.4), channel_id=1, source_target_pairs={{0,64},{8,72},{16,80},{24,88},{32,96},{40,104},{48,112},{56,120},{... | collective-permute-start | bytes 52232 | tf_op jit(solution)/shard_map/ppermute | solution.py:79
  102.3 1.8 compare_and_fusion.1
  106.9 4.0 %collective-permute-start.3 = (f32[2,128,9]{1,0,2:T(2,128)S(1)}, f32[2,128,9]{1,0,2:T(2,128)S(1)}, u32[]{:S(2)}, u32[]{:S(2)}) collective-permute-start(f32[2,128,9]{1,0,2:T(2,128)S(1)} %pad_maximum_fusion.5), channel_id=1, source_target_pairs={{0,32},{8,40},{16,48},{24,56},{32,0},{40,8},{48,16},{56,24},{64,96... | collective-permute-start | bytes 27656 | tf_op jit(solution)/shard_map/ppermute | solution.py:79
  111.5 2.5 %collective-permute-done.3 = f32[2,128,9]{1,0,2:T(2,128)S(1)} collective-permute-done((f32[2,128,9]{1,0,2:T(2,128)S(1)}, f32[2,128,9]{1,0,2:T(2,128)S(1)}, u32[]{:S(2)}, u32[]{:S(2)}) %collective-permute-start.3) | collective-permute-done | bytes 9248 | tf_op jit(solution)/shard_map/ppermute | solution.py:79
  115.2 2.9 %collective-permute-start.4 = (f32[2,128,5]{1,0,2:T(2,128)}, f32[2,128,5]{1,0,2:T(2,128)}, u32[]{:S(2)}, u32[]{:S(2)}) collective-permute-start(f32[2,128,5]{1,0,2:T(2,128)} %pad_maximum_fusion.6), channel_id=1, source_target_pairs={{0,16},{8,24},{16,0},{24,8},{32,48},{40,56},{48,32},{56,40},{64,80... | collective-permute-start | bytes 15368 | tf_op jit(solution)/shard_map/ppermute | solution.py:79
  118.1 6.7 %all-gather.6.cloned.1.call-done = f32[8,2,128,128]{3,2,1,0:T(8,128)} async-done(((f32[1,2,128,128]{3,2,1,0:T(8,128)}), f32[8,2,128,128]{3,2,1,0:T(8,128)}) %all-gather.6.cloned.1.call-update) | async-done | bytes 1048592 | tf_op jit(solution)/shard_map/all_gather | solution.py:43
  124.8 1.8 copy.347
  127.2 2.3 %select_reduce_fusion.1 = (f32[2,128,128]{1,0,2:T(2,128)}, f32[2,128,128]{1,0,2:T(2,128)S(1)}) fusion(f32[8,2,128,128]{2,1,0,3:T(2,128)S(1)} %copy.347, pred[8]{0:T(512)(128)(4,1)S(1)} %copy-done.15, pred[8]{0:T(512)(128)(4,1)S(1)} %copy-done.14), kind=kLoop, calls=%fused_computation.37 | loop fusion | flops 983040 | bytes 1310736 | tf_op jit(solution)/shard_map/reduce_sum | solution.py:26
  129.5 1.6 copy.349
  133.2 2.1 %collective-permute-start.5 = (f32[2,128,3]{1,0,2:T(2,128)S(1)}, f32[2,128,3]{1,0,2:T(2,128)S(1)}, u32[]{:S(2)}, u32[]{:S(2)}) collective-permute-start(f32[2,128,3]{1,0,2:T(2,128)S(1)} %pad_maximum_fusion.7), channel_id=1, source_target_pairs={{0,8},{8,0},{16,24},{24,16},{32,40},{40,32},{48,56},{56,48},{64,72... | collective-permute-start | bytes 9224 | tf_op jit(solution)/shard_map/ppermute | solution.py:79
  135.4 1.3 add_select_fusion.1
  139.4 7.1 %all-to-all-start.1 = ((f32[2,128,2]{0,2,1:T(2,128)}), f32[2,128,2]{0,2,1:T(2,128)S(1)}, u32[]{:S(2)}, u32[]{:S(2)}) async-start(f32[2,128,2]{0,2,1:T(2,128)} %copy.373), calls=%async_computation.1 | async-start | bytes 262144 | tf_op jit(solution)/shard_map/all_to_all | solution.py:214
  148.3 7.6 %all-to-all-done.1 = f32[2,128,2]{0,2,1:T(2,128)S(1)} async-done(((f32[2,128,2]{0,2,1:T(2,128)}), f32[2,128,2]{0,2,1:T(2,128)S(1)}, u32[]{:S(2)}, u32[]{:S(2)}) %all-to-all-start.1) | async-done | bytes 2080 | tf_op jit(solution)/shard_map/all_to_all | solution.py:214
  156.8 16.5 %all-gather.8.cloned.1.call-done = f32[16,128,128]{2,1,0:T(8,128)} async-done(((f32[2,128,128]{2,1,0:T(8,128)}), f32[16,128,128]{2,1,0:T(8,128)}) %all-gather.8.cloned.1.call-update) | async-done | bytes 1048592 | tf_op jit(solution)/shard_map/all_gather | solution.py:61
  173.3 1.8 copy.350
  (154 shorter events, 32.3 us)
Async XLA Ops:
  7.2 24.2 %all-to-all-start = ((bf16[16,16,2]{1,2,0:T(2,128)(2,1)}), bf16[16,16,2]{1,2,0:T(2,128)(2,1)S(1)}, u32[]{:S(2)}, u32[]{:S(2)}) async-start(bf16[16,16,2]{1,2,0:T(2,128)(2,1)} %param.10), calls=%async_computation | async-start | bytes 16384 | tf_op jit(solution)/shard_map/all_to_all | solution.py:120
  17.5 107.3 %all-gather.6.cloned.1.call-start = ((), (), s32[]{:S(2)}) async-start(), calls=%async_computation.2 | async-start | bytes 1179648 | tf_op jit(solution)/shard_map/all_gather | solution.py:43
  17.5 0.7 copy-start.18
  25.7 1.1 copy-start.2
  27.1 2.8 %copy-start.3 = (bf16[512,256]{1,0:T(8,128)(2,1)S(1)}, bf16[512,256]{1,0:T(8,128)(2,1)}, u32[]{:S(2)}) copy-start(bf16[512,256]{1,0:T(8,128)(2,1)} %param.7) | copy-start | bytes 786436
  29.2 46.5 %copy-start.5 = (f32[1,2,128,128]{2,3,1,0:T(8,128)}, f32[1,2,128,128]{2,3,1,0:T(8,128)S(1)}, u32[]{:S(2)}) copy-start(f32[1,2,128,128]{2,3,1,0:T(8,128)S(1)} %get-tuple-element.22) | copy-start | bytes 393220
  29.2 0.7 copy-start.19
  29.9 1.0 copy-start.1
  75.7 2.7 %copy-start.7 = (f32[1,2,128,128]{2,3,1,0:T(8,128)}, f32[1,2,128,128]{2,3,1,0:T(8,128)S(1)}, u32[]{:S(2)}) copy-start(f32[1,2,128,128]{2,3,1,0:T(8,128)S(1)} %stack.6) | copy-start | bytes 393220
  78.1 0.9 copy-start.6
  80.1 10.3 %collective-permute-start = (f32[2,128,65]{1,2,0:T(8,128)S(1)}, f32[2,128,65]{1,2,0:T(8,128)S(1)}, u32[]{:S(2)}, u32[]{:S(2)}) collective-permute-start(f32[2,128,65]{1,2,0:T(8,128)S(1)} %pad_maximum_fusion.1), channel_id=1, source_target_pairs={{0,256},{8,264},{16,272},{24,280},{32,288},{40,296},{48,304},{56,3... | collective-permute-start | bytes 199688 | tf_op jit(solution)/shard_map/ppermute | solution.py:79
  91.1 9.1 %collective-permute-start.1 = (f32[2,128,33]{1,0,2:T(2,128)S(1)}, f32[2,128,33]{1,0,2:T(2,128)S(1)}, u32[]{:S(2)}, u32[]{:S(2)}) collective-permute-start(f32[2,128,33]{1,0,2:T(2,128)S(1)} %pad_maximum_fusion.3), channel_id=1, source_target_pairs={{0,128},{8,136},{16,144},{24,152},{32,160},{40,168},{48,176},{56,1... | collective-permute-start | bytes 101384 | tf_op jit(solution)/shard_map/ppermute | solution.py:79
  100.2 73.1 %all-gather.8.cloned.1.call-start = ((), (), s32[]{:S(2)}) async-start(), calls=%async_computation.3 | async-start | bytes 1179648 | tf_op jit(solution)/shard_map/all_gather | solution.py:61
  100.3 6.5 %collective-permute-start.2 = (f32[2,128,17]{1,0,2:T(2,128)S(1)}, f32[2,128,17]{1,0,2:T(2,128)S(1)}, u32[]{:S(2)}, u32[]{:S(2)}) collective-permute-start(f32[2,128,17]{1,0,2:T(2,128)S(1)} %pad_maximum_fusion.4), channel_id=1, source_target_pairs={{0,64},{8,72},{16,80},{24,88},{32,96},{40,104},{48,112},{56,120},{... | collective-permute-start | bytes 52232 | tf_op jit(solution)/shard_map/ppermute | solution.py:79
  106.9 7.1 %collective-permute-start.3 = (f32[2,128,9]{1,0,2:T(2,128)S(1)}, f32[2,128,9]{1,0,2:T(2,128)S(1)}, u32[]{:S(2)}, u32[]{:S(2)}) collective-permute-start(f32[2,128,9]{1,0,2:T(2,128)S(1)} %pad_maximum_fusion.5), channel_id=1, source_target_pairs={{0,32},{8,40},{16,48},{24,56},{32,0},{40,8},{48,16},{56,24},{64,96... | collective-permute-start | bytes 27656 | tf_op jit(solution)/shard_map/ppermute | solution.py:79
  115.2 16.3 %collective-permute-start.4 = (f32[2,128,5]{1,0,2:T(2,128)}, f32[2,128,5]{1,0,2:T(2,128)}, u32[]{:S(2)}, u32[]{:S(2)}) collective-permute-start(f32[2,128,5]{1,0,2:T(2,128)} %pad_maximum_fusion.6), channel_id=1, source_target_pairs={{0,16},{8,24},{16,0},{24,8},{32,48},{40,56},{48,32},{56,40},{64,80... | collective-permute-start | bytes 15368 | tf_op jit(solution)/shard_map/ppermute | solution.py:79
  131.2 4.2 %copy-start = (f32[1,2,128,128]{2,3,1,0:T(8,128)S(1)}, f32[1,2,128,128]{2,3,1,0:T(8,128)}, u32[]{:S(2)}) copy-start(f32[1,2,128,128]{2,3,1,0:T(8,128)} %get-tuple-element.17) | copy-start | bytes 393220
  133.2 5.3 %collective-permute-start.5 = (f32[2,128,3]{1,0,2:T(2,128)S(1)}, f32[2,128,3]{1,0,2:T(2,128)S(1)}, u32[]{:S(2)}, u32[]{:S(2)}) collective-permute-start(f32[2,128,3]{1,0,2:T(2,128)S(1)} %pad_maximum_fusion.7), channel_id=1, source_target_pairs={{0,8},{8,0},{16,24},{24,16},{32,40},{40,32},{48,56},{56,48},{64,72... | collective-permute-start | bytes 9224 | tf_op jit(solution)/shard_map/ppermute | solution.py:79
  139.4 16.6 %all-to-all-start.1 = ((f32[2,128,2]{0,2,1:T(2,128)}), f32[2,128,2]{0,2,1:T(2,128)S(1)}, u32[]{:S(2)}, u32[]{:S(2)}) async-start(f32[2,128,2]{0,2,1:T(2,128)} %copy.373), calls=%async_computation.1 | async-start | bytes 262144 | tf_op jit(solution)/shard_map/all_to_all | solution.py:214
  173.3 1.8 copy-start.16
  175.7 0.9 copy-start.9
  175.8 0.9 copy-start.4
  175.8 1.0 copy-start.8
  175.8 0.9 copy-start.17
  (6 other events, 3.8 us)
Sparse Core Ops, SparseCore 0:
  100.3 24.4 all-gather.5
  131.3 41.9 all-gather.7

commit v9 on v8

--- a/solution.py
+++ b/solution.py
@@ -26,7 +26,7 @@
     return jnp.sum(jnp.where(mask[:, None, None, None], stacked, 0.0), 0)
 
 
-def carried_in(aggregate, last_open, backward, kind, extra=None):
+def carried_in(aggregate, last_open, backward, kind, far_kind, extra=None):
     inner = lax.axis_size(INNER)
     outer = lax.axis_size(OUTER)
     col = lax.axis_index(INNER)
@@ -55,9 +55,9 @@
         carry = (row * inner + cols >= row_bound)
     local_sum = masked_sum(mine, in_row)
     row_part = masked_sum(carry, in_row)
-    sent = row_part.astype(kind)
-    if extra is not None:
-        sent = jnp.concatenate([sent, row_extra.astype(kind)], -1)
+    sent = row_part.astype(far_kind)
+    if extra is not None:
+        sent = jnp.concatenate([sent, row_extra.astype(far_kind)], -1)
     across = lax.all_gather(sent, OUTER)
     if extra is not None:
         all_extra = jnp.moveaxis(across[..., width:], 0, -2)
@@ -154,7 +154,7 @@
         prefix_list.append(held)
         running = held + raw_updates[position]
     entering, weight_local = carried_in(
-        running, last_open, False, jnp.bfloat16, extra=head_groups
+        running, last_open, False, jnp.bfloat16, jnp.bfloat16, extra=head_groups
     )
     raw_states = jnp.stack(prefix_list) + jnp.where(
         reach_left[:, None, None, None], entering[None], 0.0
@@ -218,7 +218,7 @@
     for position in reversed(range(block_count)):
         suffix_list[position] = running
         running = jnp.where(starts_here[position], zero_state, running + state_grads[position])
-    leaving = carried_in(running, next_open, True, jnp.float32)
+    leaving = carried_in(running, next_open, True, jnp.bfloat16, jnp.float32)
     suffix = jnp.stack(suffix_list) + jnp.where(
         reach_right[:, None, None, None], leaving[None], 0.0
     )

time: 188 us -> 178 us (0.947)
  blocking collectives: 40.3 us -> 53.4 us
  waiting for transfers between devices: 36.8 us -> 24.5 us
  local copies, waits for them, and re-layouts: 21.3 us -> 15.8 us
  other arithmetic: 22.3 us -> 17.2 us
    all_gather x1 -> x2, blocking collectives: 13.2 us -> 26.3 us  [carried_in(): in_row = lax.all_gather(sent, INNER)]
    all_gather x1, waiting for transfers between devices: 16.5 us -> 8.68 us  [carried_in(): across = lax.all_gather(sent, OUTER)]
    all_gather x1 -> x0, waiting for transfers between devices: 6.69 us -> none  [carried_in(): in_row = lax.all_gather(sent, INNER)]
    select_n x2 -> x1, other arithmetic: 4.64 us -> 1.32 us  [local(): jnp.where(starts_here[position], zero_state, running + state_grads[positi...]
    convert_element_type x1 -> x2, other arithmetic: 2.02 us -> 5.34 us  [carried_in(): sent = aggregate.astype(kind)]
    unnamed x48 -> x34, local copies, waits for them, and re-layouts: 9.98 us -> 7.25 us
  transfers between devices with their start and end apart: 10 -> 9, of which waited for: 5 -> 5; matrix products, arithmetic and copies ran while one was open for 16% -> 12% of each run, Pallas kernels for 0% -> 0%
where the time goes in v9:
time: 178 us; the launch traced here: 177 us
  blocking collectives  53.4 us (30%)
  starting transfers between devices  39.9 us (22%)
  waiting for transfers between devices  24.5 us (14%)
  between operations  19.9 us (11%)
  other arithmetic  17.2 us (10%)
  local copies, waits for them, and re-layouts  15.8 us (9%)
  matrix products  6.05 us (3%)
    all_gather x1, blocking collectives, carried_in(): across = lax.all_gather(sent, OUTER)  27.1 us
    all_gather x2, blocking collectives, carried_in(): in_row = lax.all_gather(sent, INNER)  26.3 us
    ppermute x6, starting transfers between devices, exchanged(): return lax.ppermute(x, (OUTER, INNER), [(i, i ^ bit) for i in range(count)])  22.4 us
    all_to_all x1, starting transfers between devices, local(): lax.all_to_all(feature_weight, 'fsdp', split_axis=0, concat_axis=1, tiled...  10.3 us
    all_to_all x1, waiting for transfers between devices, local(): lax.all_to_all(weight_columns, 'fsdp', split_axis=1, concat_axis=0, tiled...  9.16 us
    all_gather x1, waiting for transfers between devices, carried_in(): across = lax.all_gather(sent, OUTER)  8.68 us
    unnamed x34, local copies, waits for them, and re-layouts  7.25 us
    all_to_all x1, starting transfers between devices, local(): lax.all_to_all(weight_columns, 'fsdp', split_axis=1, concat_axis=0, tiled...  7.16 us
  transfers between devices with their start and end apart: 9, of which 5 were waited for; matrix products, arithmetic and copies ran while one was open for 12% of the time, Pallas kernels for 0%

profile of v9, /device:TPU:2, one launch (start us, length us, event | category | flops | bytes accessed | tf_op | source)
XLA Modules:
  0.0 176.8 jit_solution(14341490272746955956)
XLA Ops:
  7.2 10.3 %all-to-all-start = ((bf16[16,16,2]{1,2,0:T(2,128)(2,1)}), bf16[16,16,2]{1,2,0:T(2,128)(2,1)S(1)}, u32[]{:S(2)}, u32[]{:S(2)}) async-start(bf16[16,16,2]{1,2,0:T(2,128)(2,1)} %param.10), calls=%async_computation | async-start | bytes 16384 | tf_op jit(solution)/shard_map/all_to_all | solution.py:120
  26.3 1.3 compare_and_fusion.1
  27.7 1.2 compare_and_fusion.3
  28.9 1.1 reshape.154
  30.3 2.0 %fusion.53 = (bf16[2,128,128]{1,2,0:T(8,128)(2,1)S(1)}, f32[1,2,128,128]{2,3,1,0:T(8,128)S(1)}, f32[1,2,128,128]{2,3,1,0:T(8,128)S(1)}, f32[1,2,128,128]{2,3,1,0:T(8,128)S(1)}) fusion(f32[4,2,128,128]{2,3,1,0:T(8,128)S(1)} %fusion.34, pred[]{:T(512)} %bitcast.3, pred[]{:T(512)} %bitcast.2, pred[]{:T(512)} %bitcast.1), kind=kLoop, calls=%fused_computation.95 | loop fusion | flops 229376 | bytes 983043 | tf_op jit(solution)/shard_map/convert_element_type | solution.py:40
  34.6 13.2 %all-gather = bf16[16,128,130]{1,2,0:T(8,128)(2,1)S(1)} all-gather(bf16[2,128,130]{1,2,0:T(8,128)(2,1)S(1)} %pad_maximum_fusion.2), channel_id=2, replica_groups=mesh['seq_row'=8,'seq_col'=8,'fsdp'=8] {'seq_col'}, dimensions={0}, use_global_device_ids=true | all-gather | bytes 599040 | tf_op jit(solution)/shard_map/all_gather | solution.py:43
  47.9 1.6 fusion.17
  49.7 27.1 %all-gather.1 = bf16[16,128,144]{1,2,0:T(8,128)(2,1)S(1)} all-gather(bf16[2,128,144]{1,2,0:T(8,128)(2,1)S(1)} %copy.310), channel_id=3, replica_groups=mesh['seq_row'=8,'seq_col'=8,'fsdp'=8] {'seq_row'}, dimensions={0}, use_global_device_ids=true | all-gather | bytes 663552 | tf_op jit(solution)/shard_map/all_gather | solution.py:61
  83.3 6.3 %collective-permute-start = (f32[2,128,65]{1,2,0:T(8,128)S(1)}, f32[2,128,65]{1,2,0:T(8,128)S(1)}, u32[]{:S(2)}, u32[]{:S(2)}) collective-permute-start(f32[2,128,65]{1,2,0:T(8,128)S(1)} %pad_maximum_fusion.1), channel_id=1, source_target_pairs={{0,256},{8,264},{16,272},{24,280},{32,288},{40,296},{48,304},{56,3... | collective-permute-start | bytes 199688 | tf_op jit(solution)/shard_map/ppermute | solution.py:79
  90.1 3.5 %collective-permute-done = f32[2,128,65]{1,2,0:T(8,128)S(1)} collective-permute-done((f32[2,128,65]{1,2,0:T(8,128)S(1)}, f32[2,128,65]{1,2,0:T(8,128)S(1)}, u32[]{:S(2)}, u32[]{:S(2)}) %collective-permute-start) | collective-permute-done | bytes 66592 | tf_op jit(solution)/shard_map/ppermute | solution.py:79
  93.8 5.2 %collective-permute-start.1 = (f32[2,128,33]{1,0,2:T(2,128)S(1)}, f32[2,128,33]{1,0,2:T(2,128)S(1)}, u32[]{:S(2)}, u32[]{:S(2)}) collective-permute-start(f32[2,128,33]{1,0,2:T(2,128)S(1)} %pad_maximum_fusion.3), channel_id=1, source_target_pairs={{0,128},{8,136},{16,144},{24,152},{32,160},{40,168},{48,176},{56,1... | collective-permute-start | bytes 101384 | tf_op jit(solution)/shard_map/ppermute | solution.py:79
  99.0 3.3 %select_convert_fusion = (bf16[1,2,128,128]{2,3,1,0:T(8,128)(2,1)S(1)}, f32[1,2,128,128]{2,3,1,0:T(8,128)}, f32[1,2,128,128]{2,3,1,0:T(8,128)}) fusion(f32[1,2,128,128]{2,3,1,0:T(8,128)S(1)} %copy.410, pred[]{:T(512)} %bitcast.31, f32[1,2,128,128]{2,3,1,0:T(8,128)S(1)} %copy.409, pred[]{:T(512)} %bitcast.1, f32[1,2,128,128]{2,3,1,0:T(8,128)S(1)} %copy.408, ...), kind=kLoop, calls=%fused_computation.89 | loop fusion | flops 262144 | bytes 851972 | tf_op jit(solution)/shard_map/convert_element_type | solution.py:40
  102.6 1.9 %collective-permute-start.2 = (f32[2,128,17]{1,0,2:T(2,128)S(1)}, f32[2,128,17]{1,0,2:T(2,128)S(1)}, u32[]{:S(2)}, u32[]{:S(2)}) collective-permute-start(f32[2,128,17]{1,0,2:T(2,128)S(1)} %pad_maximum_fusion.4), channel_id=1, source_target_pairs={{0,64},{8,72},{16,80},{24,88},{32,96},{40,104},{48,112},{56,120},{... | collective-permute-start | bytes 52232 | tf_op jit(solution)/shard_map/ppermute | solution.py:79
  104.5 13.1 %all_gather.26 = bf16[8,2,128,128]{3,2,1,0:T(8,128)(2,1)S(1)} all-gather(bf16[1,2,128,128]{3,2,1,0:T(8,128)(2,1)S(1)} %copy.343), channel_id=1, replica_groups=mesh['seq_row'=8,'seq_col'=8,'fsdp'=8] {'seq_col'}, dimensions={0}, use_global_device_ids=true | all-gather | bytes 589824 | tf_op jit(solution)/shard_map/all_gather | solution.py:43
  118.2 4.2 %collective-permute-start.3 = (f32[2,128,9]{1,0,2:T(2,128)S(1)}, f32[2,128,9]{1,0,2:T(2,128)S(1)}, u32[]{:S(2)}, u32[]{:S(2)}) collective-permute-start(f32[2,128,9]{1,0,2:T(2,128)S(1)} %pad_maximum_fusion.5), channel_id=1, source_target_pairs={{0,32},{8,40},{16,48},{24,56},{32,0},{40,8},{48,16},{56,24},{64,96... | collective-permute-start | bytes 27656 | tf_op jit(solution)/shard_map/ppermute | solution.py:79
  122.3 1.5 fusion.20
  125.3 2.9 %collective-permute-start.4 = (f32[2,128,5]{1,0,2:T(2,128)S(1)}, f32[2,128,5]{1,0,2:T(2,128)S(1)}, u32[]{:S(2)}, u32[]{:S(2)}) collective-permute-start(f32[2,128,5]{1,0,2:T(2,128)S(1)} %pad_maximum_fusion.6), channel_id=1, source_target_pairs={{0,16},{8,24},{16,0},{24,8},{32,48},{40,56},{48,32},{56,40},{64,80... | collective-permute-start | bytes 15368 | tf_op jit(solution)/shard_map/ppermute | solution.py:79
  128.5 2.5 %collective-permute-done.4 = f32[2,128,5]{1,0,2:T(2,128)S(1)} collective-permute-done((f32[2,128,5]{1,0,2:T(2,128)S(1)}, f32[2,128,5]{1,0,2:T(2,128)S(1)}, u32[]{:S(2)}, u32[]{:S(2)}) %collective-permute-start.4) | collective-permute-done | bytes 5152 | tf_op jit(solution)/shard_map/ppermute | solution.py:79
  131.0 1.9 %collective-permute-start.5 = (f32[2,128,3]{1,0,2:T(2,128)S(1)}, f32[2,128,3]{1,0,2:T(2,128)S(1)}, u32[]{:S(2)}, u32[]{:S(2)}) collective-permute-start(f32[2,128,3]{1,0,2:T(2,128)S(1)} %pad_maximum_fusion.7), channel_id=1, source_target_pairs={{0,8},{8,0},{16,24},{24,16},{32,40},{40,32},{48,56},{56,48},{64,72... | collective-permute-start | bytes 9224 | tf_op jit(solution)/shard_map/ppermute | solution.py:79
  132.9 1.3 add_select_fusion
  136.9 7.2 %all-to-all-start.1 = ((f32[2,128,2]{0,2,1:T(2,128)}), f32[2,128,2]{0,2,1:T(2,128)S(1)}, u32[]{:S(2)}, u32[]{:S(2)}) async-start(f32[2,128,2]{0,2,1:T(2,128)} %copy.369), calls=%async_computation.1 | async-start | bytes 262144 | tf_op jit(solution)/shard_map/all_to_all | solution.py:214
  144.6 9.2 %all-to-all-done.1 = f32[2,128,2]{0,2,1:T(2,128)S(1)} async-done(((f32[2,128,2]{0,2,1:T(2,128)}), f32[2,128,2]{0,2,1:T(2,128)S(1)}, u32[]{:S(2)}, u32[]{:S(2)}) %all-to-all-start.1) | async-done | bytes 2080 | tf_op jit(solution)/shard_map/all_to_all | solution.py:214
  154.6 8.7 %all-gather.5.cloned.1.call-done = f32[16,128,128]{2,1,0:T(8,128)} async-done(((f32[2,128,128]{2,1,0:T(8,128)}), f32[16,128,128]{2,1,0:T(8,128)}) %all-gather.5.cloned.1.call-update) | async-done | bytes 1048592 | tf_op jit(solution)/shard_map/all_gather | solution.py:61
  163.3 1.8 copy.346
  (138 shorter events, 24.6 us)
Async XLA Ops:
  7.2 27.3 %all-to-all-start = ((bf16[16,16,2]{1,2,0:T(2,128)(2,1)}), bf16[16,16,2]{1,2,0:T(2,128)(2,1)S(1)}, u32[]{:S(2)}, u32[]{:S(2)}) async-start(bf16[16,16,2]{1,2,0:T(2,128)(2,1)} %param.10), calls=%async_computation | async-start | bytes 16384 | tf_op jit(solution)/shard_map/all_to_all | solution.py:120
  17.5 145.8 %all-gather.5.cloned.1.call-start = ((), (), s32[]{:S(2)}) async-start(), calls=%async_computation.2 | async-start | bytes 1179648 | tf_op jit(solution)/shard_map/all_gather | solution.py:61
  17.5 0.7 copy-start.11
  28.9 1.1 copy-start.3
  30.3 2.8 %copy-start.4 = (bf16[512,256]{1,0:T(8,128)(2,1)S(1)}, bf16[512,256]{1,0:T(8,128)(2,1)}, u32[]{:S(2)}) copy-start(bf16[512,256]{1,0:T(8,128)(2,1)} %param.7) | copy-start | bytes 786436
  32.4 46.5 %copy-start.5 = (f32[1,2,128,128]{2,3,1,0:T(8,128)}, f32[1,2,128,128]{2,3,1,0:T(8,128)S(1)}, u32[]{:S(2)}) copy-start(f32[1,2,128,128]{2,3,1,0:T(8,128)S(1)} %get-tuple-element.22) | copy-start | bytes 393220
  32.4 0.7 copy-start.12
  33.1 1.0 copy-start.2
  78.9 2.7 %copy-start.7 = (f32[1,2,128,128]{2,3,1,0:T(8,128)}, f32[1,2,128,128]{2,3,1,0:T(8,128)S(1)}, u32[]{:S(2)}) copy-start(f32[1,2,128,128]{2,3,1,0:T(8,128)S(1)} %stack.6) | copy-start | bytes 393220
  81.4 0.9 copy-start.6
  83.3 10.3 %collective-permute-start = (f32[2,128,65]{1,2,0:T(8,128)S(1)}, f32[2,128,65]{1,2,0:T(8,128)S(1)}, u32[]{:S(2)}, u32[]{:S(2)}) collective-permute-start(f32[2,128,65]{1,2,0:T(8,128)S(1)} %pad_maximum_fusion.1), channel_id=1, source_target_pairs={{0,256},{8,264},{16,272},{24,280},{32,288},{40,296},{48,304},{56,3... | collective-permute-start | bytes 199688 | tf_op jit(solution)/shard_map/ppermute | solution.py:79
  93.8 8.7 %collective-permute-start.1 = (f32[2,128,33]{1,0,2:T(2,128)S(1)}, f32[2,128,33]{1,0,2:T(2,128)S(1)}, u32[]{:S(2)}, u32[]{:S(2)}) collective-permute-start(f32[2,128,33]{1,0,2:T(2,128)S(1)} %pad_maximum_fusion.3), channel_id=1, source_target_pairs={{0,128},{8,136},{16,144},{24,152},{32,160},{40,168},{48,176},{56,1... | collective-permute-start | bytes 101384 | tf_op jit(solution)/shard_map/ppermute | solution.py:79
  102.6 15.5 %collective-permute-start.2 = (f32[2,128,17]{1,0,2:T(2,128)S(1)}, f32[2,128,17]{1,0,2:T(2,128)S(1)}, u32[]{:S(2)}, u32[]{:S(2)}) collective-permute-start(f32[2,128,17]{1,0,2:T(2,128)S(1)} %pad_maximum_fusion.4), channel_id=1, source_target_pairs={{0,64},{8,72},{16,80},{24,88},{32,96},{40,104},{48,112},{56,120},{... | collective-permute-start | bytes 52232 | tf_op jit(solution)/shard_map/ppermute | solution.py:79
  118.2 7.1 %collective-permute-start.3 = (f32[2,128,9]{1,0,2:T(2,128)S(1)}, f32[2,128,9]{1,0,2:T(2,128)S(1)}, u32[]{:S(2)}, u32[]{:S(2)}) collective-permute-start(f32[2,128,9]{1,0,2:T(2,128)S(1)} %pad_maximum_fusion.5), channel_id=1, source_target_pairs={{0,32},{8,40},{16,48},{24,56},{32,0},{40,8},{48,16},{56,24},{64,96... | collective-permute-start | bytes 27656 | tf_op jit(solution)/shard_map/ppermute | solution.py:79
  125.3 7.6 %copy-start = (f32[1,2,128,128]{2,3,1,0:T(8,128)S(1)}, f32[1,2,128,128]{2,3,1,0:T(8,128)}, u32[]{:S(2)}) copy-start(f32[1,2,128,128]{2,3,1,0:T(8,128)} %get-tuple-element.17) | copy-start | bytes 393220
  125.3 5.6 %collective-permute-start.4 = (f32[2,128,5]{1,0,2:T(2,128)S(1)}, f32[2,128,5]{1,0,2:T(2,128)S(1)}, u32[]{:S(2)}, u32[]{:S(2)}) collective-permute-start(f32[2,128,5]{1,0,2:T(2,128)S(1)} %pad_maximum_fusion.6), channel_id=1, source_target_pairs={{0,16},{8,24},{16,0},{24,8},{32,48},{40,56},{48,32},{56,40},{64,80... | collective-permute-start | bytes 15368 | tf_op jit(solution)/shard_map/ppermute | solution.py:79
  131.0 5.1 %collective-permute-start.5 = (f32[2,128,3]{1,0,2:T(2,128)S(1)}, f32[2,128,3]{1,0,2:T(2,128)S(1)}, u32[]{:S(2)}, u32[]{:S(2)}) collective-permute-start(f32[2,128,3]{1,0,2:T(2,128)S(1)} %pad_maximum_fusion.7), channel_id=1, source_target_pairs={{0,8},{8,0},{16,24},{24,16},{32,40},{40,32},{48,56},{56,48},{64,72... | collective-permute-start | bytes 9224 | tf_op jit(solution)/shard_map/ppermute | solution.py:79
  136.9 16.9 %all-to-all-start.1 = ((f32[2,128,2]{0,2,1:T(2,128)}), f32[2,128,2]{0,2,1:T(2,128)S(1)}, u32[]{:S(2)}, u32[]{:S(2)}) async-start(f32[2,128,2]{0,2,1:T(2,128)} %copy.369), calls=%async_computation.1 | async-start | bytes 262144 | tf_op jit(solution)/shard_map/all_to_all | solution.py:214
  165.7 0.9 copy-start.9
  165.7 1.0 copy-start.10
  165.8 1.0 copy-start.1
  165.8 1.0 copy-start.8
Sparse Core Ops, SparseCore 0:
  124.8 38.4 all-gather.4
